TPU v7x, 128 devices: a whole 4x4x4 slice. The times are simulated.
128 devices in a mesh: rows: 32 (over y, x, core), rep: 4 (over z).
Axes of the slice: x: 4, y: 4, z: 4, core: 2. Of those that a mesh axis runs over, the one named last changes fastest.
Arguments:
- weights: bfloat16 [80, 2097152], P('rep', 'rows'), may hold values from 0.25 to 4
- cell_ids: int32 [2097152], P('rows'), may hold values from 0 to 31
- group_sizes: int32 [32, 1024], P('rows'), may hold values from 32 to 96, as said below
- group_county: int32 [32768, 1], P('rows'), may hold values from 0 to 1023; in each aligned block of 1024 rows (0 to 1023, 1024 to 2047, ...) at most 2 rows name the same one
- age_rate: float32 [1024, 4], P('rows'), may hold values from 8 to 40
- kind_rate: float32 [1024, 8], P('rows'), may hold values from 2 to 20
Outputs:
- raked: float32 [32768, 2560], P('rows', 'rep')
- spread: float32 [32768, 32], P('rows')
Inputs may be any that keep to these rules, and one draw needn't show every extreme that they name: `group_sizes`: each shard's 1024 sizes sum to 65536. `group_county`: among the 1024 block groups of one shard, no county holds more than 2.
All inputs are finite; a program needn't handle non-finite values.
Results may differ from a plain program's by a relative error of at most 0.0003.
Values sent between devices are 32-bit elements; how exact they have to be, the bound alone decides.
No kernel may reach another device: no remote copies, remote signals or barrier semaphores. Data moves between devices by JAX's collectives and lax.ppermute only.
A program may use at most 64 MiB of HBM per device.

v0:
```python
import jax
import jax.numpy as jnp
from jax import lax
from jax.sharding import PartitionSpec as P

AGES = 4
KINDS = 8
CELLS = 32
LOW = 32
ITERS = 4


def rake(county_tables, groups_in, age_rate, kind_rate):
    county_rows = county_tables.shape[0]
    current = county_tables.reshape(county_rows, -1, AGES, KINDS)
    age_goal = (age_rate * groups_in[:, None])[:, None, :]
    kind_goal = (kind_rate * groups_in[:, None])[:, None, :]
    factor = jnp.ones_like(current)
    for sweep_index in range(ITERS):
        ratios = age_goal / jnp.maximum(jnp.sum(current, axis=3), 1.0)
        current = current * ratios[:, :, :, None]
        factor = factor * ratios[:, :, :, None]
        ratios = kind_goal / jnp.maximum(jnp.sum(current, axis=2), 1.0)
        current = current * ratios[:, :, None, :]
        factor = factor * ratios[:, :, None, :]
    return factor.reshape(county_rows, -1)


def exact_dot(left, right):
    return jnp.dot(left, right, precision=lax.Precision.HIGHEST, preferred_element_type=jnp.float32)


def tabulate(weights, cell_ids, group_sizes):
    reps_here, records_here = weights.shape
    group_here = group_sizes.shape[1]
    row_width = reps_here * CELLS
    block_rows = min(4096, records_here)
    window = block_rows // LOW + 2
    group_range = jnp.arange(group_here, dtype=jnp.int32)
    upper = (group_range[:, None] <= group_range[None, :]).astype(jnp.float32)
    sizes_float = group_sizes.astype(jnp.float32)
    group_ends = exact_dot(sizes_float, upper)[0].astype(jnp.int32)
    group_starts = group_ends - group_sizes[0]
    beyond = jnp.full((window,), records_here + 1, jnp.int32)
    ends_padded = jnp.concatenate([group_ends, beyond])
    starts_padded = jnp.concatenate([group_starts, beyond])
    cell_range = jnp.arange(CELLS, dtype=jnp.int32)
    block_range = jnp.arange(block_rows, dtype=jnp.int32)

    def add_block(block_index, totals):
        start = block_index * block_rows
        weight_block = lax.dynamic_slice_in_dim(weights, start, block_rows, 1)
        cell_block = lax.dynamic_slice_in_dim(cell_ids, start, block_rows, 0)
        first_slot = jnp.sum((group_ends <= start).astype(jnp.int32))
        ends_window = lax.dynamic_slice_in_dim(ends_padded, first_slot, window, 0)
        starts_window = lax.dynamic_slice_in_dim(starts_padded, first_slot, window, 0)
        place = start + block_range
        slot_hot = (
            (place[:, None] >= starts_window[None, :]) & (place[:, None] < ends_window[None, :])
        ).astype(jnp.bfloat16)
        cell_hot = (cell_block[None, None, :] == cell_range[None, :, None]).astype(jnp.bfloat16)
        spread_cells = (weight_block[:, None, :] * cell_hot).reshape(row_width, block_rows)
        product = jnp.dot(spread_cells, slot_hot, preferred_element_type=jnp.float32)
        current = lax.dynamic_slice_in_dim(totals, first_slot, window, 1)
        return lax.dynamic_update_slice_in_dim(totals, current + product, first_slot, 1)

    totals = jnp.zeros((row_width, group_here + window), jnp.float32)
    totals = lax.fori_loop(0, records_here // block_rows, add_block, totals)
    return totals[:, :group_here].T


def local(weights, cell_ids, group_sizes, group_county, age_rate, kind_rate):
    tables = tabulate(weights, cell_ids, group_sizes)
    group_here, row_width = tables.shape
    county_ids = group_county[:, 0]
    owners = lax.axis_size("rows")
    county_here = age_rate.shape[0]
    counties = county_here * owners
    pair_slots = max(2, 5 * group_here // (2 * counties))
    same_county = county_ids[:, None] == county_ids[None, :]
    group_order = jnp.arange(group_here, dtype=jnp.int32)
    earlier = group_order[:, None] > group_order[None, :]
    rank_within = jnp.sum((same_county & earlier).astype(jnp.int32), axis=1)
    slot_index = county_ids * pair_slots + rank_within
    slot_range = jnp.arange(counties * pair_slots, dtype=jnp.int32)
    slot_hot = (slot_index[:, None] == slot_range[None, :]).astype(jnp.float32)
    outgoing = exact_dot(slot_hot.T, tables).reshape(counties, pair_slots, row_width)
    present = jnp.sum(slot_hot, axis=0).reshape(counties, pair_slots)
    arrived, arrived_flags = (
        lax.all_to_all(outgoing, "rows", split_axis=0, concat_axis=1, tiled=True),
        lax.all_to_all(present, "rows", split_axis=0, concat_axis=1, tiled=True),
    )
    factor = rake(jnp.sum(arrived, axis=1), jnp.sum(arrived_flags, axis=1), age_rate, kind_rate)
    returned = lax.all_to_all(
        arrived * factor[:, None, :], "rows", split_axis=1, concat_axis=0, tiled=True
    )
    raked = exact_dot(slot_hot, returned.reshape(counties * pair_slots, row_width))
    reps_here = row_width // CELLS
    shaped = raked.reshape(group_here, reps_here, CELLS)
    total_reps = reps_here * lax.axis_size("rep")
    centre = lax.psum(jnp.sum(shaped, axis=1), "rep") / total_reps
    deviation = lax.psum(jnp.sum(jnp.square(shaped - centre[:, None, :]), axis=1), "rep")
    return (raked, deviation * (4.0 / total_reps))


def solution(mesh):
    placed = (
        P("rep", "rows"),
        P("rows"),
        P("rows", None),
        P("rows", None),
        P("rows", None),
        P("rows", None),
    )
    return jax.shard_map(
        local,
        mesh=mesh,
        in_specs=placed,
        out_specs=(P("rows", "rep"), P("rows", None)),
        check_vma=False,
    )
```

profile of v0, /device:TPU:1, one launch (start us, length us, event | category | flops | bytes accessed | tf_op | source)
XLA Modules:
  0.0 534.6 jit_solution(4150225946074218056)
XLA Ops:
  11.5 8.6 %all-to-all-start.1 = ((f32[32,32,2]{1,2,0:T(2,128)}), f32[32,32,2]{1,2,0:T(2,128)S(1)}, u32[]{:S(2)}, u32[]{:S(2)}) async-start(f32[32,32,2]{1,2,0:T(2,128)} %copy.28), calls=%async_computation.1 | async-start | bytes 65536 | tf_op jit(solution)/shard_map/all_to_all | solution.py:91
  22.4 216.4 %while.14 = (s32[]{:T(128)}, f32[640,1154]{0,1:T(8,128)S(1)}, s32[1024]{0:T(1024)S(1)}, bf16[20,65536]{1,0:T(8,128)(2,1)}, s32[65536]{0:T(1024)}, /*index=5*/s32...) while((s32[]{:T(128)}, f32[640,1154]{0,1:T(8,128)S(1)}, ...), condition=%wide.region_3.0_spmd.clone, body=%wide.region_1.3_spmd.clone.sunk | while | flops 686145792 | bytes 12922137 | solution.py:68
  29.6 4.3 fusion.35
  43.1 4.3 fusion.35
  56.7 4.3 fusion.35
  70.2 4.3 fusion.35
  97.2 4.3 fusion.35
  124.3 4.3 fusion.35
  191.9 4.3 fusion.35
  205.4 4.3 fusion.35
  219.0 4.3 fusion.35
  232.5 4.3 fusion.35
  238.8 13.5 %fusion.16 = f32[2048,640]{1,0:T(8,128)} fusion(s32[1024]{0:T(1024)S(1)} %bitcast.49, f32[640,1154]{0,1:T(8,128)S(1)} %get-tuple-element.156), kind=kOutput, calls=%fused_computation.19 | convolution fusion | flops 16108224512 | bytes 7868416 | tf_op jit(solution)/shard_map/dot_general | solution.py:30
  252.3 7.4 %reshape.177 = f32[1024,2,640]{2,1,0:T(2,128)} reshape(f32[2048,640]{1,0:T(8,128)} %fusion.16) | data formatting | bytes 10485760 | tf_op jit(solution)/shard_map/reshape | solution.py:87
  259.7 7.6 %all-to-all-start = ((f32[1024,2,640]{2,1,0:T(2,128)}), f32[1024,2,640]{2,1,0:T(2,128)}, u32[]{:S(2)}, u32[]{:S(2)}) async-start(f32[1024,2,640]{2,1,0:T(2,128)} %reshape.177), calls=%async_computation | async-start | bytes 10485760 | tf_op jit(solution)/shard_map/all_to_all | solution.py:90
  267.7 61.5 %all-to-all-done = f32[1024,2,640]{2,1,0:T(2,128)} async-done(((f32[1024,2,640]{2,1,0:T(2,128)}), f32[1024,2,640]{2,1,0:T(2,128)}, u32[]{:S(2)}, u32[]{:S(2)}) %all-to-all-start) | async-done | bytes 5242912 | tf_op jit(solution)/shard_map/all_to_all | solution.py:90
  329.2 5.2 copy.26
  337.1 5.3 copy.27
  347.0 69.1 %all_to_all.46 = f32[32,64,640]{2,0,1:T(8,128)S(1)} all-to-all(f32[32,64,640]{2,0,1:T(8,128)S(1)} %bitcast_multiply_fusion), channel_id=1, replica_groups=mesh['rows'=32,'rep'=4] {'rows'}, dimensions={1} | all-to-all | bytes 10485760 | tf_op jit(solution)/shard_map/all_to_all | solution.py:94
  416.1 6.4 %copy.34 = f32[32,32,2,640]{3,2,0,1:T(2,128)} copy(f32[32,32,2,640]{3,0,2,1:T(8,128)S(1)} %bitcast.41) | data formatting | bytes 10485760 | tf_op jit(solution)/shard_map/all_to_all | solution.py:94
  422.4 7.6 %reshape.179 = f32[2048,640]{1,0:T(8,128)} reshape(f32[32,32,2,640]{3,2,1,0:T(2,128)} %bitcast.42) | data formatting | bytes 10485760 | tf_op jit(solution)/shard_map/reshape | solution.py:97
  430.0 11.2 %fusion.15 = f32[1024,640]{0,1:T(8,128)S(1)} fusion(f32[2048,640]{1,0:T(8,128)} %reshape.179, s32[1024]{0:T(1024)S(1)} %bitcast.50), kind=kOutput, calls=%fused_computation.18 | convolution fusion | flops 16108224512 | bytes 7868416 | tf_op jit(solution)/shard_map/dot_general | solution.py:30
  442.1 39.2 %all-reduce.5.cloned.1.call-done = f32[1024,32]{0,1:T(8,128)} async-done(((f32[1024,32]{0,1:T(8,128)}), f32[1024,32]{0,1:T(8,128)}) %all-reduce.5.cloned.1.call-update) | async-done | bytes 131088 | tf_op jit(solution)/shard_map/psum | solution.py:101
  485.3 40.9 %all-reduce.7.cloned.1.call-done = f32[1024,32]{0,1:T(8,128)} async-done(((f32[1024,32]{0,1:T(8,128)}), f32[1024,32]{0,1:T(8,128)}) %all-reduce.7.cloned.1.call-update) | async-done | bytes 131088 | tf_op jit(solution)/shard_map/psum | solution.py:102
  (199 shorter events, 162.4 us)
Async XLA Ops:
  11.5 248.1 %all-to-all-start.1 = ((f32[32,32,2]{1,2,0:T(2,128)}), f32[32,32,2]{1,2,0:T(2,128)S(1)}, u32[]{:S(2)}, u32[]{:S(2)}) async-start(f32[32,32,2]{1,2,0:T(2,128)} %copy.28), calls=%async_computation.1 | async-start | bytes 65536 | tf_op jit(solution)/shard_map/all_to_all | solution.py:91
  259.7 8.0 %copy-start.1 = (f32[32,4]{0,1:T(4,128)S(1)}, f32[32,4]{0,1:T(4,128)}, u32[]{:S(2)}) copy-start(f32[32,4]{0,1:T(4,128)} %param.12) | copy-start | bytes 1540
  259.7 8.0 %copy-start = (f32[32,8]{0,1:T(8,128)S(1)}, f32[32,8]{0,1:T(8,128)}, u32[]{:S(2)}) copy-start(f32[32,8]{0,1:T(8,128)} %param.13) | copy-start | bytes 3076
  259.7 69.5 %all-to-all-start = ((f32[1024,2,640]{2,1,0:T(2,128)}), f32[1024,2,640]{2,1,0:T(2,128)}, u32[]{:S(2)}, u32[]{:S(2)}) async-start(f32[1024,2,640]{2,1,0:T(2,128)} %reshape.177), calls=%async_computation | async-start | bytes 10485760 | tf_op jit(solution)/shard_map/all_to_all | solution.py:90
  267.3 214.0 %all-reduce.5.cloned.1.call-start = ((), (), s32[]{:S(2)}) async-start(), calls=%async_computation.3 | async-start | bytes 262144 | tf_op jit(solution)/shard_map/psum | solution.py:101
  442.1 84.1 %all-reduce.7.cloned.1.call-start = ((), (), s32[]{:S(2)}) async-start(), calls=%async_computation.4 | async-start | bytes 262144 | tf_op jit(solution)/shard_map/psum | solution.py:102
Sparse Core Ops, SparseCore 0:
  442.2 39.0 all-reduce.4
  484.2 41.9 all-reduce.6
where the time goes:
time: 539 us; the launch traced here: 535 us
  waiting for transfers between devices  142 us (26%)
  local copies, waits for them, and re-layouts  95.7 us (18%)
  matrix products  95.4 us (18%)
  other arithmetic  70.8 us (13%)
  blocking collectives  69.1 us (13%)
  loops' own time  31.2 us (6%)
  starting transfers between devices  16.5 us (3%)
  between operations  14.2 us (3%)
    dot_general x16, matrix products, add_block(): jnp.dot(spread_cells, slot_hot, preferred_element_type=jnp.float32)  69.4 us
    all_to_all x1, blocking collectives, local(): lax.all_to_all(arrived * factor[:, None, :], 'rows', split_axis=1, concat...  69.1 us
    all_to_all x1, waiting for transfers between devices, local(): lax.all_to_all(outgoing, 'rows', split_axis=0, concat_axis=1, tiled=True)  61.5 us
    mul x16, other arithmetic, add_block(): weight_block[:, None, :] * cell_hot  44.4 us
    psum x1, waiting for transfers between devices, local(): lax.psum(jnp.sum(jnp.square(shaped - centre[:, None, :]), axis=1), 'rep')  40.9 us
    psum x1, waiting for transfers between devices, local(): centre = lax.psum(jnp.sum(shaped, axis=1), 'rep') / total_reps  39.2 us
    another operation x1, loops' own time, tabulate(): totals = lax.fori_loop(0, records_here // block_rows, add_block, totals)  31.2 us
    dynamic_update_slice x16, local copies, waits for them, and re-layouts, add_block(): lax.dynamic_update_slice_in_dim(totals, current + product, first_slot, 1)  30.8 us
  transfers between devices with their start and end apart: 4, of which 3 were waited for; matrix products, arithmetic and copies ran while one was open for 39% of the time, Pallas kernels for 0%

commit v1 on v0

v1 whole, which is shorter than its diff:
```python
import jax
import jax.numpy as jnp
from jax import lax
from jax.experimental import pallas as pl
from jax.experimental.pallas import tpu as pltpu
from jax.sharding import PartitionSpec as P

AGES = 4
KINDS = 8
CELLS = 32
LOW = 32
ITERS = 4
BLOCK = 128
SPAN = 8
USE_KERNEL = True


def tab_kernel(offs_ref, seg_ref, w_ref, out_ref):
    steps = seg_ref.shape[0]
    width = SPAN * CELLS
    out_ref[...] = jnp.zeros_like(out_ref)
    rows = lax.broadcasted_iota(jnp.int32, (width, BLOCK), 0)

    def body(b, carry):
        seg = seg_ref[pl.ds(b, 1), :]
        hot = (rows == seg).astype(jnp.bfloat16)
        start = pl.multiple_of(b * BLOCK, BLOCK)
        w = w_ref[:, pl.ds(start, BLOCK)]
        part = lax.dot_general(
            w, hot, (((1,), (1,)), ((), ())), preferred_element_type=jnp.float32
        )
        off = pl.multiple_of(offs_ref[b], 128)
        out_ref[:, pl.ds(off, width)] += part
        return carry

    lax.fori_loop(0, steps, body, 0, unroll=8)


def tab_plain(offs, seg, weights, out_width):
    reps = weights.shape[0]
    steps = seg.shape[0]
    width = SPAN * CELLS
    hot = (seg[:, None, :] == jnp.arange(width, dtype=jnp.int32)[None, :, None])
    w = weights.reshape(reps, steps, BLOCK)
    part = jnp.einsum("rbi,bni->brn", w.astype(jnp.float32), hot.astype(jnp.float32),
                      precision=lax.Precision.HIGHEST)
    cols = offs[:, None] + jnp.arange(width, dtype=jnp.int32)[None, :]
    out = jnp.zeros((reps, out_width), jnp.float32)
    return out.at[:, cols.reshape(-1)].add(part.transpose(1, 0, 2).reshape(reps, -1))


def tabulate(weights, cell_ids, group_sizes):
    reps, records = weights.shape
    sizes = group_sizes[0]
    groups = sizes.shape[0]
    ends = jnp.cumsum(sizes).astype(jnp.int32)
    steps = records // BLOCK
    block_start = jnp.arange(steps, dtype=jnp.int32) * BLOCK
    first = jnp.sum((ends[None, :] <= block_start[:, None]).astype(jnp.int32), axis=1)
    base = first - first % 4
    ends_pad = jnp.concatenate([ends, jnp.full((SPAN,), records + 1, jnp.int32)])
    window = ends_pad[base[:, None] + jnp.arange(SPAN - 1, dtype=jnp.int32)[None, :]]
    place = block_start[:, None] + jnp.arange(BLOCK, dtype=jnp.int32)[None, :]
    local = jnp.zeros((steps, BLOCK), jnp.int32)
    for j in range(SPAN - 1):
        local = local + (window[:, j:j + 1] <= place).astype(jnp.int32)
    seg = local * CELLS + cell_ids.reshape(steps, BLOCK)
    offs = (base * CELLS).astype(jnp.int32)
    out_width = (groups + SPAN) * CELLS
    if USE_KERNEL:
        out = pl.pallas_call(
            tab_kernel,
            out_shape=jax.ShapeDtypeStruct((reps, out_width), jnp.float32),
            in_specs=[
                pl.BlockSpec(memory_space=pltpu.SMEM),
                pl.BlockSpec(memory_space=pltpu.VMEM),
                pl.BlockSpec(memory_space=pltpu.VMEM),
            ],
            out_specs=pl.BlockSpec(memory_space=pltpu.VMEM),
            cost_estimate=pl.CostEstimate(
                flops=2 * reps * records * SPAN * CELLS,
                bytes_accessed=weights.size * 2 + seg.size * 4 + reps * out_width * 4,
                transcendentals=0,
            ),
        )(offs, seg, weights)
    else:
        out = tab_plain(offs, seg, weights, out_width)
    out = out[:, :groups * CELLS].reshape(reps, groups, CELLS)
    return out.transpose(1, 0, 2).reshape(groups, reps * CELLS)


def rake_all(county_tables, groups_in, age_rate, kind_rate):
    counties, width = county_tables.shape
    reps = width // CELLS
    span = counties * reps
    current = county_tables.reshape(counties, reps, CELLS).transpose(2, 0, 1)
    current = current.reshape(AGES, KINDS, span)
    age_goal = (age_rate * groups_in[:, None]).T
    age_goal = jnp.broadcast_to(age_goal[:, :, None], (AGES, counties, reps)).reshape(AGES, span)
    kind_goal = (kind_rate * groups_in[:, None]).T
    kind_goal = jnp.broadcast_to(kind_goal[:, :, None], (KINDS, counties, reps)).reshape(KINDS, span)
    factor = jnp.ones_like(current)
    for sweep_index in range(ITERS):
        ratios = age_goal / jnp.maximum(jnp.sum(current, axis=1), 1.0)
        current = current * ratios[:, None, :]
        factor = factor * ratios[:, None, :]
        ratios = kind_goal / jnp.maximum(jnp.sum(current, axis=0), 1.0)
        current = current * ratios[None, :, :]
        factor = factor * ratios[None, :, :]
    factor = factor.reshape(CELLS, counties, reps).transpose(1, 2, 0)
    return factor.reshape(counties, width)


def local(weights, cell_ids, group_sizes, group_county, age_rate, kind_rate):
    rates = lax.all_gather(jnp.concatenate([age_rate, kind_rate], axis=1), "rows", tiled=True)
    tables = tabulate(weights, cell_ids, group_sizes)
    groups, width = tables.shape
    reps = width // CELLS
    county = group_county[:, 0]
    counties = rates.shape[0]
    group_range = jnp.arange(groups, dtype=jnp.int32)
    same = county[:, None] == county[None, :]
    earlier = group_range[:, None] > group_range[None, :]
    second = jnp.any(same & earlier, axis=1)
    county_range = jnp.arange(counties, dtype=jnp.int32)
    hits = county[None, :] == county_range[:, None]
    first_hit = hits & ~second[None, :]
    second_hit = hits & second[None, :]
    pick1 = jnp.where(jnp.any(first_hit, axis=1),
                      jnp.sum(jnp.where(first_hit, group_range[None, :], 0), axis=1), groups)
    pick2 = jnp.where(jnp.any(second_hit, axis=1),
                      jnp.sum(jnp.where(second_hit, group_range[None, :], 0), axis=1), groups)
    padded = jnp.concatenate([tables, jnp.zeros((1, width), tables.dtype)], axis=0)
    partial = jnp.take(padded, pick1, axis=0) + jnp.take(padded, pick2, axis=0)
    present = jnp.sum(hits.astype(jnp.float32), axis=1)
    county_tables, groups_in = lax.psum((partial, present), "rows")
    factor = rake_all(county_tables, groups_in, rates[:, :AGES], rates[:, AGES:])
    raked = tables * jnp.take(factor, county, axis=0)

    shaped = raked.reshape(groups, reps, CELLS)
    part_sum = jnp.sum(shaped, axis=1)
    part_mean = part_sum / reps
    part_m2 = jnp.sum(jnp.square(shaped - part_mean[:, None, :]), axis=1)
    stats = jnp.concatenate([part_sum, part_m2], axis=1)
    shards = lax.axis_size("rep")
    me = lax.axis_index("rep")
    received = [stats] + [
        lax.ppermute(stats, "rep", [(i, (i + s) % shards) for i in range(shards)])
        for s in range(1, shards)
    ]
    by_source = []
    for source in range(shards):
        value = jnp.zeros_like(stats)
        for s in range(shards):
            value = jnp.where((me - s) % shards == source, received[s], value)
        by_source.append(value)
    total_reps = reps * shards
    total = by_source[0][:, :CELLS]
    for source in range(1, shards):
        total = total + by_source[source][:, :CELLS]
    centre = total / total_reps
    deviation = None
    for source in range(shards):
        spread_in = by_source[source][:, CELLS:]
        gap = by_source[source][:, :CELLS] / reps - centre
        term = spread_in + reps * jnp.square(gap)
        deviation = term if deviation is None else deviation + term
    return (raked, deviation * (4.0 / total_reps))


def solution(mesh):
    placed = (
        P("rep", "rows"),
        P("rows"),
        P("rows", None),
        P("rows", None),
        P("rows", None),
        P("rows", None),
    )
    return jax.shard_map(
        local,
        mesh=mesh,
        in_specs=placed,
        out_specs=(P("rows", "rep"), P("rows", None)),
        check_vma=False,
    )
```

time: 539 us -> 346 us (0.64)
  waiting for transfers between devices: 142 us -> 19.6 us
  matrix products: 95.4 us -> 0 us
  local copies, waits for them, and re-layouts: 95.7 us -> 142 us
  loops' own time: 31.2 us -> 0 us
  Pallas kernels: 0 us -> 22.6 us
  other arithmetic: 70.8 us -> 48.5 us
  blocking collectives: 69.1 us -> 89.2 us
  starting transfers between devices: 16.5 us -> 3.84 us
    dot_general x19 -> x0, matrix products: 95.4 us -> none  [the longest x16 69.4 us: add_block(): jnp.dot(spread_cells, slot_hot, preferred_element_type=jnp.float32)]
    psum x2 -> x1, waiting for transfers between devices: 80.1 us -> 8.87 us  [local(): county_tables, groups_in = lax.psum((partial, present), 'rows')]
    all_to_all x1 -> x0, blocking collectives: 69.1 us -> none  [local(): lax.all_to_all(arrived * factor[:, None, :], 'rows', split_axis=1, concat...]
    psum x0 -> x1, blocking collectives: none -> 62.3 us  [local(): county_tables, groups_in = lax.psum((partial, present), 'rows')]
    all_to_all x2 -> x0, waiting for transfers between devices: 61.5 us -> none  [the longest x1 61.5 us: local(): lax.all_to_all(outgoing, 'rows', split_axis=0, concat_axis=1, tiled=True)]
    gather x0 -> x7, local copies, waits for them, and re-layouts: none -> 42.9 us  [the longest x2 19.2 us: tabulate(): ends_pad[base[:, None] + jnp.arange(SPAN - 1, dtype=jnp.int32)[None, :]]]
    mul x20 -> x4, other arithmetic: 47.5 us -> 4.75 us  [the longest x1 3.55 us: local(): raked = tables * jnp.take(factor, county, axis=0)]
    another operation x1 -> x0, loops' own time: 31.2 us -> none  [tabulate(): totals = lax.fori_loop(0, records_here // block_rows, add_block, totals)]
  transfers between devices with their start and end apart: 4 -> 4, of which waited for: 3 -> 4; matrix products, arithmetic and copies ran while one was open for 39% -> 5% of each run, Pallas kernels for 0% -> 0%
where the time goes in v1:
time: 346 us; the launch traced here: 340 us
  local copies, waits for them, and re-layouts  142 us (41%)
  blocking collectives  89.2 us (26%)
  other arithmetic  48.5 us (14%)
  Pallas kernels  22.6 us (7%)
  waiting for transfers between devices  19.6 us (6%)
  between operations  14.6 us (4%)
  starting transfers between devices  3.84 us (1%)
    psum x1, blocking collectives, local(): county_tables, groups_in = lax.psum((partial, present), 'rows')  62.3 us
    all_gather x1, blocking collectives, local(): lax.all_gather(jnp.concatenate([age_rate, kind_rate], axis=1), 'rows', ti...  26.9 us
    pallas_call x1, Pallas kernels, tabulate(): pl.pallas_call(tab_kernel, out_shape=jax.ShapeDtypeStruct((reps, out_widt...  22.6 us
    mul x1, local copies, waits for them, and re-layouts, rake_all(): factor = factor * ratios[None, :, :]  21.6 us
    gather x2, local copies, waits for them, and re-layouts, tabulate(): ends_pad[base[:, None] + jnp.arange(SPAN - 1, dtype=jnp.int32)[None, :]]  19.2 us
    reshape x1, local copies, waits for them, and re-layouts, rake_all(): current = current.reshape(AGES, KINDS, span)  19 us
    gather x3, local copies, waits for them, and re-layouts, local(): raked = tables * jnp.take(factor, county, axis=0)  13.4 us
    transpose x1, local copies, waits for them, and re-layouts, rake_all(): factor = factor.reshape(CELLS, counties, reps).transpose(1, 2, 0)  11.3 us
  transfers between devices with their start and end apart: 4, of which 4 were waited for; matrix products, arithmetic and copies ran while one was open for 5% of the time, Pallas kernels for 0%

profile of v1, /device:TPU:1, one launch (start us, length us, event | category | flops | bytes accessed | tf_op | source)
XLA Modules:
  0.0 340.1 jit_solution(3476083836818130950)
XLA Ops:
  15.5 19.0 %gather_fusion = s32[3584]{0:T(1024)S(1)} fusion(s32[1032]{0:T(1024)S(1)} %concatenate.12, s32[4096]{0:T(1024)S(1)} %pad_clamp_fusion), kind=kCustom, calls=%fused_computation.2 | custom fusion | bytes 43008 | tf_op jit(solution)/shard_map/gather | solution.py:62
  37.2 22.6 %shard_map.77 = f32[20,33024]{1,0:T(8,128)} custom-call(s32[512]{0:T(512)} %get-tuple-element.20.offs_ref, s32[512,128]{1,0:T(8,128)} %bitcast_add_fusion.seg_ref, bf16[20,65536]{1,0:T(8,128)(2,1)} %w_ref.1), custom_call_target="tpu_custom_call" | custom-call | flops 671088640 | bytes 5525504 | tf_op jit(solution)/shard_map/pallas_call | solution.py:71
  61.7 5.4 %reshape.220 = f32[20,1024,32]{2,1,0:T(8,128)} reshape(f32[20,32768]{1,0:T(8,128)S(1)} %slice-done) | data formatting | bytes 5242880 | tf_op jit(solution)/shard_map/reshape | solution.py:88
  67.1 6.6 %copy.44 = f32[1024,20,32]{0,2,1:T(8,128)S(1)} copy(f32[1024,20,32]{2,0,1:T(8,128)} %bitcast.27) | data formatting | bytes 5242880 | tf_op jit(solution)/shard_map/transpose | solution.py:89
  77.7 5.2 %gather_fusion.2 = f32[1024,640]{1,0:T(8,128)} fusion(f32[1025,640]{1,0:T(8,128)S(1)} %concatenate.14, s32[1024]{0:T(1024)S(1)} %get-tuple-element.28), kind=kCustom, calls=%fused_computation.clone | custom fusion | bytes 5246976 | tf_op jit(solution)/shard_map/jit(_take)/gather | solution.py:134
  82.8 5.2 %gather_fusion.3 = f32[1024,640]{1,0:T(8,128)} fusion(f32[1025,640]{1,0:T(8,128)S(1)} %concatenate.14, s32[1024]{0:T(1024)S(1)} %get-tuple-element.29), kind=kCustom, calls=%fused_computation.1.clone | custom fusion | bytes 5246976 | tf_op jit(solution)/shard_map/jit(_take)/gather | solution.py:134
  88.0 3.9 %select_add_fusion = f32[1024,640]{1,0:T(8,128)} fusion(f32[1024,640]{1,0:T(8,128)} %gather_fusion.3, f32[1024,640]{1,0:T(8,128)} %gather_fusion.2, pred[1024]{0:T(1024)(128)(4,1)S(1)} %get-tuple-element.26, pred[1024]{0:T(1024)(128)(4,1)S(1)} %get-tuple-element.27), kind=kLoop, calls=%fused_computation.17 | loop fusion | flops 1966080 | bytes 7866368 | tf_op jit(solution)/shard_map/add | solution.py:134
  94.1 8.9 %copy.48 = f32[32,1024,20]{2,1,0:T(8,128)} copy(f32[32,1024,20]{1,0,2:T(8,128)S(1)} %bitcast.29) | data formatting | bytes 5242880 | tf_op jit(solution)/shard_map/transpose | solution.py:96
  102.9 19.0 %reshape.224 = f32[4,8,20480]{2,1,0:T(8,128)} reshape(f32[32,1024,20]{2,1,0:T(8,128)} %copy.48) | data formatting | bytes 5242880 | tf_op jit(solution)/shard_map/reshape | solution.py:97
  122.6 26.9 %all-gather = f32[32,32,12]{1,2,0:T(8,128)S(1)} all-gather(f32[1,32,12]{1,2,0:T(8,128)S(1)} %maximum_bitcast_fusion), channel_id=1, replica_groups=mesh['rows'=32,'rep'=4] {'rows'}, dimensions={0}, use_global_device_ids=true | all-gather | bytes 50688 | tf_op jit(solution)/shard_map/all_gather | solution.py:115
  150.2 62.3 %psum.14 = f32[1024]{0:T(1024)S(1)} all-reduce(f32[1024]{0:T(1024)S(1)} %convert_reduce_fusion), channel_id=1, replica_groups=mesh['rows'=32,'rep'=4] {'rows'}, use_global_device_ids=true, to_apply=%region_4.5 | all-reduce | flops 1024 | bytes 8192 | tf_op jit(solution)/shard_map/psum | solution.py:136
  213.2 2.7 reshape.222
  218.5 6.2 %reshape.225 = f32[8,20480]{1,0:T(8,128)S(1)} reshape(f32[8,1024,20]{2,1,0:T(8,128)} %broadcast_in_dim.44) | data formatting | bytes 1310720 | tf_op jit(solution)/shard_map/reshape | solution.py:101
  224.7 8.9 %all-reduce.4.cloned.1.call-done = f32[4,8,20480]{2,1,0:T(8,128)} async-done(((f32[4,8,20480]{2,1,0:T(8,128)}), f32[4,8,20480]{2,1,0:T(8,128)}) %all-reduce.4.cloned.1.call-update) | async-done | bytes 2621456 | tf_op jit(solution)/shard_map/psum | solution.py:136
  233.6 3.3 reduce_sum.130
  246.1 21.6 %reshape.229 = f32[32,1024,20]{2,1,0:T(8,128)} reshape(f32[4,8,20480]{2,1,0:T(8,128)S(1)} %multiply_multiply_fusion) | data formatting | bytes 5242880 | tf_op jit(solution)/shard_map/mul | solution.py:109
  267.7 11.3 %copy.49 = f32[1024,20,32]{0,2,1:T(8,128)} copy(f32[1024,20,32]{1,0,2:T(8,128)} %bitcast.28) | data formatting | bytes 5242880 | tf_op jit(solution)/shard_map/transpose | solution.py:110
  281.2 5.2 %gather_fusion.1 = f32[1024,640]{1,0:T(8,128)} fusion(f32[1024,640]{1,0:T(8,128)S(1)} %copy.50, s32[1024]{0:T(1024)S(1)} %broadcast_clamp_fusion), kind=kCustom, calls=%fused_computation.3 | custom fusion | bytes 5246976 | tf_op jit(solution)/shard_map/jit(_take)/gather | solution.py:138
  288.5 6.0 %copy.53 = f32[1024,20,32]{2,0,1:T(8,128)} copy(f32[1024,20,32]{0,2,1:T(8,128)S(1)} %bitcast.32) | data formatting | bytes 5242880 | tf_op jit(solution)/shard_map/jit(_take)/gather | solution.py:138
  294.5 8.5 %fusion.7 = f32[1024,32]{1,0:T(8,128)S(1)} fusion(f32[1024,20,32]{2,0,1:T(8,128)} %copy.53, pred[1024]{0:T(1024)(128)(4,1)S(1)} %get-tuple-element.18, f32[20,1024,32]{2,1,0:T(8,128)} %reshape.220), kind=kLoop, calls=%fused_computation.29 | loop fusion | flops 1933312 | bytes 5374976 | tf_op jit(solution)/shard_map/reduce_sum | solution.py:141
  303.5 9.3 %multiply_reduce_fusion = f32[1024,32]{1,0:T(8,128)} fusion(f32[1024,32]{1,0:T(8,128)S(1)} %copy.55, f32[1024,20,32]{2,0,1:T(8,128)} %copy.53, pred[1024]{0:T(1024)(128)(4,1)S(1)} %get-tuple-element.18, f32[20,1024,32]{2,1,0:T(8,128)} %reshape.220), kind=kLoop, calls=%fused_computation.4 | loop fusion | flops 3244032 | bytes 5506048 | tf_op jit(solution)/shard_map/reduce_sum | solution.py:143
  314.0 2.7 collective-permute-start
  317.8 3.6 %select_multiply_fusion.1 = f32[1024,640]{1,0:T(8,128)} fusion(f32[1024,640]{1,0:T(8,128)} %copy.51, f32[1024,640]{1,0:T(8,128)S(1)} %copy-done.1, pred[1024]{0:T(1024)(128)(4,1)S(1)} %get-tuple-element.18), kind=kLoop, calls=%fused_computation.19 | loop fusion | flops 1310720 | bytes 7865344 | tf_op jit(solution)/shard_map/mul | solution.py:138
  325.1 7.0 %collective-permute-done.2 = f32[1024,64]{0,1:T(8,128)S(1)} collective-permute-done((f32[1024,64]{0,1:T(8,128)S(1)}, f32[1024,64]{0,1:T(8,128)S(1)}, u32[]{:S(2)}, u32[]{:S(2)}) %collective-permute-start.2) | collective-permute-done | bytes 262176 | tf_op jit(solution)/shard_map/ppermute | solution.py:148
  (82 shorter events, 44.3 us)
Async XLA Ops:
  7.2 226.4 %all-reduce.4.cloned.1.call-start = ((), (), s32[]{:S(2)}) async-start(), calls=%async_computation | async-start | bytes 5242880 | tf_op jit(solution)/shard_map/psum | solution.py:136
  15.5 20.3 %copy-start.3 = (s32[65536]{0:T(1024)S(1)}, s32[65536]{0:T(1024)}, u32[]{:S(2)}) copy-start(s32[65536]{0:T(1024)} %param.9) | copy-start | bytes 786436
  59.8 1.9 slice-start
  121.9 0.7 copy-start.4
  121.9 0.7 copy-start.6
  121.9 27.8 %copy-start.5 = (s32[1024,1]{0,1:T(1,128)S(1)}, s32[1024,1]{0,1:T(1,128)}, u32[]{:S(2)}) copy-start(s32[1024,1]{0,1:T(1,128)} %param.11) | copy-start | bytes 12292
  233.6 4.5 %copy-start = (f32[4,8,20480]{2,1,0:T(8,128)S(1)}, f32[4,8,20480]{2,1,0:T(8,128)}, u32[]{:S(2)}) copy-start(f32[4,8,20480]{2,1,0:T(8,128)} %all-reduce.4.cloned.1.call-done) | copy-start | bytes 7864324
  238.4 1.3 copy-start.2
  303.5 14.3 %copy-start.1 = (f32[1024,640]{1,0:T(8,128)S(1)}, f32[1024,640]{1,0:T(8,128)}, u32[]{:S(2)}) copy-start(f32[1024,640]{1,0:T(8,128)} %gather_fusion.1) | copy-start | bytes 7864324
  314.0 8.6 %collective-permute-start = (f32[1024,64]{0,1:T(8,128)S(1)}, f32[1024,64]{0,1:T(8,128)S(1)}, u32[]{:S(2)}, u32[]{:S(2)}) collective-permute-start(f32[1024,64]{0,1:T(8,128)S(1)} %pad_maximum_fusion), channel_id=1, source_target_pairs={{0,3},{1,0},{2,1},{3,2},{4,7},{5,4},{6,5},{7,6},{8,11},{9,8},{10,9... | collective-permute-start | bytes 786440 | tf_op jit(solution)/shard_map/ppermute | solution.py:148
  316.7 8.4 %collective-permute-start.1 = (f32[1024,64]{0,1:T(8,128)S(1)}, f32[1024,64]{0,1:T(8,128)S(1)}, u32[]{:S(2)}, u32[]{:S(2)}) collective-permute-start(f32[1024,64]{0,1:T(8,128)S(1)} %pad_maximum_fusion), channel_id=1, source_target_pairs={{0,2},{1,3},{2,0},{3,1},{4,6},{5,7},{6,4},{7,5},{8,10},{9,11},{10,... | collective-permute-start | bytes 786440 | tf_op jit(solution)/shard_map/ppermute | solution.py:148
  317.1 15.0 %collective-permute-start.2 = (f32[1024,64]{0,1:T(8,128)S(1)}, f32[1024,64]{0,1:T(8,128)S(1)}, u32[]{:S(2)}, u32[]{:S(2)}) collective-permute-start(f32[1024,64]{0,1:T(8,128)S(1)} %pad_maximum_fusion), channel_id=1, source_target_pairs={{0,1},{1,2},{2,3},{3,0},{4,5},{5,6},{6,7},{7,4},{8,9},{9,10},{10,1... | collective-permute-start | bytes 786440 | tf_op jit(solution)/shard_map/ppermute | solution.py:148
Sparse Core Ops, SparseCore 0:
  122.1 111.4 all-reduce.3

commit v2 on v1

v2 whole, which is shorter than its diff:
```python
import jax
import jax.numpy as jnp
from jax import lax
from jax.experimental import pallas as pl
from jax.experimental.pallas import tpu as pltpu
from jax.sharding import PartitionSpec as P

AGES = 4
KINDS = 8
CELLS = 32
LOW = 32
ITERS = 4
BLOCK = 128
SPAN = 8
USE_KERNEL = True


def tab_kernel(base_ref, ends_ref, cell_ref, w_ref, out_ref):
    steps = cell_ref.shape[0]
    width = SPAN * CELLS
    out_ref[...] = jnp.zeros_like(out_ref)
    rows = lax.broadcasted_iota(jnp.int32, (width, BLOCK), 0)
    lane = lax.broadcasted_iota(jnp.int32, (1, BLOCK), 1)

    def body(b, carry):
        first = base_ref[b]
        place = lane + b * BLOCK
        local = jnp.zeros((1, BLOCK), jnp.int32)
        for j in range(SPAN - 1):
            local = local + (place >= ends_ref[first + j]).astype(jnp.int32)
        seg = local * CELLS + cell_ref[pl.ds(b, 1), :]
        hot = (rows == seg).astype(jnp.bfloat16)
        start = pl.multiple_of(b * BLOCK, BLOCK)
        w = w_ref[:, pl.ds(start, BLOCK)]
        part = lax.dot_general(
            w, hot, (((1,), (1,)), ((), ())), preferred_element_type=jnp.float32
        )
        off = pl.multiple_of(first * CELLS, 128)
        out_ref[:, pl.ds(off, width)] += part
        return carry

    lax.fori_loop(0, steps, body, 0, unroll=4)


def tab_plain(base, ends_pad, cells, weights, out_width):
    reps = weights.shape[0]
    steps = cells.shape[0]
    width = SPAN * CELLS
    window = ends_pad[base[:, None] + jnp.arange(SPAN - 1, dtype=jnp.int32)[None, :]]
    place = (jnp.arange(steps, dtype=jnp.int32) * BLOCK)[:, None] + jnp.arange(BLOCK, dtype=jnp.int32)[None, :]
    local = jnp.zeros((steps, BLOCK), jnp.int32)
    for j in range(SPAN - 1):
        local = local + (place >= window[:, j:j + 1]).astype(jnp.int32)
    seg = local * CELLS + cells
    hot = (seg[:, None, :] == jnp.arange(width, dtype=jnp.int32)[None, :, None])
    w = weights.reshape(reps, steps, BLOCK)
    part = jnp.einsum("rbi,bni->brn", w.astype(jnp.float32), hot.astype(jnp.float32),
                      precision=lax.Precision.HIGHEST)
    cols = (base * CELLS)[:, None] + jnp.arange(width, dtype=jnp.int32)[None, :]
    out = jnp.zeros((reps, out_width), jnp.float32)
    return out.at[:, cols.reshape(-1)].add(part.transpose(1, 0, 2).reshape(reps, -1))


def tabulate(weights, cell_ids, group_sizes):
    reps, records = weights.shape
    sizes = group_sizes[0]
    groups = sizes.shape[0]
    ends = jnp.cumsum(sizes).astype(jnp.int32)
    steps = records // BLOCK
    block_start = jnp.arange(steps, dtype=jnp.int32) * BLOCK
    first = jnp.sum((ends[None, :] <= block_start[:, None]).astype(jnp.int32), axis=1)
    base = (first - first % 4).astype(jnp.int32)
    ends_pad = jnp.concatenate([ends, jnp.full((SPAN,), records + 1, jnp.int32)])
    cells = cell_ids.reshape(steps, BLOCK)
    out_width = (groups + SPAN) * CELLS
    if USE_KERNEL:
        out = pl.pallas_call(
            tab_kernel,
            out_shape=jax.ShapeDtypeStruct((reps, out_width), jnp.float32),
            in_specs=[
                pl.BlockSpec(memory_space=pltpu.SMEM),
                pl.BlockSpec(memory_space=pltpu.SMEM),
                pl.BlockSpec(memory_space=pltpu.VMEM),
                pl.BlockSpec(memory_space=pltpu.VMEM),
            ],
            out_specs=pl.BlockSpec(memory_space=pltpu.VMEM),
            cost_estimate=pl.CostEstimate(
                flops=2 * reps * records * SPAN * CELLS,
                bytes_accessed=weights.size * 2 + cells.size * 4 + reps * out_width * 4,
                transcendentals=0,
            ),
        )(base, ends_pad, cells, weights)
    else:
        out = tab_plain(base, ends_pad, cells, weights, out_width)
    out = out[:, :groups * CELLS].reshape(reps, groups, CELLS)
    return out.transpose(1, 0, 2).reshape(groups, reps * CELLS)


def exact_dot(left, right):
    return jnp.dot(left, right, precision=lax.Precision.HIGHEST, preferred_element_type=jnp.float32)


def rake_own(county_tables, groups_in, age_rate, kind_rate):
    counties, width = county_tables.shape
    reps = width // CELLS
    span = counties * reps
    current = county_tables.reshape(counties, reps, CELLS).transpose(2, 0, 1)
    current = current.reshape(AGES, KINDS, span)
    age_goal = (age_rate * groups_in[:, None]).T
    age_goal = jnp.broadcast_to(age_goal[:, :, None], (AGES, counties, reps)).reshape(AGES, span)
    kind_goal = (kind_rate * groups_in[:, None]).T
    kind_goal = jnp.broadcast_to(kind_goal[:, :, None], (KINDS, counties, reps)).reshape(KINDS, span)
    age_factor = jnp.ones((AGES, span), jnp.float32)
    kind_factor = jnp.ones((KINDS, span), jnp.float32)
    for sweep_index in range(ITERS):
        ratios = age_goal / jnp.maximum(jnp.sum(current, axis=1), 1.0)
        current = current * ratios[:, None, :]
        age_factor = age_factor * ratios
        ratios = kind_goal / jnp.maximum(jnp.sum(current, axis=0), 1.0)
        current = current * ratios[None, :, :]
        kind_factor = kind_factor * ratios
    age_factor = age_factor.reshape(AGES, counties, reps).transpose(1, 2, 0).reshape(counties, reps * AGES)
    kind_factor = kind_factor.reshape(KINDS, counties, reps).transpose(1, 2, 0).reshape(counties, reps * KINDS)
    return jnp.concatenate([age_factor, kind_factor], axis=1)


def spreaders(reps):
    col = jnp.arange(reps * CELLS, dtype=jnp.int32)
    rep_of, cell_of = col // CELLS, col % CELLS
    age_row = jnp.arange(reps * AGES, dtype=jnp.int32)
    kind_row = jnp.arange(reps * KINDS, dtype=jnp.int32)
    to_age = ((age_row[:, None] // AGES == rep_of[None, :])
              & (age_row[:, None] % AGES == cell_of[None, :] // KINDS)).astype(jnp.float32)
    to_kind = ((kind_row[:, None] // KINDS == rep_of[None, :])
               & (kind_row[:, None] % KINDS == cell_of[None, :] % KINDS)).astype(jnp.float32)
    cell_sum = (cell_of[:, None] == jnp.arange(CELLS, dtype=jnp.int32)[None, :]).astype(jnp.float32)
    return to_age, to_kind, cell_sum


def local(weights, cell_ids, group_sizes, group_county, age_rate, kind_rate):
    tables = tabulate(weights, cell_ids, group_sizes)
    groups, width = tables.shape
    reps = width // CELLS
    county = group_county[:, 0]
    owners = lax.axis_size("rows")
    county_here = age_rate.shape[0]
    counties = county_here * owners
    group_range = jnp.arange(groups, dtype=jnp.int32)
    same = county[:, None] == county[None, :]
    earlier = group_range[:, None] > group_range[None, :]
    second = jnp.any(same & earlier, axis=1)
    county_range = jnp.arange(counties, dtype=jnp.int32)
    hits = county[None, :] == county_range[:, None]
    first_hit = hits & ~second[None, :]
    second_hit = hits & second[None, :]
    pick1 = jnp.where(jnp.any(first_hit, axis=1),
                      jnp.sum(jnp.where(first_hit, group_range[None, :], 0), axis=1), groups)
    pick2 = jnp.where(jnp.any(second_hit, axis=1),
                      jnp.sum(jnp.where(second_hit, group_range[None, :], 0), axis=1), groups)
    padded = jnp.concatenate([tables, jnp.zeros((1, width), tables.dtype)], axis=0)
    partial = jnp.take(padded, pick1, axis=0) + jnp.take(padded, pick2, axis=0)
    present = jnp.sum(hits.astype(jnp.float32), axis=1).reshape(owners, 1, county_here)
    present = jnp.pad(present, ((0, 0), (0, 0), (0, width - county_here)))
    outgoing = jnp.concatenate([partial.reshape(owners, county_here, width), present], axis=1)
    arrived = lax.all_to_all(
        outgoing.reshape(owners * (county_here + 1), width), "rows", 0, 0, tiled=True
    ).reshape(owners, county_here + 1, width)
    summed = jnp.sum(arrived, axis=0)
    county_tables = summed[:county_here]
    groups_in = summed[county_here, :county_here]
    factors = rake_own(county_tables, groups_in, age_rate, kind_rate)
    factors = lax.all_gather(factors, "rows", tiled=True)
    mine = jnp.take(factors, county, axis=0)
    to_age, to_kind, cell_sum = spreaders(reps)
    factor = exact_dot(mine[:, :reps * AGES], to_age) * exact_dot(mine[:, reps * AGES:], to_kind)
    raked = tables * factor

    part_sum = exact_dot(raked, cell_sum)
    part_mean = part_sum / reps
    gap = raked - exact_dot(part_mean, cell_sum.T)
    part_m2 = exact_dot(jnp.square(gap), cell_sum)
    stats = jnp.concatenate([part_sum, part_m2], axis=1)
    shards = lax.axis_size("rep")
    me = lax.axis_index("rep")
    received = [stats] + [
        lax.ppermute(stats, "rep", [(i, (i + s) % shards) for i in range(shards)])
        for s in range(1, shards)
    ]
    by_source = []
    for source in range(shards):
        value = jnp.zeros_like(stats)
        for s in range(shards):
            value = jnp.where((me - s) % shards == source, received[s], value)
        by_source.append(value)
    total_reps = reps * shards
    total = by_source[0][:, :CELLS]
    for source in range(1, shards):
        total = total + by_source[source][:, :CELLS]
    centre = total / total_reps
    deviation = None
    for source in range(shards):
        spread_in = by_source[source][:, CELLS:]
        off_centre = by_source[source][:, :CELLS] / reps - centre
        term = spread_in + reps * jnp.square(off_centre)
        deviation = term if deviation is None else deviation + term
    return (raked, deviation * (4.0 / total_reps))


def solution(mesh):
    placed = (
        P("rep", "rows"),
        P("rows"),
        P("rows", None),
        P("rows", None),
        P("rows", None),
        P("rows", None),
    )
    return jax.shard_map(
        local,
        mesh=mesh,
        in_specs=placed,
        out_specs=(P("rows", "rep"), P("rows", None)),
        check_vma=False,
    )
```

time: 346 us -> 185 us (0.53); the launches traced: 340 us -> 185 us
  local copies, waits for them, and re-layouts: 142 us -> 35.5 us
  blocking collectives: 89.2 us -> 25.1 us
  waiting for transfers between devices: 19.6 us -> 54.7 us
  other arithmetic: 48.5 us -> 15.7 us
  between operations: 14.6 us -> 1.09 us
  starting transfers between devices: 3.84 us -> 13.2 us
  Pallas kernels: 22.6 us -> 31.5 us
  matrix products: 0 us -> 7.7 us
    psum x1 -> x0, blocking collectives: 62.3 us -> none  [local(): county_tables, groups_in = lax.psum((partial, present), 'rows')]
    all_to_all x0 -> x1, waiting for transfers between devices: none -> 40.7 us  [local(): lax.all_to_all(outgoing.reshape(owners * (county_here + 1), width), 'rows...]
    reshape x4 -> x7, local copies, waits for them, and re-layouts: 30 us -> 0.87 us  [the longest x1 0.28 us: rake_own(): current = current.reshape(AGES, KINDS, span)]
    gather x5 -> x1, local copies, waits for them, and re-layouts: 32.6 us -> 3.46 us  [local(): mine = jnp.take(factors, county, axis=0)]
    reduce_sum x11 -> x10, other arithmetic: 28.2 us -> 1.63 us  [the longest x1 1.18 us: local(): jnp.sum(hits.astype(jnp.float32), axis=1).reshape(owners, 1, county_here)]
    mul x1, local copies, waits for them, and re-layouts: 21.6 us -> 0.01 us  [rake_own(): age_goal = (age_rate * groups_in[:, None]).T]
    transpose x2 -> x3, local copies, waits for them, and re-layouts: 20.2 us -> 0.75 us  [the longest x1 0.53 us: rake_own(): current = county_tables.reshape(counties, reps, CELLS).transpose(2, 0, 1)]
    pallas_call x1, Pallas kernels: 22.6 us -> 31.5 us  [tabulate(): pl.pallas_call(tab_kernel, out_shape=jax.ShapeDtypeStruct((reps, out_widt...]
  transfers between devices with their start and end apart: 4 -> 4, of which waited for: 4 -> 3; matrix products, arithmetic and copies ran while one was open for 5% -> 0% of each run, Pallas kernels for 0% -> 0%
where the time goes in v2:
time: 185 us
  waiting for transfers between devices  54.7 us (30%)
  local copies, waits for them, and re-layouts  35.5 us (19%)
  Pallas kernels  31.5 us (17%)
  blocking collectives  25.1 us (14%)
  other arithmetic  15.7 us (8%)
  starting transfers between devices  13.2 us (7%)
  matrix products  7.7 us (4%)
    all_to_all x1, waiting for transfers between devices, local(): lax.all_to_all(outgoing.reshape(owners * (county_here + 1), width), 'rows...  40.7 us
    pallas_call x1, Pallas kernels, tabulate(): pl.pallas_call(tab_kernel, out_shape=jax.ShapeDtypeStruct((reps, out_widt...  31.5 us
    all_gather x1, blocking collectives, local(): factors = lax.all_gather(factors, 'rows', tiled=True)  25.1 us
    ppermute x3, waiting for transfers between devices, local(): lax.ppermute(stats, 'rep', [(i, (i + s) % shards) for i in range(shards)])  14.1 us
    gather x2, local copies, waits for them, and re-layouts, local(): partial = jnp.take(padded, pick1, axis=0) + jnp.take(padded, pick2, axis=0)  10.3 us
    all_to_all x1, starting transfers between devices, local(): lax.all_to_all(outgoing.reshape(owners * (county_here + 1), width), 'rows...  8.69 us
    dot_general x5, matrix products, exact_dot(): jnp.dot(left, right, precision=lax.Precision.HIGHEST, preferred_element_t...  7.7 us
    transpose x1, local copies, waits for them, and re-layouts, tabulate(): return out.transpose(1, 0, 2).reshape(groups, reps * CELLS)  6.56 us
  transfers between devices with their start and end apart: 4, of which 3 were waited for; matrix products, arithmetic and copies ran while one was open for 0% of the time, Pallas kernels for 0%

profile of v2, /device:TPU:1, one launch (start us, length us, event | category | flops | bytes accessed | tf_op | source)
XLA Modules:
  0.0 184.6 jit_solution(17148755373462609427)
XLA Ops:
  1.8 1.3 fusion.5
  3.1 1.8 fusion.2
  4.9 2.6 %select_reduce_fusion.1 = (s32[1024]{0:T(1024)S(1)}, s32[1024]{0:T(1024)S(1)}) fusion(s32[1024]{0:T(1024)} %bitcast.35, pred[1024]{0:T(1024)(128)(4,1)S(1)} %not.8, pred[1024]{0:T(1024)(128)(4,1)S(1)} %fusion.5), kind=kLoop, calls=%fused_computation.5 | loop fusion | flops 7337984 | bytes 14336 | tf_op jit(solution)/shard_map/reduce_sum | solution.py:157
  10.3 31.5 %shard_map.77 = f32[20,33024]{1,0:T(8,128)} custom-call(s32[512]{0:T(512)} %fusion.50.base_ref, s32[1032]{0:T(1024)} %concatenate.15.ends_ref, s32[512,128]{1,0:T(8,128)} %bitcast.28, bf16[20,65536]{1,0:T(8,128)(2,1)} %w_ref.1), custom_call_target="tpu_custom_call" | custom-call | flops 671088640 | bytes 5525504 | tf_op jit(solution)/shard_map/pallas_call | solution.py:77
  41.9 1.9 %slice-done = f32[20,32768]{1,0:T(8,128)S(1)} async-done(((f32[20,33024]{1,0:T(8,128)}), f32[20,32768]{1,0:T(8,128)S(1)}, s32[]{:S(2)}) %slice-start) | async-done | bytes 2621464 | tf_op jit(solution)/shard_map/slice | solution.py:95
  43.8 5.4 %reshape.364 = f32[20,1024,32]{2,1,0:T(8,128)} reshape(f32[20,32768]{1,0:T(8,128)S(1)} %slice-done) | data formatting | bytes 5242880 | tf_op jit(solution)/shard_map/reshape | solution.py:95
  49.2 6.6 %copy.19 = f32[1024,20,32]{0,2,1:T(8,128)S(1)} copy(f32[1024,20,32]{2,0,1:T(8,128)} %bitcast.23) | data formatting | bytes 5242880 | tf_op jit(solution)/shard_map/transpose | solution.py:96
  55.8 2.1 %copy.26 = f32[1024,640]{1,0:T(8,128)} copy(f32[1024,640]{0,1:T(8,128)S(1)} %bitcast.25) | data formatting | bytes 5242880 | tf_op jit(solution)/shard_map/reshape | solution.py:96
  57.9 1.9 %concatenate.16 = f32[1025,640]{1,0:T(8,128)S(1)} pad(f32[1024,640]{1,0:T(8,128)} %copy.26, f32[]{:T(128)} %constant.206.clone.1), padding=0_1x0_0 | pad | bytes 5245444 | tf_op jit(solution)/shard_map/concatenate | solution.py:160
  59.8 5.2 %gather_fusion.2 = f32[1024,640]{1,0:T(8,128)} fusion(f32[1025,640]{1,0:T(8,128)S(1)} %concatenate.16, s32[1024]{0:T(1024)S(1)} %get-tuple-element.30), kind=kCustom, calls=%fused_computation.1.clone | custom fusion | bytes 5246976 | tf_op jit(solution)/shard_map/jit(_take)/gather | solution.py:161
  65.0 5.2 %gather_fusion.1 = f32[1024,640]{1,0:T(8,128)} fusion(f32[1025,640]{1,0:T(8,128)S(1)} %concatenate.16, s32[1024]{0:T(1024)S(1)} %get-tuple-element.29), kind=kCustom, calls=%fused_computation.clone | custom fusion | bytes 5246976 | tf_op jit(solution)/shard_map/jit(_take)/gather | solution.py:161
  70.2 2.9 %select_add_fusion = f32[1024,640]{1,0:T(8,128)S(1)} fusion(f32[1024,640]{1,0:T(8,128)} %gather_fusion.2, f32[1024,640]{1,0:T(8,128)} %gather_fusion.1, pred[1024]{0:T(1024)(128)(4,1)S(1)} %get-tuple-element.27, pred[1024]{0:T(1024)(128)(4,1)S(1)} %get-tuple-element.28), kind=kLoop, calls=%fused_computation.16 | loop fusion | flops 1966080 | bytes 7866368 | tf_op jit(solution)/shard_map/add | solution.py:161
  73.0 1.9 %select_maximum_fusion = f32[32,33,640]{2,1,0:T(8,128)} fusion(f32[32,1,32]{2,1,0:T(1,128)S(1)} %reshape.367, f32[32,32,640]{2,1,0:T(8,128)S(1)} %bitcast.24), kind=kLoop, calls=%fused_computation.14 | loop fusion | flops 2027520 | bytes 5328896 | tf_op jit(solution)/shard_map/concatenate | solution.py:164
  74.9 8.7 %all-to-all-start = ((f32[32,33,640]{2,1,0:T(8,128)}), f32[32,33,640]{2,1,0:T(8,128)S(1)}, u32[]{:S(2)}, u32[]{:S(2)}) async-start(f32[32,33,640]{2,1,0:T(8,128)} %select_maximum_fusion), calls=%async_computation | async-start | bytes 6553600 | tf_op jit(solution)/shard_map/all_to_all | solution.py:165
  83.8 40.7 %all-to-all-done = f32[32,33,640]{2,1,0:T(8,128)S(1)} async-done(((f32[32,33,640]{2,1,0:T(8,128)}), f32[32,33,640]{2,1,0:T(8,128)S(1)}, u32[]{:S(2)}, u32[]{:S(2)}) %all-to-all-start) | async-done | bytes 2703392 | tf_op jit(solution)/shard_map/all_to_all | solution.py:165
  128.2 25.1 %all_gather.3 = f32[1024,240]{1,0:T(8,128)S(1)} all-gather(f32[32,240]{1,0:T(8,128)S(1)} %pad_maximum_fusion.1), channel_id=1, replica_groups=mesh['rows'=32,'rep'=4] {'rows'}, dimensions={0}, use_global_device_ids=true | all-gather | bytes 1013760 | tf_op jit(solution)/shard_map/all_gather | solution.py:172
  153.3 3.5 %gather_fusion = f32[1024,240]{1,0:T(8,128)S(1)} fusion(f32[1024,240]{1,0:T(8,128)S(1)} %all_gather.3, s32[1024]{0:T(1024)S(1)} %broadcast_clamp_fusion), kind=kCustom, calls=%fused_computation.2 | custom fusion | bytes 1970176 | tf_op jit(solution)/shard_map/jit(_take)/gather | solution.py:173
  158.5 1.8 multiply_multiply_fusion
  160.3 1.5 fusion.16
  161.8 1.5 fusion.15
  163.4 1.6 fusion.6
  165.0 3.8 %collective-permute-start = (f32[1024,64]{0,1:T(8,128)S(1)}, f32[1024,64]{0,1:T(8,128)S(1)}, u32[]{:S(2)}, u32[]{:S(2)}) collective-permute-start(f32[1024,64]{0,1:T(8,128)S(1)} %pad_maximum_fusion), channel_id=1, source_target_pairs={{0,3},{1,0},{2,1},{3,2},{4,7},{5,4},{6,5},{7,6},{8,11},{9,8},{10,9... | collective-permute-start | bytes 786440 | tf_op jit(solution)/shard_map/ppermute | solution.py:186
  169.6 10.4 %collective-permute-done = f32[1024,64]{0,1:T(8,128)S(1)} collective-permute-done((f32[1024,64]{0,1:T(8,128)S(1)}, f32[1024,64]{0,1:T(8,128)S(1)}, u32[]{:S(2)}, u32[]{:S(2)}) %collective-permute-start) | collective-permute-done | bytes 262176 | tf_op jit(solution)/shard_map/ppermute | solution.py:186
  180.0 3.6 %collective-permute-done.2 = f32[1024,64]{0,1:T(8,128)S(1)} collective-permute-done((f32[1024,64]{0,1:T(8,128)S(1)}, f32[1024,64]{0,1:T(8,128)S(1)}, u32[]{:S(2)}, u32[]{:S(2)}) %collective-permute-start.2) | collective-permute-done | bytes 262176 | tf_op jit(solution)/shard_map/ppermute | solution.py:186
  (84 shorter events, 11.1 us)
Async XLA Ops:
  41.9 1.9 %slice-start = ((f32[20,33024]{1,0:T(8,128)}), f32[20,32768]{1,0:T(8,128)S(1)}, s32[]{:S(2)}) async-start(f32[20,33024]{1,0:T(8,128)} %shard_map.77), calls=%async_computation.1 | async-start | bytes 6291456 | tf_op jit(solution)/shard_map/slice | solution.py:95
  74.9 8.8 %copy-start.2 = (s32[1024,1]{0,1:T(1,128)S(1)}, s32[1024,1]{0,1:T(1,128)}, u32[]{:S(2)}) copy-start(s32[1024,1]{0,1:T(1,128)} %param.11) | copy-start | bytes 12292
  74.9 49.5 %all-to-all-start = ((f32[32,33,640]{2,1,0:T(8,128)}), f32[32,33,640]{2,1,0:T(8,128)S(1)}, u32[]{:S(2)}, u32[]{:S(2)}) async-start(f32[32,33,640]{2,1,0:T(8,128)} %select_maximum_fusion), calls=%async_computation | async-start | bytes 6553600 | tf_op jit(solution)/shard_map/all_to_all | solution.py:165
  83.8 41.9 %copy-start.4 = (f32[32,4]{0,1:T(4,128)S(1)}, f32[32,4]{0,1:T(4,128)}, u32[]{:S(2)}) copy-start(f32[32,4]{0,1:T(4,128)} %param.12) | copy-start | bytes 1540
  83.8 42.1 %copy-start.3 = (f32[32,8]{0,1:T(8,128)S(1)}, f32[32,8]{0,1:T(8,128)}, u32[]{:S(2)}) copy-start(f32[32,8]{0,1:T(8,128)} %param.13) | copy-start | bytes 3076
  156.8 1.7 copy-start.1
  160.3 3.0 %copy-start = (f32[1024,640]{1,0:T(8,128)}, f32[1024,640]{1,0:T(8,128)S(1)}, u32[]{:S(2)}) copy-start(f32[1024,640]{1,0:T(8,128)S(1)} %multiply_multiply_fusion) | copy-start | bytes 7864324
  165.0 15.0 %collective-permute-start = (f32[1024,64]{0,1:T(8,128)S(1)}, f32[1024,64]{0,1:T(8,128)S(1)}, u32[]{:S(2)}, u32[]{:S(2)}) collective-permute-start(f32[1024,64]{0,1:T(8,128)S(1)} %pad_maximum_fusion), channel_id=1, source_target_pairs={{0,3},{1,0},{2,1},{3,2},{4,7},{5,4},{6,5},{7,6},{8,11},{9,8},{10,9... | collective-permute-start | bytes 786440 | tf_op jit(solution)/shard_map/ppermute | solution.py:186
  168.9 11.1 %collective-permute-start.1 = (f32[1024,64]{0,1:T(8,128)S(1)}, f32[1024,64]{0,1:T(8,128)S(1)}, u32[]{:S(2)}, u32[]{:S(2)}) collective-permute-start(f32[1024,64]{0,1:T(8,128)S(1)} %pad_maximum_fusion), channel_id=1, source_target_pairs={{0,2},{1,3},{2,0},{3,1},{4,6},{5,7},{6,4},{7,5},{8,10},{9,11},{10,... | collective-permute-start | bytes 786440 | tf_op jit(solution)/shard_map/ppermute | solution.py:186
  168.9 14.8 %collective-permute-start.2 = (f32[1024,64]{0,1:T(8,128)S(1)}, f32[1024,64]{0,1:T(8,128)S(1)}, u32[]{:S(2)}, u32[]{:S(2)}) collective-permute-start(f32[1024,64]{0,1:T(8,128)S(1)} %pad_maximum_fusion), channel_id=1, source_target_pairs={{0,1},{1,2},{2,3},{3,0},{4,5},{5,6},{6,7},{7,4},{8,9},{9,10},{10,1... | collective-permute-start | bytes 786440 | tf_op jit(solution)/shard_map/ppermute | solution.py:186

commit v3 on v2

--- a/solution.py
+++ b/solution.py
@@ -15,48 +15,36 @@
 USE_KERNEL = True
 
 
-def tab_kernel(base_ref, ends_ref, cell_ref, w_ref, out_ref):
-    steps = cell_ref.shape[0]
+def tab_kernel(offs_ref, seg_ref, w_ref, out_ref):
+    steps = seg_ref.shape[0]
     width = SPAN * CELLS
     out_ref[...] = jnp.zeros_like(out_ref)
     rows = lax.broadcasted_iota(jnp.int32, (width, BLOCK), 0)
-    lane = lax.broadcasted_iota(jnp.int32, (1, BLOCK), 1)
 
     def body(b, carry):
-        first = base_ref[b]
-        place = lane + b * BLOCK
-        local = jnp.zeros((1, BLOCK), jnp.int32)
-        for j in range(SPAN - 1):
-            local = local + (place >= ends_ref[first + j]).astype(jnp.int32)
-        seg = local * CELLS + cell_ref[pl.ds(b, 1), :]
+        seg = seg_ref[pl.ds(b, 1), :]
         hot = (rows == seg).astype(jnp.bfloat16)
         start = pl.multiple_of(b * BLOCK, BLOCK)
         w = w_ref[:, pl.ds(start, BLOCK)]
         part = lax.dot_general(
             w, hot, (((1,), (1,)), ((), ())), preferred_element_type=jnp.float32
         )
-        off = pl.multiple_of(first * CELLS, 128)
+        off = pl.multiple_of(offs_ref[b], 128)
         out_ref[:, pl.ds(off, width)] += part
         return carry
 
     lax.fori_loop(0, steps, body, 0, unroll=4)
 
 
-def tab_plain(base, ends_pad, cells, weights, out_width):
+def tab_plain(offs, seg, weights, out_width):
     reps = weights.shape[0]
-    steps = cells.shape[0]
+    steps = seg.shape[0]
     width = SPAN * CELLS
-    window = ends_pad[base[:, None] + jnp.arange(SPAN - 1, dtype=jnp.int32)[None, :]]
-    place = (jnp.arange(steps, dtype=jnp.int32) * BLOCK)[:, None] + jnp.arange(BLOCK, dtype=jnp.int32)[None, :]
-    local = jnp.zeros((steps, BLOCK), jnp.int32)
-    for j in range(SPAN - 1):
-        local = local + (place >= window[:, j:j + 1]).astype(jnp.int32)
-    seg = local * CELLS + cells
     hot = (seg[:, None, :] == jnp.arange(width, dtype=jnp.int32)[None, :, None])
     w = weights.reshape(reps, steps, BLOCK)
     part = jnp.einsum("rbi,bni->brn", w.astype(jnp.float32), hot.astype(jnp.float32),
                       precision=lax.Precision.HIGHEST)
-    cols = (base * CELLS)[:, None] + jnp.arange(width, dtype=jnp.int32)[None, :]
+    cols = offs[:, None] + jnp.arange(width, dtype=jnp.int32)[None, :]
     out = jnp.zeros((reps, out_width), jnp.float32)
     return out.at[:, cols.reshape(-1)].add(part.transpose(1, 0, 2).reshape(reps, -1))
 
@@ -70,8 +58,16 @@
     block_start = jnp.arange(steps, dtype=jnp.int32) * BLOCK
     first = jnp.sum((ends[None, :] <= block_start[:, None]).astype(jnp.int32), axis=1)
     base = (first - first % 4).astype(jnp.int32)
-    ends_pad = jnp.concatenate([ends, jnp.full((SPAN,), records + 1, jnp.int32)])
-    cells = cell_ids.reshape(steps, BLOCK)
+    group_range = jnp.arange(groups, dtype=jnp.int32)
+    place = block_start[:, None] + jnp.arange(BLOCK, dtype=jnp.int32)[None, :]
+    local = jnp.zeros((steps, BLOCK), jnp.int32)
+    for j in range(SPAN - 1):
+        chosen = group_range[None, :] == (base + j)[:, None]
+        edge = jnp.sum(jnp.where(chosen, ends[None, :], 0), axis=1)
+        edge = jnp.where(base + j < groups, edge, records + 1)
+        local = local + (place >= edge[:, None]).astype(jnp.int32)
+    seg = local * CELLS + cell_ids.reshape(steps, BLOCK)
+    offs = (base * CELLS).astype(jnp.int32)
     out_width = (groups + SPAN) * CELLS
     if USE_KERNEL:
         out = pl.pallas_call(
@@ -79,19 +75,18 @@
             out_shape=jax.ShapeDtypeStruct((reps, out_width), jnp.float32),
             in_specs=[
                 pl.BlockSpec(memory_space=pltpu.SMEM),
-                pl.BlockSpec(memory_space=pltpu.SMEM),
                 pl.BlockSpec(memory_space=pltpu.VMEM),
                 pl.BlockSpec(memory_space=pltpu.VMEM),
             ],
             out_specs=pl.BlockSpec(memory_space=pltpu.VMEM),
             cost_estimate=pl.CostEstimate(
                 flops=2 * reps * records * SPAN * CELLS,
-                bytes_accessed=weights.size * 2 + cells.size * 4 + reps * out_width * 4,
+                bytes_accessed=weights.size * 2 + seg.size * 4 + reps * out_width * 4,
                 transcendentals=0,
             ),
-        )(base, ends_pad, cells, weights)
+        )(offs, seg, weights)
     else:
-        out = tab_plain(base, ends_pad, cells, weights, out_width)
+        out = tab_plain(offs, seg, weights, out_width)
     out = out[:, :groups * CELLS].reshape(reps, groups, CELLS)
     return out.transpose(1, 0, 2).reshape(groups, reps * CELLS)
 
@@ -145,20 +140,9 @@
     owners = lax.axis_size("rows")
     county_here = age_rate.shape[0]
     counties = county_here * owners
-    group_range = jnp.arange(groups, dtype=jnp.int32)
-    same = county[:, None] == county[None, :]
-    earlier = group_range[:, None] > group_range[None, :]
-    second = jnp.any(same & earlier, axis=1)
     county_range = jnp.arange(counties, dtype=jnp.int32)
     hits = county[None, :] == county_range[:, None]
-    first_hit = hits & ~second[None, :]
-    second_hit = hits & second[None, :]
-    pick1 = jnp.where(jnp.any(first_hit, axis=1),
-                      jnp.sum(jnp.where(first_hit, group_range[None, :], 0), axis=1), groups)
-    pick2 = jnp.where(jnp.any(second_hit, axis=1),
-                      jnp.sum(jnp.where(second_hit, group_range[None, :], 0), axis=1), groups)
-    padded = jnp.concatenate([tables, jnp.zeros((1, width), tables.dtype)], axis=0)
-    partial = jnp.take(padded, pick1, axis=0) + jnp.take(padded, pick2, axis=0)
+    partial = exact_dot(hits.astype(jnp.float32), tables)
     present = jnp.sum(hits.astype(jnp.float32), axis=1).reshape(owners, 1, county_here)
     present = jnp.pad(present, ((0, 0), (0, 0), (0, width - county_here)))
     outgoing = jnp.concatenate([partial.reshape(owners, county_here, width), present], axis=1)

time: 185 us -> 170 us (0.919)
  local copies, waits for them, and re-layouts: 35.5 us -> 23.9 us
  matrix products: 7.7 us -> 13 us
  other arithmetic: 15.7 us -> 11.5 us
  waiting for transfers between devices: 54.7 us -> 51.5 us
    gather x2 -> x0, local copies, waits for them, and re-layouts: 10.3 us -> none  [local(): partial = jnp.take(padded, pick1, axis=0) + jnp.take(padded, pick2, axis=0)]
    dot_general x5 -> x6, matrix products: 7.7 us -> 13 us  [exact_dot(): jnp.dot(left, right, precision=lax.Precision.HIGHEST, preferred_element_t...]
    all_to_all x1, waiting for transfers between devices: 40.7 us -> 37.4 us  [local(): lax.all_to_all(outgoing.reshape(owners * (county_here + 1), width), 'rows...]
    reduce_or x2 -> x0, other arithmetic: 3.05 us -> none  [the longest x1 1.76 us: local(): jnp.any(first_hit, axis=1)]
    concatenate x2 -> x0, local copies, waits for them, and re-layouts: 2.51 us -> none  [the longest x1 1.91 us: local(): jnp.concatenate([tables, jnp.zeros((1, width), tables.dtype)], axis=0)]
  transfers between devices with their start and end apart: 4 -> 4, of which waited for: 3 -> 3; matrix products, arithmetic and copies ran while one was open for 0% -> 2% of each run, Pallas kernels for 0% -> 0%
where the time goes in v3:
time: 170 us; the launch traced here: 169 us
  waiting for transfers between devices  51.5 us (30%)
  Pallas kernels  30.2 us (18%)
  blocking collectives  25.1 us (15%)
  local copies, waits for them, and re-layouts  23.9 us (14%)
  starting transfers between devices  13.1 us (8%)
  matrix products  13 us (8%)
  other arithmetic  11.5 us (7%)
    all_to_all x1, waiting for transfers between devices, local(): lax.all_to_all(outgoing.reshape(owners * (county_here + 1), width), 'rows...  37.4 us
    pallas_call x1, Pallas kernels, tabulate(): pl.pallas_call(tab_kernel, out_shape=jax.ShapeDtypeStruct((reps, out_widt...  30.2 us
    all_gather x1, blocking collectives, local(): factors = lax.all_gather(factors, 'rows', tiled=True)  25.1 us
    ppermute x3, waiting for transfers between devices, local(): lax.ppermute(stats, 'rep', [(i, (i + s) % shards) for i in range(shards)])  14.1 us
    dot_general x6, matrix products, exact_dot(): jnp.dot(left, right, precision=lax.Precision.HIGHEST, preferred_element_t...  13 us
    all_to_all x1, starting transfers between devices, local(): lax.all_to_all(outgoing.reshape(owners * (county_here + 1), width), 'rows...  8.59 us
    transpose x1, local copies, waits for them, and re-layouts, tabulate(): return out.transpose(1, 0, 2).reshape(groups, reps * CELLS)  6.57 us
    reshape x1, local copies, waits for them, and re-layouts, tabulate(): out = out[:, :groups * CELLS].reshape(reps, groups, CELLS)  5.43 us
  transfers between devices with their start and end apart: 4, of which 3 were waited for; matrix products, arithmetic and copies ran while one was open for 2% of the time, Pallas kernels for 0%

profile of v3, /device:TPU:1, one launch (start us, length us, event | category | flops | bytes accessed | tf_op | source)
XLA Modules:
  0.0 169.4 jit_solution(8597761210685574929)
XLA Ops:
  0.7 1.0 reduce-window.9
  2.3 2.7 %select_reduce_fusion.6 = (s32[512]{0:T(512)S(1)}, s32[512]{0:T(512)S(1)}, s32[512]{0:T(512)S(1)}, s32[512]{0:T(512)S(1)}, s32[512]{0:T(512)S(1)}, /*index=5*/s32[512]{0:T(512)S(1)}, s32[512]{0:T(512)S(1)}) fusion(s32[512]{0:T(512)S(1)} %get-tuple-element.12, s32[1024]{0:T(1024)S(1)} %add_bitcast_fusion, s32[512]{0:T(512)S(1)} %get-tuple-element.43, ...), kind=kLoop, calls=%fused_computation.25 | loop fusion | flops 11006464 | bytes 32768 | tf_op jit(solution)/shard_map/reduce_sum | solution.py:66
  5.6 2.3 %bitcast_add_fusion.seg_ref = s32[512,128]{1,0:T(8,128)} fusion(s32[65536]{0:T(1024)} %param.7, s32[512]{0:T(512)S(1)} %get-tuple-element.37, s32[512]{0:T(512)S(1)} %get-tuple-element.32, s32[512]{0:T(512)S(1)} %get-tuple-element.35, s32[512]{0:T(512)S(1)} %get-tuple-element.36, s32[512]{0:T(512)S(1)} %get-tuple-element.33, s32[512]{0:T(512)S(1)} %get-tuple-element.34, ...), kind=kLoop, calls=%fused_computation.39 | loop fusion | flops 1507328 | bytes 540672 | tf_op jit(solution)/shard_map/add | solution.py:69
  7.9 30.2 %shard_map.77 = f32[20,33024]{1,0:T(8,128)} custom-call(s32[512]{0:T(512)} %get-tuple-element.38.offs_ref, s32[512,128]{1,0:T(8,128)} %bitcast_add_fusion.seg_ref, bf16[20,65536]{1,0:T(8,128)(2,1)} %w_ref.1), custom_call_target="tpu_custom_call" | custom-call | flops 671088640 | bytes 5525504 | tf_op jit(solution)/shard_map/pallas_call | solution.py:73
  38.1 1.9 %slice-done = f32[20,32768]{1,0:T(8,128)S(1)} async-done(((f32[20,33024]{1,0:T(8,128)}), f32[20,32768]{1,0:T(8,128)S(1)}, s32[]{:S(2)}) %slice-start) | async-done | bytes 2621464 | tf_op jit(solution)/shard_map/slice | solution.py:90
  40.0 5.4 %reshape.442 = f32[20,1024,32]{2,1,0:T(8,128)} reshape(f32[20,32768]{1,0:T(8,128)S(1)} %slice-done) | data formatting | bytes 5242880 | tf_op jit(solution)/shard_map/reshape | solution.py:90
  45.4 6.6 %copy.19 = f32[1024,20,32]{0,2,1:T(8,128)S(1)} copy(f32[1024,20,32]{2,0,1:T(8,128)} %bitcast.26) | data formatting | bytes 5242880 | tf_op jit(solution)/shard_map/transpose | solution.py:91
  52.6 5.4 %fusion = f32[32,32,640]{2,1,0:T(8,128)S(1)} fusion(f32[1024,640,1]{0,1,2:T(8,128)S(1)} %bitcast.27, s32[32,32]{1,0:T(8,128)S(1)} %multiply_add_fusion, s32[1024]{0:T(1024)S(1)} %bitcast.35), kind=kOutput, calls=%fused_computation.3 | convolution fusion | flops 8054112256 | bytes 5251072 | tf_op jit(solution)/shard_map/dot_general | solution.py:95
  58.0 1.9 %select_maximum_fusion = f32[32,33,640]{2,1,0:T(8,128)} fusion(f32[32,1,32]{2,1,0:T(1,128)S(1)} %reshape.444, f32[32,32,640]{2,1,0:T(8,128)S(1)} %fusion), kind=kLoop, calls=%fused_computation.5 | loop fusion | flops 2027520 | bytes 5328896 | tf_op jit(solution)/shard_map/concatenate | solution.py:148
  59.9 8.6 %all-to-all-start = ((f32[32,33,640]{2,1,0:T(8,128)}), f32[32,33,640]{2,1,0:T(8,128)S(1)}, u32[]{:S(2)}, u32[]{:S(2)}) async-start(f32[32,33,640]{2,1,0:T(8,128)} %select_maximum_fusion), calls=%async_computation | async-start | bytes 6553600 | tf_op jit(solution)/shard_map/all_to_all | solution.py:149
  68.5 3.3 %copy.26 = f32[1024,640]{1,0:T(8,128)} copy(f32[1024,640]{0,1:T(8,128)} %bitcast.28) | data formatting | bytes 5242880 | tf_op jit(solution)/shard_map/reshape | solution.py:91
  71.8 37.4 %all-to-all-done = f32[32,33,640]{2,1,0:T(8,128)S(1)} async-done(((f32[32,33,640]{2,1,0:T(8,128)}), f32[32,33,640]{2,1,0:T(8,128)S(1)}, u32[]{:S(2)}, u32[]{:S(2)}) %all-to-all-start) | async-done | bytes 2703392 | tf_op jit(solution)/shard_map/all_to_all | solution.py:149
  113.1 25.1 %all_gather.3 = f32[1024,240]{1,0:T(8,128)S(1)} all-gather(f32[32,240]{1,0:T(8,128)S(1)} %pad_maximum_fusion.1), channel_id=1, replica_groups=mesh['rows'=32,'rep'=4] {'rows'}, dimensions={0}, use_global_device_ids=true | all-gather | bytes 1013760 | tf_op jit(solution)/shard_map/all_gather | solution.py:156
  138.2 3.5 %gather_fusion = f32[1024,240]{1,0:T(8,128)S(1)} fusion(f32[1024,240]{1,0:T(8,128)S(1)} %all_gather.3, s32[1024]{0:T(1024)S(1)} %broadcast_clamp_fusion), kind=kCustom, calls=%fused_computation | custom fusion | bytes 1970176 | tf_op jit(solution)/shard_map/jit(_take)/gather | solution.py:157
  141.8 1.3 fusion.8
  143.4 1.8 %multiply_multiply_fusion = f32[1024,640]{1,0:T(8,128)S(1)} fusion(f32[1024,640]{1,0:T(8,128)S(1)} %copy-done.1, f32[1024,640]{1,0:T(8,128)S(1)} %fusion.8, f32[1024,240]{1,0:T(8,128)S(1)} %broadcast_select_fusion, s32[640]{0:T(1024)S(1)} %add_select_fusion, s32[640]{0:T(1024)S(1)} %get-tuple-element.45, s32[160]{0:T(256)S(1)} %get-tuple-element.48, ...), kind=kOutput, calls=%fused_computation.10 | convolution fusion | flops 1259909120 | bytes 8853760 | tf_op jit(solution)/shard_map/dot_general | solution.py:95
  145.2 1.5 fusion.14
  146.6 1.5 fusion.13
  148.2 1.6 fusion.2
  149.8 3.8 %collective-permute-start = (f32[1024,64]{0,1:T(8,128)S(1)}, f32[1024,64]{0,1:T(8,128)S(1)}, u32[]{:S(2)}, u32[]{:S(2)}) collective-permute-start(f32[1024,64]{0,1:T(8,128)S(1)} %pad_maximum_fusion), channel_id=1, source_target_pairs={{0,3},{1,0},{2,1},{3,2},{4,7},{5,4},{6,5},{7,6},{8,11},{9,8},{10,9... | collective-permute-start | bytes 786440 | tf_op jit(solution)/shard_map/ppermute | solution.py:170
  153.7 0.7 collective-permute-start.2
  154.3 10.4 %collective-permute-done = f32[1024,64]{0,1:T(8,128)S(1)} collective-permute-done((f32[1024,64]{0,1:T(8,128)S(1)}, f32[1024,64]{0,1:T(8,128)S(1)}, u32[]{:S(2)}, u32[]{:S(2)}) %collective-permute-start) | collective-permute-done | bytes 262176 | tf_op jit(solution)/shard_map/ppermute | solution.py:170
  164.8 3.6 %collective-permute-done.2 = f32[1024,64]{0,1:T(8,128)S(1)} collective-permute-done((f32[1024,64]{0,1:T(8,128)S(1)}, f32[1024,64]{0,1:T(8,128)S(1)}, u32[]{:S(2)}, u32[]{:S(2)}) %collective-permute-start.2) | collective-permute-done | bytes 262176 | tf_op jit(solution)/shard_map/ppermute | solution.py:170
  168.6 0.8 fusion.33
  (81 shorter events, 6.1 us)
Async XLA Ops:
  38.1 1.9 %slice-start = ((f32[20,33024]{1,0:T(8,128)}), f32[20,32768]{1,0:T(8,128)S(1)}, s32[]{:S(2)}) async-start(f32[20,33024]{1,0:T(8,128)} %shard_map.77), calls=%async_computation.1 | async-start | bytes 6291456 | tf_op jit(solution)/shard_map/slice | solution.py:90
  45.4 6.6 %copy-start.3 = (s32[1024,1]{0,1:T(1,128)S(1)}, s32[1024,1]{0,1:T(1,128)}, u32[]{:S(2)}) copy-start(s32[1024,1]{0,1:T(1,128)} %param.9) | copy-start | bytes 12292
  52.0 6.0 %copy-start.2 = (f32[1024,20,32]{0,2,1:T(8,128)}, f32[1024,20,32]{0,2,1:T(8,128)S(1)}, u32[]{:S(2)}) copy-start(f32[1024,20,32]{0,2,1:T(8,128)S(1)} %copy.19) | copy-start | bytes 7864324
  59.9 49.4 %all-to-all-start = ((f32[32,33,640]{2,1,0:T(8,128)}), f32[32,33,640]{2,1,0:T(8,128)S(1)}, u32[]{:S(2)}, u32[]{:S(2)}) async-start(f32[32,33,640]{2,1,0:T(8,128)} %select_maximum_fusion), calls=%async_computation | async-start | bytes 6553600 | tf_op jit(solution)/shard_map/all_to_all | solution.py:149
  71.8 38.6 %copy-start.5 = (f32[32,4]{0,1:T(4,128)S(1)}, f32[32,4]{0,1:T(4,128)}, u32[]{:S(2)}) copy-start(f32[32,4]{0,1:T(4,128)} %param.10) | copy-start | bytes 1540
  71.8 38.9 %copy-start.4 = (f32[32,8]{0,1:T(8,128)S(1)}, f32[32,8]{0,1:T(8,128)}, u32[]{:S(2)}) copy-start(f32[32,8]{0,1:T(8,128)} %param.11) | copy-start | bytes 3076
  141.6 1.7 %copy-start.1 = (f32[1024,640]{1,0:T(8,128)S(1)}, f32[1024,640]{1,0:T(8,128)}, u32[]{:S(2)}) copy-start(f32[1024,640]{1,0:T(8,128)} %copy.26) | copy-start | bytes 7864324
  145.1 3.0 %copy-start = (f32[1024,640]{1,0:T(8,128)}, f32[1024,640]{1,0:T(8,128)S(1)}, u32[]{:S(2)}) copy-start(f32[1024,640]{1,0:T(8,128)S(1)} %multiply_multiply_fusion) | copy-start | bytes 7864324
  149.8 15.0 %collective-permute-start = (f32[1024,64]{0,1:T(8,128)S(1)}, f32[1024,64]{0,1:T(8,128)S(1)}, u32[]{:S(2)}, u32[]{:S(2)}) collective-permute-start(f32[1024,64]{0,1:T(8,128)S(1)} %pad_maximum_fusion), channel_id=1, source_target_pairs={{0,3},{1,0},{2,1},{3,2},{4,7},{5,4},{6,5},{7,6},{8,11},{9,8},{10,9... | collective-permute-start | bytes 786440 | tf_op jit(solution)/shard_map/ppermute | solution.py:170
  153.6 11.1 %collective-permute-start.1 = (f32[1024,64]{0,1:T(8,128)S(1)}, f32[1024,64]{0,1:T(8,128)S(1)}, u32[]{:S(2)}, u32[]{:S(2)}) collective-permute-start(f32[1024,64]{0,1:T(8,128)S(1)} %pad_maximum_fusion), channel_id=1, source_target_pairs={{0,2},{1,3},{2,0},{3,1},{4,6},{5,7},{6,4},{7,5},{8,10},{9,11},{10,... | collective-permute-start | bytes 786440 | tf_op jit(solution)/shard_map/ppermute | solution.py:170
  153.7 14.8 %collective-permute-start.2 = (f32[1024,64]{0,1:T(8,128)S(1)}, f32[1024,64]{0,1:T(8,128)S(1)}, u32[]{:S(2)}, u32[]{:S(2)}) collective-permute-start(f32[1024,64]{0,1:T(8,128)S(1)} %pad_maximum_fusion), channel_id=1, source_target_pairs={{0,1},{1,2},{2,3},{3,0},{4,5},{5,6},{6,7},{7,4},{8,9},{9,10},{10,1... | collective-permute-start | bytes 786440 | tf_op jit(solution)/shard_map/ppermute | solution.py:170

commit v4 on v3

--- a/solution.py
+++ b/solution.py
@@ -33,7 +33,7 @@
         out_ref[:, pl.ds(off, width)] += part
         return carry
 
-    lax.fori_loop(0, steps, body, 0, unroll=4)
+    lax.fori_loop(0, steps, body, 0, unroll=8)
 
 
 def tab_plain(offs, seg, weights, out_width):
@@ -57,7 +57,7 @@
     steps = records // BLOCK
     block_start = jnp.arange(steps, dtype=jnp.int32) * BLOCK
     first = jnp.sum((ends[None, :] <= block_start[:, None]).astype(jnp.int32), axis=1)
-    base = (first - first % 4).astype(jnp.int32)
+    base = jnp.minimum(first - first % 4, groups - SPAN).astype(jnp.int32)
     group_range = jnp.arange(groups, dtype=jnp.int32)
     place = block_start[:, None] + jnp.arange(BLOCK, dtype=jnp.int32)[None, :]
     local = jnp.zeros((steps, BLOCK), jnp.int32)
@@ -68,7 +68,7 @@
         local = local + (place >= edge[:, None]).astype(jnp.int32)
     seg = local * CELLS + cell_ids.reshape(steps, BLOCK)
     offs = (base * CELLS).astype(jnp.int32)
-    out_width = (groups + SPAN) * CELLS
+    out_width = groups * CELLS
     if USE_KERNEL:
         out = pl.pallas_call(
             tab_kernel,
@@ -87,7 +87,7 @@
         )(offs, seg, weights)
     else:
         out = tab_plain(offs, seg, weights, out_width)
-    out = out[:, :groups * CELLS].reshape(reps, groups, CELLS)
+    out = out.reshape(reps, groups, CELLS)
     return out.transpose(1, 0, 2).reshape(groups, reps * CELLS)
 
 
@@ -153,7 +153,10 @@
     county_tables = summed[:county_here]
     groups_in = summed[county_here, :county_here]
     factors = rake_own(county_tables, groups_in, age_rate, kind_rate)
-    factors = lax.all_gather(factors, "rows", tiled=True)
+    sent = jnp.broadcast_to(factors[None], (owners,) + factors.shape)
+    factors = lax.all_to_all(
+        sent.reshape(owners * county_here, factors.shape[1]), "rows", 0, 0, tiled=True
+    )
     mine = jnp.take(factors, county, axis=0)
     to_age, to_kind, cell_sum = spreaders(reps)
     factor = exact_dot(mine[:, :reps * AGES], to_age) * exact_dot(mine[:, reps * AGES:], to_kind)

time: 170 us -> 158 us (0.929)
  blocking collectives: 25.1 us -> 49.7 us
  waiting for transfers between devices: 51.5 us -> 27.9 us
  Pallas kernels: 30.2 us -> 22.7 us
  starting transfers between devices: 13.1 us -> 8.51 us
    all_to_all x0 -> x1, blocking collectives: none -> 49.7 us  [local(): lax.all_to_all(outgoing.reshape(owners * (county_here + 1), width), 'rows...]
    all_gather x1 -> x0, blocking collectives: 25.1 us -> none  [local(): factors = lax.all_gather(factors, 'rows', tiled=True)]
    all_to_all x1, waiting for transfers between devices: 37.4 us -> 13.8 us  [local(): lax.all_to_all(sent.reshape(owners * county_here, factors.shape[1]), 'row...]
    pallas_call x1, Pallas kernels: 30.2 us -> 22.7 us  [tabulate(): pl.pallas_call(tab_kernel, out_shape=jax.ShapeDtypeStruct((reps, out_widt...]
    all_to_all x1, starting transfers between devices: 8.59 us -> 3.99 us  [local(): lax.all_to_all(sent.reshape(owners * county_here, factors.shape[1]), 'row...]
    slice x3 -> x1, local copies, waits for them, and re-layouts: 1.96 us -> 0.07 us  [the longest x2 1.89 us: tabulate(): out = out[:, :groups * CELLS].reshape(reps, groups, CELLS)]
where the time goes in v4:
time: 158 us; the launch traced here: 157 us
  blocking collectives  49.7 us (31%)
  waiting for transfers between devices  27.9 us (18%)
  local copies, waits for them, and re-layouts  24.3 us (15%)
  Pallas kernels  22.7 us (14%)
  matrix products  13 us (8%)
  other arithmetic  9.8 us (6%)
  starting transfers between devices  8.51 us (5%)
    all_to_all x1, blocking collectives, local(): lax.all_to_all(outgoing.reshape(owners * (county_here + 1), width), 'rows...  49.7 us
    pallas_call x1, Pallas kernels, tabulate(): pl.pallas_call(tab_kernel, out_shape=jax.ShapeDtypeStruct((reps, out_widt...  22.7 us
    ppermute x3, waiting for transfers between devices, local(): lax.ppermute(stats, 'rep', [(i, (i + s) % shards) for i in range(shards)])  14.1 us
    all_to_all x1, waiting for transfers between devices, local(): lax.all_to_all(sent.reshape(owners * county_here, factors.shape[1]), 'row...  13.8 us
    dot_general x6, matrix products, exact_dot(): jnp.dot(left, right, precision=lax.Precision.HIGHEST, preferred_element_t...  13 us
    reshape x1, local copies, waits for them, and re-layouts, tabulate(): out = out.reshape(reps, groups, CELLS)  6.69 us
    transpose x1, local copies, waits for them, and re-layouts, tabulate(): return out.transpose(1, 0, 2).reshape(groups, reps * CELLS)  6.57 us
    ppermute x3, starting transfers between devices, local(): lax.ppermute(stats, 'rep', [(i, (i + s) % shards) for i in range(shards)])  4.53 us
  transfers between devices with their start and end apart: 4, of which 3 were waited for; matrix products, arithmetic and copies ran while one was open for 2% of the time, Pallas kernels for 0%

profile of v4, /device:TPU:1, one launch (start us, length us, event | category | flops | bytes accessed | tf_op | source)
XLA Modules:
  0.0 157.0 jit_solution(10357837577650951169)
XLA Ops:
  0.7 1.0 reduce-window.9
  2.3 2.7 %select_reduce_fusion.6 = (s32[512]{0:T(512)S(1)}, s32[512]{0:T(512)S(1)}, s32[512]{0:T(512)S(1)}, s32[512]{0:T(512)S(1)}, s32[512]{0:T(512)S(1)}, /*index=5*/s32[512]{0:T(512)S(1)}, s32[512]{0:T(512)S(1)}) fusion(s32[512]{0:T(512)S(1)} %get-tuple-element.12, s32[1024]{0:T(1024)S(1)} %add_bitcast_fusion, s32[512]{0:T(512)S(1)} %get-tuple-element.43, ...), kind=kLoop, calls=%fused_computation.25 | loop fusion | flops 11006464 | bytes 32768 | tf_op jit(solution)/shard_map/reduce_sum | solution.py:66
  5.0 0.6 compare_select_fusion.7
  5.6 2.3 %bitcast_add_fusion.seg_ref = s32[512,128]{1,0:T(8,128)} fusion(s32[65536]{0:T(1024)} %param.7, s32[512]{0:T(512)S(1)} %get-tuple-element.37, s32[512]{0:T(512)S(1)} %get-tuple-element.32, s32[512]{0:T(512)S(1)} %get-tuple-element.35, s32[512]{0:T(512)S(1)} %get-tuple-element.36, s32[512]{0:T(512)S(1)} %get-tuple-element.33, s32[512]{0:T(512)S(1)} %get-tuple-element.34, ...), kind=kLoop, calls=%fused_computation.39 | loop fusion | flops 1507328 | bytes 540672 | tf_op jit(solution)/shard_map/add | solution.py:69
  7.9 22.7 %shard_map.77 = f32[20,32768]{1,0:T(8,128)} custom-call(s32[512]{0:T(512)} %get-tuple-element.38.offs_ref, s32[512,128]{1,0:T(8,128)} %bitcast_add_fusion.seg_ref, bf16[20,65536]{1,0:T(8,128)(2,1)} %w_ref.1), custom_call_target="tpu_custom_call" | custom-call | flops 671088640 | bytes 5505024 | tf_op jit(solution)/shard_map/pallas_call | solution.py:73
  30.5 6.7 %reshape.448 = f32[20,1024,32]{2,1,0:T(8,128)} reshape(f32[20,32768]{1,0:T(8,128)} %shard_map.77) | data formatting | bytes 5242880 | tf_op jit(solution)/shard_map/reshape | solution.py:90
  37.2 6.6 %copy.26 = f32[1024,20,32]{0,2,1:T(8,128)S(1)} copy(f32[1024,20,32]{2,0,1:T(8,128)} %bitcast.28) | data formatting | bytes 5242880 | tf_op jit(solution)/shard_map/transpose | solution.py:91
  44.4 5.4 %fusion = f32[32,32,640]{2,1,0:T(8,128)S(1)} fusion(f32[1024,640,1]{0,1,2:T(8,128)S(1)} %bitcast.29, s32[32,32]{1,0:T(8,128)S(1)} %multiply_add_fusion, s32[1024]{0:T(1024)S(1)} %bitcast.37), kind=kOutput, calls=%fused_computation.3 | convolution fusion | flops 8054112256 | bytes 5251072 | tf_op jit(solution)/shard_map/dot_general | solution.py:95
  50.0 49.7 %all_to_all.15 = f32[32,33,640]{2,1,0:T(8,128)S(1)} all-to-all(f32[32,33,640]{2,1,0:T(8,128)S(1)} %select_maximum_fusion), channel_id=1, replica_groups=mesh['rows'=32,'rep'=4] {'rows'}, dimensions={0} | all-to-all | bytes 5406720 | tf_op jit(solution)/shard_map/all_to_all | solution.py:149
  103.5 1.1 broadcast_in_dim.62
  104.6 4.0 %all-to-all-start.1 = ((f32[32,32,240]{2,1,0:T(8,128)}), f32[32,32,240]{2,1,0:T(8,128)S(1)}, u32[]{:S(2)}, u32[]{:S(2)}) async-start(f32[32,32,240]{2,1,0:T(8,128)} %broadcast_in_dim.62), calls=%async_computation.1 | async-start | bytes 2097152 | tf_op jit(solution)/shard_map/all_to_all | solution.py:157
  108.6 3.2 %copy.33 = f32[1024,640]{1,0:T(8,128)} copy(f32[1024,640]{0,1:T(8,128)} %bitcast.30) | data formatting | bytes 5242880 | tf_op jit(solution)/shard_map/reshape | solution.py:91
  111.9 13.8 %all-to-all-done.1 = f32[32,32,240]{2,1,0:T(8,128)S(1)} async-done(((f32[32,32,240]{2,1,0:T(8,128)}), f32[32,32,240]{2,1,0:T(8,128)S(1)}, u32[]{:S(2)}, u32[]{:S(2)}) %all-to-all-start.1) | async-done | bytes 983072 | tf_op jit(solution)/shard_map/all_to_all | solution.py:157
  125.8 3.5 %gather_fusion = f32[1024,240]{1,0:T(8,128)S(1)} fusion(f32[1024,240]{1,0:T(8,128)S(1)} %bitcast.27, s32[1024]{0:T(1024)S(1)} %broadcast_clamp_fusion), kind=kCustom, calls=%fused_computation | custom fusion | bytes 1970176 | tf_op jit(solution)/shard_map/jit(_take)/gather | solution.py:160
  129.5 1.3 fusion.8
  131.0 1.8 %multiply_multiply_fusion = f32[1024,640]{1,0:T(8,128)S(1)} fusion(f32[1024,640]{1,0:T(8,128)S(1)} %copy-done.2, f32[1024,640]{1,0:T(8,128)S(1)} %fusion.8, f32[1024,240]{1,0:T(8,128)S(1)} %broadcast_select_fusion, s32[640]{0:T(1024)S(1)} %add_select_fusion, s32[640]{0:T(1024)S(1)} %get-tuple-element.45, s32[160]{0:T(256)S(1)} %get-tuple-element.48, ...), kind=kOutput, calls=%fused_computation.10 | convolution fusion | flops 1259909120 | bytes 8853760 | tf_op jit(solution)/shard_map/dot_general | solution.py:95
  132.8 1.5 fusion.14
  134.2 1.5 fusion.13
  135.8 1.6 %fusion.2 = f32[1024,32]{0,1:T(8,128)S(1)} fusion(f32[1024,640]{1,0:T(8,128)S(1)} %multiply_multiply_fusion, f32[1024,640]{1,0:T(8,128)S(1)} %fusion.13, s32[640]{0:T(1024)S(1)} %fusion.43), kind=kOutput, calls=%fused_computation.7 | convolution fusion | flops 252989440 | bytes 5376512 | tf_op jit(solution)/shard_map/dot_general | solution.py:95
  137.4 3.8 %collective-permute-start = (f32[1024,64]{0,1:T(8,128)S(1)}, f32[1024,64]{0,1:T(8,128)S(1)}, u32[]{:S(2)}, u32[]{:S(2)}) collective-permute-start(f32[1024,64]{0,1:T(8,128)S(1)} %pad_maximum_fusion), channel_id=1, source_target_pairs={{0,3},{1,0},{2,1},{3,2},{4,7},{5,4},{6,5},{7,6},{8,11},{9,8},{10,9... | collective-permute-start | bytes 786440 | tf_op jit(solution)/shard_map/ppermute | solution.py:173
  141.3 0.7 collective-permute-start.2
  142.0 10.2 %collective-permute-done = f32[1024,64]{0,1:T(8,128)S(1)} collective-permute-done((f32[1024,64]{0,1:T(8,128)S(1)}, f32[1024,64]{0,1:T(8,128)S(1)}, u32[]{:S(2)}, u32[]{:S(2)}) %collective-permute-start) | collective-permute-done | bytes 262176 | tf_op jit(solution)/shard_map/ppermute | solution.py:173
  152.2 3.9 %collective-permute-done.2 = f32[1024,64]{0,1:T(8,128)S(1)} collective-permute-done((f32[1024,64]{0,1:T(8,128)S(1)}, f32[1024,64]{0,1:T(8,128)S(1)}, u32[]{:S(2)}, u32[]{:S(2)}) %collective-permute-start.2) | collective-permute-done | bytes 262176 | tf_op jit(solution)/shard_map/ppermute | solution.py:173
  156.2 0.8 fusion.33
  (80 shorter events, 5.7 us)
Async XLA Ops:
  37.2 6.6 %copy-start.4 = (s32[1024,1]{0,1:T(1,128)S(1)}, s32[1024,1]{0,1:T(1,128)}, u32[]{:S(2)}) copy-start(s32[1024,1]{0,1:T(1,128)} %param.9) | copy-start | bytes 12292
  43.8 6.0 %copy-start.1 = (f32[1024,20,32]{0,2,1:T(8,128)}, f32[1024,20,32]{0,2,1:T(8,128)S(1)}, u32[]{:S(2)}) copy-start(f32[1024,20,32]{0,2,1:T(8,128)S(1)} %copy.26) | copy-start | bytes 7864324
  99.7 1.2 copy-start.5
  99.7 1.4 copy-start.3
  104.6 21.2 %all-to-all-start.1 = ((f32[32,32,240]{2,1,0:T(8,128)}), f32[32,32,240]{2,1,0:T(8,128)S(1)}, u32[]{:S(2)}, u32[]{:S(2)}) async-start(f32[32,32,240]{2,1,0:T(8,128)} %broadcast_in_dim.62), calls=%async_computation.1 | async-start | bytes 2097152 | tf_op jit(solution)/shard_map/all_to_all | solution.py:157
  129.2 1.7 %copy-start.2 = (f32[1024,640]{1,0:T(8,128)S(1)}, f32[1024,640]{1,0:T(8,128)}, u32[]{:S(2)}) copy-start(f32[1024,640]{1,0:T(8,128)} %copy.33) | copy-start | bytes 7864324
  132.8 3.0 %copy-start = (f32[1024,640]{1,0:T(8,128)}, f32[1024,640]{1,0:T(8,128)S(1)}, u32[]{:S(2)}) copy-start(f32[1024,640]{1,0:T(8,128)S(1)} %multiply_multiply_fusion) | copy-start | bytes 7864324
  137.4 14.7 %collective-permute-start = (f32[1024,64]{0,1:T(8,128)S(1)}, f32[1024,64]{0,1:T(8,128)S(1)}, u32[]{:S(2)}, u32[]{:S(2)}) collective-permute-start(f32[1024,64]{0,1:T(8,128)S(1)} %pad_maximum_fusion), channel_id=1, source_target_pairs={{0,3},{1,0},{2,1},{3,2},{4,7},{5,4},{6,5},{7,6},{8,11},{9,8},{10,9... | collective-permute-start | bytes 786440 | tf_op jit(solution)/shard_map/ppermute | solution.py:173
  141.3 10.9 %collective-permute-start.1 = (f32[1024,64]{0,1:T(8,128)S(1)}, f32[1024,64]{0,1:T(8,128)S(1)}, u32[]{:S(2)}, u32[]{:S(2)}) collective-permute-start(f32[1024,64]{0,1:T(8,128)S(1)} %pad_maximum_fusion), channel_id=1, source_target_pairs={{0,2},{1,3},{2,0},{3,1},{4,6},{5,7},{6,4},{7,5},{8,10},{9,11},{10,... | collective-permute-start | bytes 786440 | tf_op jit(solution)/shard_map/ppermute | solution.py:173
  141.3 14.8 %collective-permute-start.2 = (f32[1024,64]{0,1:T(8,128)S(1)}, f32[1024,64]{0,1:T(8,128)S(1)}, u32[]{:S(2)}, u32[]{:S(2)}) collective-permute-start(f32[1024,64]{0,1:T(8,128)S(1)} %pad_maximum_fusion), channel_id=1, source_target_pairs={{0,1},{1,2},{2,3},{3,0},{4,5},{5,6},{6,7},{7,4},{8,9},{9,10},{10,1... | collective-permute-start | bytes 786440 | tf_op jit(solution)/shard_map/ppermute | solution.py:173

commit v5 on v4

--- a/solution.py
+++ b/solution.py
@@ -146,12 +146,18 @@
     present = jnp.sum(hits.astype(jnp.float32), axis=1).reshape(owners, 1, county_here)
     present = jnp.pad(present, ((0, 0), (0, 0), (0, width - county_here)))
     outgoing = jnp.concatenate([partial.reshape(owners, county_here, width), present], axis=1)
+    half = width // 2
+    core = lax.axis_index("rows") % 2
+    low, high = outgoing[:, :, :half], outgoing[:, :, half:]
+    keep = jnp.where(core == 0, low, high)
+    give = jnp.where(core == 0, high, low)
+    keep = keep + lax.ppermute(give, "rows", [(i, i ^ 1) for i in range(owners)])
     arrived = lax.all_to_all(
-        outgoing.reshape(owners * (county_here + 1), width), "rows", 0, 0, tiled=True
-    ).reshape(owners, county_here + 1, width)
+        keep.reshape(owners * (county_here + 1), half), "rows", 0, 0, tiled=True
+    ).reshape(owners // 2, 2, county_here + 1, half)
     summed = jnp.sum(arrived, axis=0)
-    county_tables = summed[:county_here]
-    groups_in = summed[county_here, :county_here]
+    county_tables = jnp.concatenate([summed[0, :county_here], summed[1, :county_here]], axis=1)
+    groups_in = summed[0, county_here, :county_here]
     factors = rake_own(county_tables, groups_in, age_rate, kind_rate)
     sent = jnp.broadcast_to(factors[None], (owners,) + factors.shape)
     factors = lax.all_to_all(

time: 158 us -> 149 us (0.943)
  blocking collectives: 49.7 us -> 34.2 us
  waiting for transfers between devices: 27.9 us -> 31 us
  other arithmetic: 9.8 us -> 11.5 us
  starting transfers between devices: 8.51 us -> 10.2 us
    all_to_all x1, blocking collectives: 49.7 us -> 34.2 us  [local(): lax.all_to_all(keep.reshape(owners * (county_here + 1), half), 'rows', 0,...]
    ppermute x0 -> x1, waiting for transfers between devices: none -> 3.11 us  [local(): lax.ppermute(give, 'rows', [(i, i ^ 1) for i in range(owners)])]
    ppermute x0 -> x1, starting transfers between devices: none -> 1.64 us  [local(): lax.ppermute(give, 'rows', [(i, i ^ 1) for i in range(owners)])]
  transfers between devices with their start and end apart: 4 -> 5, of which waited for: 3 -> 4; matrix products, arithmetic and copies ran while one was open for 2% -> 2% of each run, Pallas kernels for 0% -> 0%
where the time goes in v5:
time: 149 us; the launch traced here: 148 us
  blocking collectives  34.2 us (23%)
  waiting for transfers between devices  31 us (21%)
  local copies, waits for them, and re-layouts  24.7 us (17%)
  Pallas kernels  22.7 us (15%)
  matrix products  13 us (9%)
  other arithmetic  11.5 us (8%)
  starting transfers between devices  10.2 us (7%)
    all_to_all x1, blocking collectives, local(): lax.all_to_all(keep.reshape(owners * (county_here + 1), half), 'rows', 0,...  34.2 us
    pallas_call x1, Pallas kernels, tabulate(): pl.pallas_call(tab_kernel, out_shape=jax.ShapeDtypeStruct((reps, out_widt...  22.7 us
    ppermute x3, waiting for transfers between devices, local(): lax.ppermute(stats, 'rep', [(i, (i + s) % shards) for i in range(shards)])  14.1 us
    all_to_all x1, waiting for transfers between devices, local(): lax.all_to_all(sent.reshape(owners * county_here, factors.shape[1]), 'row...  13.8 us
    dot_general x6, matrix products, exact_dot(): jnp.dot(left, right, precision=lax.Precision.HIGHEST, preferred_element_t...  13 us
    reshape x1, local copies, waits for them, and re-layouts, tabulate(): out = out.reshape(reps, groups, CELLS)  6.69 us
    transpose x1, local copies, waits for them, and re-layouts, tabulate(): return out.transpose(1, 0, 2).reshape(groups, reps * CELLS)  6.57 us
    ppermute x3, starting transfers between devices, local(): lax.ppermute(stats, 'rep', [(i, (i + s) % shards) for i in range(shards)])  4.53 us
  transfers between devices with their start and end apart: 5, of which 4 were waited for; matrix products, arithmetic and copies ran while one was open for 2% of the time, Pallas kernels for 0%

profile of v5, /device:TPU:1, one launch (start us, length us, event | category | flops | bytes accessed | tf_op | source)
XLA Modules:
  0.0 148.5 jit_solution(2731165777697582094)
XLA Ops:
  0.7 1.0 reduce-window.9
  2.3 2.7 %select_reduce_fusion.6 = (s32[512]{0:T(512)S(1)}, s32[512]{0:T(512)S(1)}, s32[512]{0:T(512)S(1)}, s32[512]{0:T(512)S(1)}, s32[512]{0:T(512)S(1)}, /*index=5*/s32[512]{0:T(512)S(1)}, s32[512]{0:T(512)S(1)}) fusion(s32[512]{0:T(512)S(1)} %get-tuple-element.12, s32[1024]{0:T(1024)S(1)} %add_bitcast_fusion, s32[512]{0:T(512)S(1)} %get-tuple-element.45, ...), kind=kLoop, calls=%fused_computation.25 | loop fusion | flops 11006464 | bytes 32768 | tf_op jit(solution)/shard_map/reduce_sum | solution.py:66
  5.6 2.3 %bitcast_add_fusion.seg_ref = s32[512,128]{1,0:T(8,128)} fusion(s32[65536]{0:T(1024)} %param.7, s32[512]{0:T(512)S(1)} %get-tuple-element.39, s32[512]{0:T(512)S(1)} %get-tuple-element.34, s32[512]{0:T(512)S(1)} %get-tuple-element.37, s32[512]{0:T(512)S(1)} %get-tuple-element.38, s32[512]{0:T(512)S(1)} %get-tuple-element.35, s32[512]{0:T(512)S(1)} %get-tuple-element.36, ...), kind=kLoop, calls=%fused_computation.42 | loop fusion | flops 1507328 | bytes 540672 | tf_op jit(solution)/shard_map/add | solution.py:69
  7.9 22.7 %shard_map.77 = f32[20,32768]{1,0:T(8,128)} custom-call(s32[512]{0:T(512)} %get-tuple-element.40.offs_ref, s32[512,128]{1,0:T(8,128)} %bitcast_add_fusion.seg_ref, bf16[20,65536]{1,0:T(8,128)(2,1)} %w_ref.1), custom_call_target="tpu_custom_call" | custom-call | flops 671088640 | bytes 5505024 | tf_op jit(solution)/shard_map/pallas_call | solution.py:73
  30.5 6.7 %reshape.452 = f32[20,1024,32]{2,1,0:T(8,128)} reshape(f32[20,32768]{1,0:T(8,128)} %shard_map.77) | data formatting | bytes 5242880 | tf_op jit(solution)/shard_map/reshape | solution.py:90
  37.2 6.6 %copy.28 = f32[1024,20,32]{0,2,1:T(8,128)S(1)} copy(f32[1024,20,32]{2,0,1:T(8,128)} %bitcast.30) | data formatting | bytes 5242880 | tf_op jit(solution)/shard_map/transpose | solution.py:91
  44.4 5.4 %fusion = f32[32,32,640]{2,1,0:T(8,128)S(1)} fusion(f32[1024,640,1]{0,1,2:T(8,128)S(1)} %bitcast.31, s32[32,32]{1,0:T(8,128)S(1)} %multiply_add_fusion, s32[1024]{0:T(1024)S(1)} %bitcast.39), kind=kOutput, calls=%fused_computation.3 | convolution fusion | flops 8054112256 | bytes 5251072 | tf_op jit(solution)/shard_map/dot_general | solution.py:95
  50.9 1.6 %collective-permute-start = (f32[32,33,320]{2,0,1:T(8,128)S(1)}, f32[32,33,320]{2,0,1:T(8,128)S(1)}, u32[]{:S(2)}, u32[]{:S(2)}) collective-permute-start(f32[32,33,320]{2,0,1:T(8,128)S(1)} %copy.30), channel_id=1, source_target_pairs={{0,4},{4,0},{8,12},{12,8},{16,20},{20,16},{24,28},{28,24},{32,36},... | collective-permute-start | bytes 4055048 | tf_op jit(solution)/shard_map/ppermute | solution.py:154
  52.6 3.1 %collective-permute-done = f32[32,33,320]{2,0,1:T(8,128)S(1)} collective-permute-done((f32[32,33,320]{2,0,1:T(8,128)S(1)}, f32[32,33,320]{2,0,1:T(8,128)S(1)}, u32[]{:S(2)}, u32[]{:S(2)}) %collective-permute-start) | collective-permute-done | bytes 1351712 | tf_op jit(solution)/shard_map/ppermute | solution.py:154
  55.7 1.1 copy_add_fusion
  56.8 34.2 %all_to_all.15 = f32[32,33,320]{2,1,0:T(8,128)S(1)} all-to-all(f32[32,33,320]{2,1,0:T(8,128)S(1)} %copy_add_fusion), channel_id=1, replica_groups=mesh['rows'=32,'rep'=4] {'rows'}, dimensions={0} | all-to-all | bytes 2703360 | tf_op jit(solution)/shard_map/all_to_all | solution.py:155
  95.0 1.1 broadcast_in_dim.62
  96.1 4.0 %all-to-all-start.1 = ((f32[32,32,240]{2,1,0:T(8,128)}), f32[32,32,240]{2,1,0:T(8,128)S(1)}, u32[]{:S(2)}, u32[]{:S(2)}) async-start(f32[32,32,240]{2,1,0:T(8,128)} %broadcast_in_dim.62), calls=%async_computation.1 | async-start | bytes 2097152 | tf_op jit(solution)/shard_map/all_to_all | solution.py:163
  100.1 3.2 %copy.37 = f32[1024,640]{1,0:T(8,128)} copy(f32[1024,640]{0,1:T(8,128)} %bitcast.32) | data formatting | bytes 5242880 | tf_op jit(solution)/shard_map/reshape | solution.py:91
  103.4 13.8 %all-to-all-done.1 = f32[32,32,240]{2,1,0:T(8,128)S(1)} async-done(((f32[32,32,240]{2,1,0:T(8,128)}), f32[32,32,240]{2,1,0:T(8,128)S(1)}, u32[]{:S(2)}, u32[]{:S(2)}) %all-to-all-start.1) | async-done | bytes 983072 | tf_op jit(solution)/shard_map/all_to_all | solution.py:163
  117.3 3.5 %gather_fusion = f32[1024,240]{1,0:T(8,128)S(1)} fusion(f32[1024,240]{1,0:T(8,128)S(1)} %bitcast.29, s32[1024]{0:T(1024)S(1)} %broadcast_clamp_fusion), kind=kCustom, calls=%fused_computation | custom fusion | bytes 1970176 | tf_op jit(solution)/shard_map/jit(_take)/gather | solution.py:166
  121.0 1.3 fusion.8
  122.5 1.8 %multiply_multiply_fusion = f32[1024,640]{1,0:T(8,128)S(1)} fusion(f32[1024,640]{1,0:T(8,128)S(1)} %copy-done.2, f32[1024,640]{1,0:T(8,128)S(1)} %fusion.8, f32[1024,240]{1,0:T(8,128)S(1)} %broadcast_select_fusion, s32[640]{0:T(1024)S(1)} %add_select_fusion, s32[640]{0:T(1024)S(1)} %get-tuple-element.47, s32[160]{0:T(256)S(1)} %get-tuple-element.50, ...), kind=kOutput, calls=%fused_computation.10 | convolution fusion | flops 1259909120 | bytes 8853760 | tf_op jit(solution)/shard_map/dot_general | solution.py:95
  124.3 1.5 fusion.14
  125.7 1.5 %fusion.13 = f32[1024,640]{1,0:T(8,128)S(1)} fusion(s32[640]{0:T(1024)S(1)} %fusion.43, f32[1024,32]{0,1:T(8,128)S(1)} %fusion.14), kind=kOutput, calls=%fused_computation.39 | convolution fusion | flops 251711488 | bytes 2755072 | tf_op jit(solution)/shard_map/dot_general | solution.py:95
  127.3 1.6 %fusion.2 = f32[1024,32]{0,1:T(8,128)S(1)} fusion(f32[1024,640]{1,0:T(8,128)S(1)} %multiply_multiply_fusion, f32[1024,640]{1,0:T(8,128)S(1)} %fusion.13, s32[640]{0:T(1024)S(1)} %fusion.43), kind=kOutput, calls=%fused_computation.7 | convolution fusion | flops 252989440 | bytes 5376512 | tf_op jit(solution)/shard_map/dot_general | solution.py:95
  128.9 3.8 %collective-permute-start.1 = (f32[1024,64]{0,1:T(8,128)S(1)}, f32[1024,64]{0,1:T(8,128)S(1)}, u32[]{:S(2)}, u32[]{:S(2)}) collective-permute-start(f32[1024,64]{0,1:T(8,128)S(1)} %pad_maximum_fusion), channel_id=1, source_target_pairs={{0,3},{1,0},{2,1},{3,2},{4,7},{5,4},{6,5},{7,6},{8,11},{9,8},{10,9... | collective-permute-start | bytes 786440 | tf_op jit(solution)/shard_map/ppermute | solution.py:179
  133.5 10.2 %collective-permute-done.1 = f32[1024,64]{0,1:T(8,128)S(1)} collective-permute-done((f32[1024,64]{0,1:T(8,128)S(1)}, f32[1024,64]{0,1:T(8,128)S(1)}, u32[]{:S(2)}, u32[]{:S(2)}) %collective-permute-start.1) | collective-permute-done | bytes 262176 | tf_op jit(solution)/shard_map/ppermute | solution.py:179
  143.6 3.9 %collective-permute-done.3 = f32[1024,64]{0,1:T(8,128)S(1)} collective-permute-done((f32[1024,64]{0,1:T(8,128)S(1)}, f32[1024,64]{0,1:T(8,128)S(1)}, u32[]{:S(2)}, u32[]{:S(2)}) %collective-permute-start.3) | collective-permute-done | bytes 262176 | tf_op jit(solution)/shard_map/ppermute | solution.py:179
  (87 shorter events, 8.8 us)
Async XLA Ops:
  37.2 6.6 %copy-start.4 = (s32[1024,1]{0,1:T(1,128)S(1)}, s32[1024,1]{0,1:T(1,128)}, u32[]{:S(2)}) copy-start(s32[1024,1]{0,1:T(1,128)} %param.9) | copy-start | bytes 12292
  43.8 6.0 %copy-start.1 = (f32[1024,20,32]{0,2,1:T(8,128)}, f32[1024,20,32]{0,2,1:T(8,128)S(1)}, u32[]{:S(2)}) copy-start(f32[1024,20,32]{0,2,1:T(8,128)S(1)} %copy.28) | copy-start | bytes 7864324
  50.9 4.8 %collective-permute-start = (f32[32,33,320]{2,0,1:T(8,128)S(1)}, f32[32,33,320]{2,0,1:T(8,128)S(1)}, u32[]{:S(2)}, u32[]{:S(2)}) collective-permute-start(f32[32,33,320]{2,0,1:T(8,128)S(1)} %copy.30), channel_id=1, source_target_pairs={{0,4},{4,0},{8,12},{12,8},{16,20},{20,16},{24,28},{28,24},{32,36},... | collective-permute-start | bytes 4055048 | tf_op jit(solution)/shard_map/ppermute | solution.py:154
  91.1 1.3 copy-start.5
  91.1 1.5 %copy-start.3 = (f32[32,8]{0,1:T(8,128)S(1)}, f32[32,8]{0,1:T(8,128)}, u32[]{:S(2)}) copy-start(f32[32,8]{0,1:T(8,128)} %param.11) | copy-start | bytes 3076
  96.1 21.2 %all-to-all-start.1 = ((f32[32,32,240]{2,1,0:T(8,128)}), f32[32,32,240]{2,1,0:T(8,128)S(1)}, u32[]{:S(2)}, u32[]{:S(2)}) async-start(f32[32,32,240]{2,1,0:T(8,128)} %broadcast_in_dim.62), calls=%async_computation.1 | async-start | bytes 2097152 | tf_op jit(solution)/shard_map/all_to_all | solution.py:163
  120.7 1.7 %copy-start.2 = (f32[1024,640]{1,0:T(8,128)S(1)}, f32[1024,640]{1,0:T(8,128)}, u32[]{:S(2)}) copy-start(f32[1024,640]{1,0:T(8,128)} %copy.37) | copy-start | bytes 7864324
  124.3 3.0 %copy-start = (f32[1024,640]{1,0:T(8,128)}, f32[1024,640]{1,0:T(8,128)S(1)}, u32[]{:S(2)}) copy-start(f32[1024,640]{1,0:T(8,128)S(1)} %multiply_multiply_fusion) | copy-start | bytes 7864324
  128.9 14.7 %collective-permute-start.1 = (f32[1024,64]{0,1:T(8,128)S(1)}, f32[1024,64]{0,1:T(8,128)S(1)}, u32[]{:S(2)}, u32[]{:S(2)}) collective-permute-start(f32[1024,64]{0,1:T(8,128)S(1)} %pad_maximum_fusion), channel_id=1, source_target_pairs={{0,3},{1,0},{2,1},{3,2},{4,7},{5,4},{6,5},{7,6},{8,11},{9,8},{10,9... | collective-permute-start | bytes 786440 | tf_op jit(solution)/shard_map/ppermute | solution.py:179
  132.8 10.9 %collective-permute-start.2 = (f32[1024,64]{0,1:T(8,128)S(1)}, f32[1024,64]{0,1:T(8,128)S(1)}, u32[]{:S(2)}, u32[]{:S(2)}) collective-permute-start(f32[1024,64]{0,1:T(8,128)S(1)} %pad_maximum_fusion), channel_id=1, source_target_pairs={{0,2},{1,3},{2,0},{3,1},{4,6},{5,7},{6,4},{7,5},{8,10},{9,11},{10,... | collective-permute-start | bytes 786440 | tf_op jit(solution)/shard_map/ppermute | solution.py:179
  132.8 14.8 %collective-permute-start.3 = (f32[1024,64]{0,1:T(8,128)S(1)}, f32[1024,64]{0,1:T(8,128)S(1)}, u32[]{:S(2)}, u32[]{:S(2)}) collective-permute-start(f32[1024,64]{0,1:T(8,128)S(1)} %pad_maximum_fusion), channel_id=1, source_target_pairs={{0,1},{1,2},{2,3},{3,0},{4,5},{5,6},{6,7},{7,4},{8,9},{9,10},{10,1... | collective-permute-start | bytes 786440 | tf_op jit(solution)/shard_map/ppermute | solution.py:179

commit v6 on v5

--- a/solution.py
+++ b/solution.py
@@ -15,10 +15,10 @@
 USE_KERNEL = True
 
 
-def tab_kernel(offs_ref, seg_ref, w_ref, out_ref):
+def tab_kernel(offs_ref, seg_ref, w_ref, out_ref, acc_ref):
     steps = seg_ref.shape[0]
     width = SPAN * CELLS
-    out_ref[...] = jnp.zeros_like(out_ref)
+    acc_ref[...] = jnp.zeros_like(acc_ref)
     rows = lax.broadcasted_iota(jnp.int32, (width, BLOCK), 0)
 
     def body(b, carry):
@@ -30,10 +30,19 @@
             w, hot, (((1,), (1,)), ((), ())), preferred_element_type=jnp.float32
         )
         off = pl.multiple_of(offs_ref[b], 128)
-        out_ref[:, pl.ds(off, width)] += part
+        acc_ref[:, pl.ds(off, width)] += part
         return carry
 
     lax.fori_loop(0, steps, body, 0, unroll=8)
+
+    def flip(c, carry):
+        block = acc_ref[:, pl.ds(pl.multiple_of(c * width, width), width)]
+        out_ref[pl.ds(pl.multiple_of(c * SPAN, SPAN), SPAN), :] = pltpu.einshape(
+            "r(gk)->g(rk)", block, g=SPAN, k=CELLS
+        )
+        return carry
+
+    lax.fori_loop(0, out_ref.shape[0] // SPAN, flip, 0, unroll=4)
 
 
 def tab_plain(offs, seg, weights, out_width):
@@ -70,24 +79,23 @@
     offs = (base * CELLS).astype(jnp.int32)
     out_width = groups * CELLS
     if USE_KERNEL:
-        out = pl.pallas_call(
+        return pl.pallas_call(
             tab_kernel,
-            out_shape=jax.ShapeDtypeStruct((reps, out_width), jnp.float32),
+            out_shape=jax.ShapeDtypeStruct((groups, reps * CELLS), jnp.float32),
             in_specs=[
                 pl.BlockSpec(memory_space=pltpu.SMEM),
                 pl.BlockSpec(memory_space=pltpu.VMEM),
                 pl.BlockSpec(memory_space=pltpu.VMEM),
             ],
             out_specs=pl.BlockSpec(memory_space=pltpu.VMEM),
+            scratch_shapes=[pltpu.VMEM((reps, out_width), jnp.float32)],
             cost_estimate=pl.CostEstimate(
                 flops=2 * reps * records * SPAN * CELLS,
                 bytes_accessed=weights.size * 2 + seg.size * 4 + reps * out_width * 4,
                 transcendentals=0,
             ),
         )(offs, seg, weights)
-    else:
-        out = tab_plain(offs, seg, weights, out_width)
-    out = out.reshape(reps, groups, CELLS)
+    out = tab_plain(offs, seg, weights, out_width).reshape(reps, groups, CELLS)
     return out.transpose(1, 0, 2).reshape(groups, reps * CELLS)
 
 

time: 149 us -> 149 us (level)
  local copies, waits for them, and re-layouts: 24.7 us -> 10.4 us
  Pallas kernels: 22.7 us -> 32 us
  waiting for transfers between devices: 31 us -> 34.2 us
  matrix products: 13 us -> 15 us
    pallas_call x1, Pallas kernels: 22.7 us -> 32 us  [tabulate(): pl.pallas_call(tab_kernel, out_shape=jax.ShapeDtypeStruct((groups, reps *...]
    reshape x2 -> x1, local copies, waits for them, and re-layouts: 9.92 us -> 1.52 us  [local(): partial.reshape(owners, county_here, width)]
    transpose x1 -> x0, local copies, waits for them, and re-layouts: 6.57 us -> none  [tabulate(): return out.transpose(1, 0, 2).reshape(groups, reps * CELLS)]
    all_to_all x1, waiting for transfers between devices: 13.8 us -> 17.1 us  [local(): lax.all_to_all(sent.reshape(owners * county_here, factors.shape[1]), 'row...]
    dot_general x6, matrix products: 13 us -> 15 us  [exact_dot(): jnp.dot(left, right, precision=lax.Precision.HIGHEST, preferred_element_t...]
  transfers between devices with their start and end apart: 5 -> 5, of which waited for: 4 -> 4; matrix products, arithmetic and copies ran while one was open for 2% -> 0% of each run, Pallas kernels for 0% -> 0%
where the time goes in v6:
time: 149 us
  waiting for transfers between devices  34.2 us (23%)
  blocking collectives  34.2 us (23%)
  Pallas kernels  32 us (21%)
  matrix products  15 us (10%)
  other arithmetic  11.5 us (8%)
  local copies, waits for them, and re-layouts  10.4 us (7%)
  starting transfers between devices  10.2 us (7%)
    all_to_all x1, blocking collectives, local(): lax.all_to_all(keep.reshape(owners * (county_here + 1), half), 'rows', 0,...  34.2 us
    pallas_call x1, Pallas kernels, tabulate(): pl.pallas_call(tab_kernel, out_shape=jax.ShapeDtypeStruct((groups, reps *...  32 us
    all_to_all x1, waiting for transfers between devices, local(): lax.all_to_all(sent.reshape(owners * county_here, factors.shape[1]), 'row...  17.1 us
    dot_general x6, matrix products, exact_dot(): jnp.dot(left, right, precision=lax.Precision.HIGHEST, preferred_element_t...  15 us
    ppermute x3, waiting for transfers between devices, local(): lax.ppermute(stats, 'rep', [(i, (i + s) % shards) for i in range(shards)])  14.1 us
    ppermute x3, starting transfers between devices, local(): lax.ppermute(stats, 'rep', [(i, (i + s) % shards) for i in range(shards)])  4.53 us
    all_to_all x1, starting transfers between devices, local(): lax.all_to_all(sent.reshape(owners * county_here, factors.shape[1]), 'row...  4.02 us
    gather x1, local copies, waits for them, and re-layouts, local(): mine = jnp.take(factors, county, axis=0)  3.46 us
  transfers between devices with their start and end apart: 5, of which 4 were waited for; matrix products, arithmetic and copies ran while one was open for 0% of the time, Pallas kernels for 0%

profile of v6, /device:TPU:1, one launch (start us, length us, event | category | flops | bytes accessed | tf_op | source)
XLA Modules:
  0.0 148.6 jit_solution(3376120201923838605)
XLA Ops:
  0.6 1.0 reduce-window.9
  2.3 1.2 convert_reduce_fusion
  3.5 2.7 %select_reduce_fusion.6 = (s32[512]{0:T(512)S(1)}, s32[512]{0:T(512)S(1)}, s32[512]{0:T(512)S(1)}, s32[512]{0:T(512)S(1)}, s32[512]{0:T(512)S(1)}, /*index=5*/s32[512]{0:T(512)S(1)}, s32[512]{0:T(512)S(1)}) fusion(s32[512]{0:T(512)S(1)} %get-tuple-element.12, s32[1024]{0:T(1024)S(1)} %add_bitcast_fusion, s32[512]{0:T(512)S(1)} %get-tuple-element.45, ...), kind=kLoop, calls=%fused_computation.23 | loop fusion | flops 11006464 | bytes 32768 | tf_op jit(solution)/shard_map/reduce_sum | solution.py:75
  6.8 2.3 %bitcast_add_fusion.seg_ref = s32[512,128]{1,0:T(8,128)} fusion(s32[65536]{0:T(1024)} %param.7, s32[512]{0:T(512)S(1)} %get-tuple-element.39, s32[512]{0:T(512)S(1)} %get-tuple-element.34, s32[512]{0:T(512)S(1)} %get-tuple-element.37, s32[512]{0:T(512)S(1)} %get-tuple-element.38, s32[512]{0:T(512)S(1)} %get-tuple-element.35, s32[512]{0:T(512)S(1)} %get-tuple-element.36, ...), kind=kLoop, calls=%fused_computation.40 | loop fusion | flops 1507328 | bytes 540672 | tf_op jit(solution)/shard_map/add | solution.py:78
  9.1 32.0 %shard_map.77 = f32[1024,640]{1,0:T(8,128)} custom-call(s32[512]{0:T(512)} %get-tuple-element.40.offs_ref, s32[512,128]{1,0:T(8,128)} %bitcast_add_fusion.seg_ref, bf16[20,65536]{1,0:T(8,128)(2,1)} %w_ref.1), custom_call_target="tpu_custom_call" | custom-call | flops 671088640 | bytes 5505024 | tf_op jit(solution)/shard_map/pallas_call | solution.py:82
  41.1 7.3 %fusion = f32[1024,640]{1,0:T(8,128)S(1)} fusion(f32[1024,640]{1,0:T(8,128)} %shard_map.77, s32[1024]{0:T(1024)S(1)} %bitcast.36), kind=kOutput, calls=%fused_computation.3 | convolution fusion | flops 8054112256 | bytes 5246976 | tf_op jit(solution)/shard_map/dot_general | solution.py:103
  48.4 1.5 %copy.28 = f32[32,32,640]{2,0,1:T(8,128)S(1)} copy(f32[32,32,640]{2,1,0:T(8,128)S(1)} %bitcast.30) | data formatting | bytes 5242880 | tf_op jit(solution)/shard_map/reshape | solution.py:156
  50.7 1.6 %collective-permute-start = (f32[32,33,320]{2,0,1:T(8,128)S(1)}, f32[32,33,320]{2,0,1:T(8,128)S(1)}, u32[]{:S(2)}, u32[]{:S(2)}) collective-permute-start(f32[32,33,320]{2,0,1:T(8,128)S(1)} %slice_select_fusion), channel_id=1, source_target_pairs={{0,4},{4,0},{8,12},{12,8},{16,20},{20,16},{24,28},{28,24},{32,36},... | collective-permute-start | bytes 4055048 | tf_op jit(solution)/shard_map/ppermute | solution.py:162
  52.4 3.1 %collective-permute-done = f32[32,33,320]{2,0,1:T(8,128)S(1)} collective-permute-done((f32[32,33,320]{2,0,1:T(8,128)S(1)}, f32[32,33,320]{2,0,1:T(8,128)S(1)}, u32[]{:S(2)}, u32[]{:S(2)}) %collective-permute-start) | collective-permute-done | bytes 1351712 | tf_op jit(solution)/shard_map/ppermute | solution.py:162
  56.0 1.0 copy.29
  56.9 34.2 %all_to_all.15 = f32[32,33,320]{2,1,0:T(8,128)S(1)} all-to-all(f32[32,33,320]{2,1,0:T(8,128)S(1)} %copy.29), channel_id=1, replica_groups=mesh['rows'=32,'rep'=4] {'rows'}, dimensions={0} | all-to-all | bytes 2703360 | tf_op jit(solution)/shard_map/all_to_all | solution.py:163
  95.1 1.1 broadcast_in_dim.62
  96.2 4.0 %all-to-all-start.1 = ((f32[32,32,240]{2,1,0:T(8,128)}), f32[32,32,240]{2,1,0:T(8,128)S(1)}, u32[]{:S(2)}, u32[]{:S(2)}) async-start(f32[32,32,240]{2,1,0:T(8,128)} %broadcast_in_dim.62), calls=%async_computation.1 | async-start | bytes 2097152 | tf_op jit(solution)/shard_map/all_to_all | solution.py:171
  100.3 17.1 %all-to-all-done.1 = f32[32,32,240]{2,1,0:T(8,128)S(1)} async-done(((f32[32,32,240]{2,1,0:T(8,128)}), f32[32,32,240]{2,1,0:T(8,128)S(1)}, u32[]{:S(2)}, u32[]{:S(2)}) %all-to-all-start.1) | async-done | bytes 983072 | tf_op jit(solution)/shard_map/all_to_all | solution.py:171
  117.4 3.5 %gather_fusion = f32[1024,240]{1,0:T(8,128)S(1)} fusion(f32[1024,240]{1,0:T(8,128)S(1)} %bitcast.28, s32[1024]{0:T(1024)S(1)} %broadcast_clamp_fusion), kind=kCustom, calls=%fused_computation | custom fusion | bytes 1970176 | tf_op jit(solution)/shard_map/jit(_take)/gather | solution.py:174
  121.1 1.3 fusion.6
  122.6 1.8 %multiply_multiply_fusion = f32[1024,640]{1,0:T(8,128)S(1)} fusion(f32[1024,640]{1,0:T(8,128)S(1)} %copy-done.1, f32[1024,640]{1,0:T(8,128)S(1)} %fusion.6, f32[1024,240]{1,0:T(8,128)S(1)} %broadcast_select_fusion, s32[640]{0:T(1024)S(1)} %add_select_fusion, s32[640]{0:T(1024)S(1)} %get-tuple-element.47, s32[160]{0:T(256)S(1)} %get-tuple-element.50, ...), kind=kOutput, calls=%fused_computation.9 | convolution fusion | flops 1259909120 | bytes 8853760 | tf_op jit(solution)/shard_map/dot_general | solution.py:103
  124.4 1.5 fusion.12
  125.8 1.5 %fusion.11 = f32[1024,640]{1,0:T(8,128)S(1)} fusion(s32[640]{0:T(1024)S(1)} %fusion.41, f32[1024,32]{0,1:T(8,128)S(1)} %fusion.12), kind=kOutput, calls=%fused_computation.37 | convolution fusion | flops 251711488 | bytes 2755072 | tf_op jit(solution)/shard_map/dot_general | solution.py:103
  127.4 1.6 %fusion.1 = f32[1024,32]{0,1:T(8,128)S(1)} fusion(f32[1024,640]{1,0:T(8,128)S(1)} %multiply_multiply_fusion, f32[1024,640]{1,0:T(8,128)S(1)} %fusion.11, s32[640]{0:T(1024)S(1)} %fusion.41), kind=kOutput, calls=%fused_computation.6 | convolution fusion | flops 252989440 | bytes 5376512 | tf_op jit(solution)/shard_map/dot_general | solution.py:103
  129.0 3.8 %collective-permute-start.1 = (f32[1024,64]{0,1:T(8,128)S(1)}, f32[1024,64]{0,1:T(8,128)S(1)}, u32[]{:S(2)}, u32[]{:S(2)}) collective-permute-start(f32[1024,64]{0,1:T(8,128)S(1)} %pad_maximum_fusion), channel_id=1, source_target_pairs={{0,3},{1,0},{2,1},{3,2},{4,7},{5,4},{6,5},{7,6},{8,11},{9,8},{10,9... | collective-permute-start | bytes 786440 | tf_op jit(solution)/shard_map/ppermute | solution.py:187
  133.6 10.2 %collective-permute-done.1 = f32[1024,64]{0,1:T(8,128)S(1)} collective-permute-done((f32[1024,64]{0,1:T(8,128)S(1)}, f32[1024,64]{0,1:T(8,128)S(1)}, u32[]{:S(2)}, u32[]{:S(2)}) %collective-permute-start.1) | collective-permute-done | bytes 262176 | tf_op jit(solution)/shard_map/ppermute | solution.py:187
  143.8 3.9 %collective-permute-done.3 = f32[1024,64]{0,1:T(8,128)S(1)} collective-permute-done((f32[1024,64]{0,1:T(8,128)S(1)}, f32[1024,64]{0,1:T(8,128)S(1)}, u32[]{:S(2)}, u32[]{:S(2)}) %collective-permute-start.3) | collective-permute-done | bytes 262176 | tf_op jit(solution)/shard_map/ppermute | solution.py:187
  147.8 0.8 fusion.31
  (82 shorter events, 7.6 us)
Async XLA Ops:
  9.1 32.0 %copy-start.3 = (s32[1024,1]{0,1:T(1,128)S(1)}, s32[1024,1]{0,1:T(1,128)}, u32[]{:S(2)}) copy-start(s32[1024,1]{0,1:T(1,128)} %param.9) | copy-start | bytes 12292
  50.7 4.7 %collective-permute-start = (f32[32,33,320]{2,0,1:T(8,128)S(1)}, f32[32,33,320]{2,0,1:T(8,128)S(1)}, u32[]{:S(2)}, u32[]{:S(2)}) collective-permute-start(f32[32,33,320]{2,0,1:T(8,128)S(1)} %slice_select_fusion), channel_id=1, source_target_pairs={{0,4},{4,0},{8,12},{12,8},{16,20},{20,16},{24,28},{28,24},{32,36},... | collective-permute-start | bytes 4055048 | tf_op jit(solution)/shard_map/ppermute | solution.py:162
  91.2 1.3 copy-start.4
  91.2 1.5 %copy-start.2 = (f32[32,8]{0,1:T(8,128)S(1)}, f32[32,8]{0,1:T(8,128)}, u32[]{:S(2)}) copy-start(f32[32,8]{0,1:T(8,128)} %param.11) | copy-start | bytes 3076
  96.2 21.2 %all-to-all-start.1 = ((f32[32,32,240]{2,1,0:T(8,128)}), f32[32,32,240]{2,1,0:T(8,128)S(1)}, u32[]{:S(2)}, u32[]{:S(2)}) async-start(f32[32,32,240]{2,1,0:T(8,128)} %broadcast_in_dim.62), calls=%async_computation.1 | async-start | bytes 2097152 | tf_op jit(solution)/shard_map/all_to_all | solution.py:171
  120.8 1.7 %copy-start.1 = (f32[1024,640]{1,0:T(8,128)S(1)}, f32[1024,640]{1,0:T(8,128)}, u32[]{:S(2)}) copy-start(f32[1024,640]{1,0:T(8,128)} %shard_map.77) | copy-start | bytes 7864324
  124.3 3.0 %copy-start = (f32[1024,640]{1,0:T(8,128)}, f32[1024,640]{1,0:T(8,128)S(1)}, u32[]{:S(2)}) copy-start(f32[1024,640]{1,0:T(8,128)S(1)} %multiply_multiply_fusion) | copy-start | bytes 7864324
  129.0 14.7 %collective-permute-start.1 = (f32[1024,64]{0,1:T(8,128)S(1)}, f32[1024,64]{0,1:T(8,128)S(1)}, u32[]{:S(2)}, u32[]{:S(2)}) collective-permute-start(f32[1024,64]{0,1:T(8,128)S(1)} %pad_maximum_fusion), channel_id=1, source_target_pairs={{0,3},{1,0},{2,1},{3,2},{4,7},{5,4},{6,5},{7,6},{8,11},{9,8},{10,9... | collective-permute-start | bytes 786440 | tf_op jit(solution)/shard_map/ppermute | solution.py:187
  132.9 10.9 %collective-permute-start.2 = (f32[1024,64]{0,1:T(8,128)S(1)}, f32[1024,64]{0,1:T(8,128)S(1)}, u32[]{:S(2)}, u32[]{:S(2)}) collective-permute-start(f32[1024,64]{0,1:T(8,128)S(1)} %pad_maximum_fusion), channel_id=1, source_target_pairs={{0,2},{1,3},{2,0},{3,1},{4,6},{5,7},{6,4},{7,5},{8,10},{9,11},{10,... | collective-permute-start | bytes 786440 | tf_op jit(solution)/shard_map/ppermute | solution.py:187
  132.9 14.8 %collective-permute-start.3 = (f32[1024,64]{0,1:T(8,128)S(1)}, f32[1024,64]{0,1:T(8,128)S(1)}, u32[]{:S(2)}, u32[]{:S(2)}) collective-permute-start(f32[1024,64]{0,1:T(8,128)S(1)} %pad_maximum_fusion), channel_id=1, source_target_pairs={{0,1},{1,2},{2,3},{3,0},{4,5},{5,6},{6,7},{7,4},{8,9},{9,10},{10,1... | collective-permute-start | bytes 786440 | tf_op jit(solution)/shard_map/ppermute | solution.py:187

commit v7 on v5

--- a/solution.py
+++ b/solution.py
@@ -10,8 +10,8 @@
 CELLS = 32
 LOW = 32
 ITERS = 4
-BLOCK = 128
-SPAN = 8
+BLOCK = 256
+SPAN = 12
 USE_KERNEL = True
 
 
@@ -174,17 +174,11 @@
     part_m2 = exact_dot(jnp.square(gap), cell_sum)
     stats = jnp.concatenate([part_sum, part_m2], axis=1)
     shards = lax.axis_size("rep")
-    me = lax.axis_index("rep")
-    received = [stats] + [
-        lax.ppermute(stats, "rep", [(i, (i + s) % shards) for i in range(shards)])
-        for s in range(1, shards)
-    ]
-    by_source = []
-    for source in range(shards):
-        value = jnp.zeros_like(stats)
-        for s in range(shards):
-            value = jnp.where((me - s) % shards == source, received[s], value)
-        by_source.append(value)
+    sent = jnp.broadcast_to(stats[None], (shards,) + stats.shape)
+    received = lax.all_to_all(
+        sent.reshape(shards * groups, stats.shape[1]), "rep", 0, 0, tiled=True
+    ).reshape(shards, groups, stats.shape[1])
+    by_source = [received[source] for source in range(shards)]
     total_reps = reps * shards
     total = by_source[0][:, :CELLS]
     for source in range(1, shards):

time: 149 us -> 149 us (level)
  blocking collectives: 34.2 us -> 53.3 us
  waiting for transfers between devices: 31 us -> 17 us
  starting transfers between devices: 10.2 us -> 5.66 us
  other arithmetic: 11.5 us -> 9.42 us
    all_to_all x0 -> x1, blocking collectives: none -> 19 us  [local(): lax.all_to_all(sent.reshape(shards * groups, stats.shape[1]), 'rep', 0, 0...]
    ppermute x3 -> x0, waiting for transfers between devices: 14.1 us -> none  [local(): lax.ppermute(stats, 'rep', [(i, (i + s) % shards) for i in range(shards)])]
    ppermute x3 -> x0, starting transfers between devices: 4.53 us -> none  [local(): lax.ppermute(stats, 'rep', [(i, (i + s) % shards) for i in range(shards)])]
  transfers between devices with their start and end apart: 5 -> 2, of which waited for: 4 -> 2; matrix products, arithmetic and copies ran while one was open for 2% -> 2% of each run, Pallas kernels for 0% -> 0%
where the time goes in v7:
time: 149 us; the launch traced here: 148 us
  blocking collectives  53.3 us (36%)
  local copies, waits for them, and re-layouts  26 us (17%)
  Pallas kernels  22 us (15%)
  waiting for transfers between devices  17 us (11%)
  matrix products  13 us (9%)
  other arithmetic  9.42 us (6%)
  starting transfers between devices  5.66 us (4%)
    all_to_all x1, blocking collectives, local(): lax.all_to_all(keep.reshape(owners * (county_here + 1), half), 'rows', 0,...  34.3 us
    pallas_call x1, Pallas kernels, tabulate(): pl.pallas_call(tab_kernel, out_shape=jax.ShapeDtypeStruct((reps, out_widt...  22 us
    all_to_all x1, blocking collectives, local(): lax.all_to_all(sent.reshape(shards * groups, stats.shape[1]), 'rep', 0, 0...  19 us
    all_to_all x1, waiting for transfers between devices, local(): lax.all_to_all(sent.reshape(owners * county_here, factors.shape[1]), 'row...  13.8 us
    dot_general x6, matrix products, exact_dot(): jnp.dot(left, right, precision=lax.Precision.HIGHEST, preferred_element_t...  13 us
    reshape x1, local copies, waits for them, and re-layouts, tabulate(): out = out.reshape(reps, groups, CELLS)  6.69 us
    transpose x1, local copies, waits for them, and re-layouts, tabulate(): return out.transpose(1, 0, 2).reshape(groups, reps * CELLS)  6.57 us
    all_to_all x1, starting transfers between devices, local(): lax.all_to_all(sent.reshape(owners * county_here, factors.shape[1]), 'row...  4.02 us
  transfers between devices with their start and end apart: 2, of which 2 were waited for; matrix products, arithmetic and copies ran while one was open for 2% of the time, Pallas kernels for 0%

profile of v7, /device:TPU:1, one launch (start us, length us, event | category | flops | bytes accessed | tf_op | source)
XLA Modules:
  0.0 147.5 jit_solution(11835214545899047837)
XLA Ops:
  0.7 1.0 reduce-window.9
  2.2 1.0 reshape.505
  3.2 2.0 %select_reduce_fusion.10 = (s32[256]{0:T(256)S(1)}, s32[256]{0:T(256)S(1)}, s32[256]{0:T(256)S(1)}, s32[256]{0:T(256)S(1)}, s32[256]{0:T(256)S(1)}, /*index=5*/s...) fusion(s32[256]{0:T(256)S(1)} %get-tuple-element.16, ...), kind=kLoop, calls=%fused_computation.36 | loop fusion | flops 8647936 | bytes 26624 | tf_op jit(solution)/shard_map/reduce_sum | solution.py:66
  5.8 1.2 multiply_add_fusion.seg_ref
  7.0 22.0 %shard_map.77 = f32[20,32768]{1,0:T(8,128)} custom-call(s32[256]{0:T(256)} %get-tuple-element.48.offs_ref, s32[256,256]{1,0:T(8,128)} %multiply_add_fusion.seg_ref, bf16[20,65536]{1,0:T(8,128)(2,1)} %w_ref.1), custom_call_target="tpu_custom_call" | custom-call | flops 1006632960 | bytes 5505024 | tf_op jit(solution)/shard_map/pallas_call | solution.py:73
  29.0 6.7 %reshape.506 = f32[20,1024,32]{2,1,0:T(8,128)} reshape(f32[20,32768]{1,0:T(8,128)} %shard_map.77) | data formatting | bytes 5242880 | tf_op jit(solution)/shard_map/reshape | solution.py:90
  35.6 6.6 %copy.30 = f32[1024,20,32]{0,2,1:T(8,128)S(1)} copy(f32[1024,20,32]{2,0,1:T(8,128)} %bitcast.38) | data formatting | bytes 5242880 | tf_op jit(solution)/shard_map/transpose | solution.py:91
  42.9 5.4 %fusion = f32[32,32,640]{2,1,0:T(8,128)S(1)} fusion(f32[1024,640,1]{0,1,2:T(8,128)S(1)} %bitcast.39, s32[32,32]{1,0:T(8,128)S(1)} %multiply_add_fusion.1, s32[1024]{0:T(1024)S(1)} %bitcast.49), kind=kOutput, calls=%fused_computation.3 | convolution fusion | flops 8054112256 | bytes 5251072 | tf_op jit(solution)/shard_map/dot_general | solution.py:95
  49.4 1.6 %collective-permute-start = (f32[32,33,320]{2,0,1:T(8,128)S(1)}, f32[32,33,320]{2,0,1:T(8,128)S(1)}, u32[]{:S(2)}, u32[]{:S(2)}) collective-permute-start(f32[32,33,320]{2,0,1:T(8,128)S(1)} %copy.32), channel_id=1, source_target_pairs={{0,4},{4,0},{8,12},{12,8},{16,20},{20,16},{24,28},{28,24},{32,36},... | collective-permute-start | bytes 4055048 | tf_op jit(solution)/shard_map/ppermute | solution.py:154
  51.0 3.1 %collective-permute-done = f32[32,33,320]{2,0,1:T(8,128)S(1)} collective-permute-done((f32[32,33,320]{2,0,1:T(8,128)S(1)}, f32[32,33,320]{2,0,1:T(8,128)S(1)}, u32[]{:S(2)}, u32[]{:S(2)}) %collective-permute-start) | collective-permute-done | bytes 1351712 | tf_op jit(solution)/shard_map/ppermute | solution.py:154
  54.1 1.1 copy_add_fusion
  55.2 34.3 %all_to_all.24 = f32[32,33,320]{2,1,0:T(8,128)S(1)} all-to-all(f32[32,33,320]{2,1,0:T(8,128)S(1)} %copy_add_fusion), channel_id=1, replica_groups=mesh['rows'=32,'rep'=4] {'rows'}, dimensions={0} | all-to-all | bytes 2703360 | tf_op jit(solution)/shard_map/all_to_all | solution.py:155
  93.4 1.1 broadcast_in_dim.87
  94.5 4.0 %all-to-all-start.1 = ((f32[32,32,240]{2,1,0:T(8,128)}), f32[32,32,240]{2,1,0:T(8,128)S(1)}, u32[]{:S(2)}, u32[]{:S(2)}) async-start(f32[32,32,240]{2,1,0:T(8,128)} %broadcast_in_dim.87), calls=%async_computation.1 | async-start | bytes 2097152 | tf_op jit(solution)/shard_map/all_to_all | solution.py:163
  98.5 3.2 %copy.39 = f32[1024,640]{1,0:T(8,128)} copy(f32[1024,640]{0,1:T(8,128)} %bitcast.40) | data formatting | bytes 5242880 | tf_op jit(solution)/shard_map/reshape | solution.py:91
  101.8 13.8 %all-to-all-done.1 = f32[32,32,240]{2,1,0:T(8,128)S(1)} async-done(((f32[32,32,240]{2,1,0:T(8,128)}), f32[32,32,240]{2,1,0:T(8,128)S(1)}, u32[]{:S(2)}, u32[]{:S(2)}) %all-to-all-start.1) | async-done | bytes 983072 | tf_op jit(solution)/shard_map/all_to_all | solution.py:163
  115.7 3.5 %gather_fusion = f32[1024,240]{1,0:T(8,128)S(1)} fusion(f32[1024,240]{1,0:T(8,128)S(1)} %bitcast.37, s32[1024]{0:T(1024)S(1)} %broadcast_clamp_fusion), kind=kCustom, calls=%fused_computation | custom fusion | bytes 1970176 | tf_op jit(solution)/shard_map/jit(_take)/gather | solution.py:166
  119.4 1.3 fusion.8
  120.9 1.8 %multiply_multiply_fusion = f32[1024,640]{1,0:T(8,128)S(1)} fusion(f32[1024,640]{1,0:T(8,128)S(1)} %copy-done.2, f32[1024,640]{1,0:T(8,128)S(1)} %fusion.8, f32[1024,240]{1,0:T(8,128)S(1)} %broadcast_select_fusion, s32[640]{0:T(1024)S(1)} %add_select_fusion, s32[640]{0:T(1024)S(1)} %get-tuple-element.59, s32[160]{0:T(256)S(1)} %get-tuple-element.62, ...), kind=kOutput, calls=%fused_computation.10 | convolution fusion | flops 1259909120 | bytes 8853760 | tf_op jit(solution)/shard_map/dot_general | solution.py:95
  122.7 1.5 fusion.14
  124.2 1.5 %fusion.13 = f32[1024,640]{1,0:T(8,128)S(1)} fusion(s32[640]{0:T(1024)S(1)} %fusion.47, f32[1024,32]{0,1:T(8,128)S(1)} %fusion.14), kind=kOutput, calls=%fused_computation.47 | convolution fusion | flops 251711488 | bytes 2755072 | tf_op jit(solution)/shard_map/dot_general | solution.py:95
  125.7 1.6 %fusion.2 = f32[1024,32]{0,1:T(8,128)S(1)} fusion(f32[1024,640]{1,0:T(8,128)S(1)} %multiply_multiply_fusion, f32[1024,640]{1,0:T(8,128)S(1)} %fusion.13, s32[640]{0:T(1024)S(1)} %fusion.47), kind=kOutput, calls=%fused_computation.7 | convolution fusion | flops 252989440 | bytes 5376512 | tf_op jit(solution)/shard_map/dot_general | solution.py:95
  127.5 19.0 %all_to_all.25 = f32[4,1024,64]{1,2,0:T(8,128)S(1)} all-to-all(f32[4,1024,64]{1,2,0:T(8,128)S(1)} %broadcast_in_dim.89), channel_id=1, replica_groups=mesh['rows'=32,'rep'=4] {'rep'}, dimensions={0} | all-to-all | bytes 2097152 | tf_op jit(solution)/shard_map/all_to_all | solution.py:178
  146.7 0.8 fusion.37
  (84 shorter events, 7.3 us)
Async XLA Ops:
  35.6 6.6 %copy-start.4 = (s32[1024,1]{0,1:T(1,128)S(1)}, s32[1024,1]{0,1:T(1,128)}, u32[]{:S(2)}) copy-start(s32[1024,1]{0,1:T(1,128)} %param.9) | copy-start | bytes 12292
  42.2 6.0 %copy-start.1 = (f32[1024,20,32]{0,2,1:T(8,128)}, f32[1024,20,32]{0,2,1:T(8,128)S(1)}, u32[]{:S(2)}) copy-start(f32[1024,20,32]{0,2,1:T(8,128)S(1)} %copy.30) | copy-start | bytes 7864324
  49.4 4.8 %collective-permute-start = (f32[32,33,320]{2,0,1:T(8,128)S(1)}, f32[32,33,320]{2,0,1:T(8,128)S(1)}, u32[]{:S(2)}, u32[]{:S(2)}) collective-permute-start(f32[32,33,320]{2,0,1:T(8,128)S(1)} %copy.32), channel_id=1, source_target_pairs={{0,4},{4,0},{8,12},{12,8},{16,20},{20,16},{24,28},{28,24},{32,36},... | collective-permute-start | bytes 4055048 | tf_op jit(solution)/shard_map/ppermute | solution.py:154
  89.5 1.3 copy-start.5
  89.5 1.5 %copy-start.3 = (f32[32,8]{0,1:T(8,128)S(1)}, f32[32,8]{0,1:T(8,128)}, u32[]{:S(2)}) copy-start(f32[32,8]{0,1:T(8,128)} %param.11) | copy-start | bytes 3076
  94.5 21.2 %all-to-all-start.1 = ((f32[32,32,240]{2,1,0:T(8,128)}), f32[32,32,240]{2,1,0:T(8,128)S(1)}, u32[]{:S(2)}, u32[]{:S(2)}) async-start(f32[32,32,240]{2,1,0:T(8,128)} %broadcast_in_dim.87), calls=%async_computation.1 | async-start | bytes 2097152 | tf_op jit(solution)/shard_map/all_to_all | solution.py:163
  119.2 1.7 %copy-start.2 = (f32[1024,640]{1,0:T(8,128)S(1)}, f32[1024,640]{1,0:T(8,128)}, u32[]{:S(2)}) copy-start(f32[1024,640]{1,0:T(8,128)} %copy.39) | copy-start | bytes 7864324
  122.7 3.0 %copy-start = (f32[1024,640]{1,0:T(8,128)}, f32[1024,640]{1,0:T(8,128)S(1)}, u32[]{:S(2)}) copy-start(f32[1024,640]{1,0:T(8,128)S(1)} %multiply_multiply_fusion) | copy-start | bytes 7864324

commit v8 on v7

--- a/solution.py
+++ b/solution.py
@@ -33,7 +33,7 @@
         out_ref[:, pl.ds(off, width)] += part
         return carry
 
-    lax.fori_loop(0, steps, body, 0, unroll=8)
+    lax.fori_loop(0, steps, body, 0, unroll=16)
 
 
 def tab_plain(offs, seg, weights, out_width):

time: 149 us -> 147 us (0.987)
  Pallas kernels: 22 us -> 20.1 us
    pallas_call x1, Pallas kernels: 22 us -> 20.1 us  [tabulate(): pl.pallas_call(tab_kernel, out_shape=jax.ShapeDtypeStruct((reps, out_widt...]
where the time goes in v8:
time: 147 us; the launch traced here: 146 us
  blocking collectives  53.3 us (36%)
  local copies, waits for them, and re-layouts  26.1 us (18%)
  Pallas kernels  20.1 us (14%)
  waiting for transfers between devices  16.9 us (11%)
  matrix products  13 us (9%)
  other arithmetic  9.42 us (6%)
  starting transfers between devices  5.68 us (4%)
    all_to_all x1, blocking collectives, local(): lax.all_to_all(keep.reshape(owners * (county_here + 1), half), 'rows', 0,...  34.2 us
    pallas_call x1, Pallas kernels, tabulate(): pl.pallas_call(tab_kernel, out_shape=jax.ShapeDtypeStruct((reps, out_widt...  20.1 us
    all_to_all x1, blocking collectives, local(): lax.all_to_all(sent.reshape(shards * groups, stats.shape[1]), 'rep', 0, 0...  19.1 us
    all_to_all x1, waiting for transfers between devices, local(): lax.all_to_all(sent.reshape(owners * county_here, factors.shape[1]), 'row...  13.8 us
    dot_general x6, matrix products, exact_dot(): jnp.dot(left, right, precision=lax.Precision.HIGHEST, preferred_element_t...  13 us
    reshape x1, local copies, waits for them, and re-layouts, tabulate(): out = out.reshape(reps, groups, CELLS)  6.69 us
    transpose x1, local copies, waits for them, and re-layouts, tabulate(): return out.transpose(1, 0, 2).reshape(groups, reps * CELLS)  6.57 us
    all_to_all x1, starting transfers between devices, local(): lax.all_to_all(sent.reshape(owners * county_here, factors.shape[1]), 'row...  4.03 us
  transfers between devices with their start and end apart: 2, of which 2 were waited for; matrix products, arithmetic and copies ran while one was open for 2% of the time, Pallas kernels for 0%

profile of v8, /device:TPU:1, one launch (start us, length us, event | category | flops | bytes accessed | tf_op | source)
XLA Modules:
  0.0 145.7 jit_solution(6187473934934272311)
XLA Ops:
  0.7 1.0 reduce-window.9
  2.2 1.0 reshape.505
  3.2 2.0 %select_reduce_fusion.10 = (s32[256]{0:T(256)S(1)}, s32[256]{0:T(256)S(1)}, s32[256]{0:T(256)S(1)}, s32[256]{0:T(256)S(1)}, s32[256]{0:T(256)S(1)}, /*index=5*/s...) fusion(s32[256]{0:T(256)S(1)} %get-tuple-element.16, ...), kind=kLoop, calls=%fused_computation.36 | loop fusion | flops 8647936 | bytes 26624 | tf_op jit(solution)/shard_map/reduce_sum | solution.py:66
  5.8 1.2 multiply_add_fusion.seg_ref
  7.0 20.1 %shard_map.77 = f32[20,32768]{1,0:T(8,128)} custom-call(s32[256]{0:T(256)} %get-tuple-element.48.offs_ref, s32[256,256]{1,0:T(8,128)} %multiply_add_fusion.seg_ref, bf16[20,65536]{1,0:T(8,128)(2,1)} %w_ref.1), custom_call_target="tpu_custom_call" | custom-call | flops 1006632960 | bytes 5505024 | tf_op jit(solution)/shard_map/pallas_call | solution.py:73
  27.2 6.7 %reshape.506 = f32[20,1024,32]{2,1,0:T(8,128)} reshape(f32[20,32768]{1,0:T(8,128)} %shard_map.77) | data formatting | bytes 5242880 | tf_op jit(solution)/shard_map/reshape | solution.py:90
  33.8 6.6 %copy.30 = f32[1024,20,32]{0,2,1:T(8,128)S(1)} copy(f32[1024,20,32]{2,0,1:T(8,128)} %bitcast.38) | data formatting | bytes 5242880 | tf_op jit(solution)/shard_map/transpose | solution.py:91
  41.0 5.4 %fusion = f32[32,32,640]{2,1,0:T(8,128)S(1)} fusion(f32[1024,640,1]{0,1,2:T(8,128)S(1)} %bitcast.39, s32[32,32]{1,0:T(8,128)S(1)} %multiply_add_fusion.1, s32[1024]{0:T(1024)S(1)} %bitcast.49), kind=kOutput, calls=%fused_computation.3 | convolution fusion | flops 8054112256 | bytes 5251072 | tf_op jit(solution)/shard_map/dot_general | solution.py:95
  47.6 1.7 %collective-permute-start = (f32[32,33,320]{2,0,1:T(8,128)S(1)}, f32[32,33,320]{2,0,1:T(8,128)S(1)}, u32[]{:S(2)}, u32[]{:S(2)}) collective-permute-start(f32[32,33,320]{2,0,1:T(8,128)S(1)} %copy.32), channel_id=1, source_target_pairs={{0,4},{4,0},{8,12},{12,8},{16,20},{20,16},{24,28},{28,24},{32,36},... | collective-permute-start | bytes 4055048 | tf_op jit(solution)/shard_map/ppermute | solution.py:154
  49.2 3.1 %collective-permute-done = f32[32,33,320]{2,0,1:T(8,128)S(1)} collective-permute-done((f32[32,33,320]{2,0,1:T(8,128)S(1)}, f32[32,33,320]{2,0,1:T(8,128)S(1)}, u32[]{:S(2)}, u32[]{:S(2)}) %collective-permute-start) | collective-permute-done | bytes 1351712 | tf_op jit(solution)/shard_map/ppermute | solution.py:154
  52.3 1.1 copy_add_fusion
  53.4 34.2 %all_to_all.24 = f32[32,33,320]{2,1,0:T(8,128)S(1)} all-to-all(f32[32,33,320]{2,1,0:T(8,128)S(1)} %copy_add_fusion), channel_id=1, replica_groups=mesh['rows'=32,'rep'=4] {'rows'}, dimensions={0} | all-to-all | bytes 2703360 | tf_op jit(solution)/shard_map/all_to_all | solution.py:155
  91.6 1.1 broadcast_in_dim.87
  92.7 4.0 %all-to-all-start.1 = ((f32[32,32,240]{2,1,0:T(8,128)}), f32[32,32,240]{2,1,0:T(8,128)S(1)}, u32[]{:S(2)}, u32[]{:S(2)}) async-start(f32[32,32,240]{2,1,0:T(8,128)} %broadcast_in_dim.87), calls=%async_computation.1 | async-start | bytes 2097152 | tf_op jit(solution)/shard_map/all_to_all | solution.py:163
  96.7 3.2 %copy.39 = f32[1024,640]{1,0:T(8,128)} copy(f32[1024,640]{0,1:T(8,128)} %bitcast.40) | data formatting | bytes 5242880 | tf_op jit(solution)/shard_map/reshape | solution.py:91
  100.0 13.8 %all-to-all-done.1 = f32[32,32,240]{2,1,0:T(8,128)S(1)} async-done(((f32[32,32,240]{2,1,0:T(8,128)}), f32[32,32,240]{2,1,0:T(8,128)S(1)}, u32[]{:S(2)}, u32[]{:S(2)}) %all-to-all-start.1) | async-done | bytes 983072 | tf_op jit(solution)/shard_map/all_to_all | solution.py:163
  113.9 3.5 %gather_fusion = f32[1024,240]{1,0:T(8,128)S(1)} fusion(f32[1024,240]{1,0:T(8,128)S(1)} %bitcast.37, s32[1024]{0:T(1024)S(1)} %broadcast_clamp_fusion), kind=kCustom, calls=%fused_computation | custom fusion | bytes 1970176 | tf_op jit(solution)/shard_map/jit(_take)/gather | solution.py:166
  117.6 1.3 fusion.8
  119.1 1.8 %multiply_multiply_fusion = f32[1024,640]{1,0:T(8,128)S(1)} fusion(f32[1024,640]{1,0:T(8,128)S(1)} %copy-done.2, f32[1024,640]{1,0:T(8,128)S(1)} %fusion.8, f32[1024,240]{1,0:T(8,128)S(1)} %broadcast_select_fusion, s32[640]{0:T(1024)S(1)} %add_select_fusion, s32[640]{0:T(1024)S(1)} %get-tuple-element.59, s32[160]{0:T(256)S(1)} %get-tuple-element.62, ...), kind=kOutput, calls=%fused_computation.10 | convolution fusion | flops 1259909120 | bytes 8853760 | tf_op jit(solution)/shard_map/dot_general | solution.py:95
  120.9 1.5 %fusion.14 = f32[1024,32]{0,1:T(8,128)S(1)} fusion(f32[1024,640]{1,0:T(8,128)S(1)} %multiply_multiply_fusion, s32[640]{0:T(1024)S(1)} %fusion.47), kind=kOutput, calls=%fused_computation.48 | convolution fusion | flops 251678720 | bytes 2755072 | tf_op jit(solution)/shard_map/dot_general | solution.py:95
  122.3 1.5 %fusion.13 = f32[1024,640]{1,0:T(8,128)S(1)} fusion(s32[640]{0:T(1024)S(1)} %fusion.47, f32[1024,32]{0,1:T(8,128)S(1)} %fusion.14), kind=kOutput, calls=%fused_computation.47 | convolution fusion | flops 251711488 | bytes 2755072 | tf_op jit(solution)/shard_map/dot_general | solution.py:95
  123.9 1.6 %fusion.2 = f32[1024,32]{0,1:T(8,128)S(1)} fusion(f32[1024,640]{1,0:T(8,128)S(1)} %multiply_multiply_fusion, f32[1024,640]{1,0:T(8,128)S(1)} %fusion.13, s32[640]{0:T(1024)S(1)} %fusion.47), kind=kOutput, calls=%fused_computation.7 | convolution fusion | flops 252989440 | bytes 5376512 | tf_op jit(solution)/shard_map/dot_general | solution.py:95
  125.7 19.1 %all_to_all.25 = f32[4,1024,64]{1,2,0:T(8,128)S(1)} all-to-all(f32[4,1024,64]{1,2,0:T(8,128)S(1)} %broadcast_in_dim.89), channel_id=1, replica_groups=mesh['rows'=32,'rep'=4] {'rep'}, dimensions={0} | all-to-all | bytes 2097152 | tf_op jit(solution)/shard_map/all_to_all | solution.py:178
  144.9 0.8 fusion.37
  (84 shorter events, 7.3 us)
Async XLA Ops:
  33.8 6.6 %copy-start.4 = (s32[1024,1]{0,1:T(1,128)S(1)}, s32[1024,1]{0,1:T(1,128)}, u32[]{:S(2)}) copy-start(s32[1024,1]{0,1:T(1,128)} %param.9) | copy-start | bytes 12292
  40.4 6.0 %copy-start.1 = (f32[1024,20,32]{0,2,1:T(8,128)}, f32[1024,20,32]{0,2,1:T(8,128)S(1)}, u32[]{:S(2)}) copy-start(f32[1024,20,32]{0,2,1:T(8,128)S(1)} %copy.30) | copy-start | bytes 7864324
  47.6 4.8 %collective-permute-start = (f32[32,33,320]{2,0,1:T(8,128)S(1)}, f32[32,33,320]{2,0,1:T(8,128)S(1)}, u32[]{:S(2)}, u32[]{:S(2)}) collective-permute-start(f32[32,33,320]{2,0,1:T(8,128)S(1)} %copy.32), channel_id=1, source_target_pairs={{0,4},{4,0},{8,12},{12,8},{16,20},{20,16},{24,28},{28,24},{32,36},... | collective-permute-start | bytes 4055048 | tf_op jit(solution)/shard_map/ppermute | solution.py:154
  87.7 1.3 copy-start.5
  87.7 1.5 %copy-start.3 = (f32[32,8]{0,1:T(8,128)S(1)}, f32[32,8]{0,1:T(8,128)}, u32[]{:S(2)}) copy-start(f32[32,8]{0,1:T(8,128)} %param.11) | copy-start | bytes 3076
  92.7 21.2 %all-to-all-start.1 = ((f32[32,32,240]{2,1,0:T(8,128)}), f32[32,32,240]{2,1,0:T(8,128)S(1)}, u32[]{:S(2)}, u32[]{:S(2)}) async-start(f32[32,32,240]{2,1,0:T(8,128)} %broadcast_in_dim.87), calls=%async_computation.1 | async-start | bytes 2097152 | tf_op jit(solution)/shard_map/all_to_all | solution.py:163
  117.3 1.7 %copy-start.2 = (f32[1024,640]{1,0:T(8,128)S(1)}, f32[1024,640]{1,0:T(8,128)}, u32[]{:S(2)}) copy-start(f32[1024,640]{1,0:T(8,128)} %copy.39) | copy-start | bytes 7864324
  120.9 3.0 %copy-start = (f32[1024,640]{1,0:T(8,128)}, f32[1024,640]{1,0:T(8,128)S(1)}, u32[]{:S(2)}) copy-start(f32[1024,640]{1,0:T(8,128)S(1)} %multiply_multiply_fusion) | copy-start | bytes 7864324

commit v9 on v8

--- a/solution.py
+++ b/solution.py
@@ -33,7 +33,7 @@
         out_ref[:, pl.ds(off, width)] += part
         return carry
 
-    lax.fori_loop(0, steps, body, 0, unroll=16)
+    lax.fori_loop(0, steps, body, 0, unroll=32)
 
 
 def tab_plain(offs, seg, weights, out_width):
@@ -163,7 +163,7 @@
     factors = lax.all_to_all(
         sent.reshape(owners * county_here, factors.shape[1]), "rows", 0, 0, tiled=True
     )
-    mine = jnp.take(factors, county, axis=0)
+    mine = exact_dot(hits.T.astype(jnp.float32), factors)
     to_age, to_kind, cell_sum = spreaders(reps)
     factor = exact_dot(mine[:, :reps * AGES], to_age) * exact_dot(mine[:, reps * AGES:], to_kind)
     raked = tables * factor

time: 147 us -> 146 us (level)
  local copies, waits for them, and re-layouts: 26.1 us -> 21.3 us
  matrix products: 13 us -> 16.6 us
    dot_general x6 -> x7, matrix products: 13 us -> 16.6 us  [exact_dot(): jnp.dot(left, right, precision=lax.Precision.HIGHEST, preferred_element_t...]
    gather x1 -> x0, local copies, waits for them, and re-layouts: 3.46 us -> none  [local(): mine = jnp.take(factors, county, axis=0)]
  transfers between devices with their start and end apart: 2 -> 2, of which waited for: 2 -> 2; matrix products, arithmetic and copies ran while one was open for 2% -> 1% of each run, Pallas kernels for 0% -> 0%
where the time goes in v9:
time: 146 us; the launch traced here: 145 us
  blocking collectives  53.3 us (37%)
  local copies, waits for them, and re-layouts  21.3 us (15%)
  Pallas kernels  19.2 us (13%)
  waiting for transfers between devices  18.1 us (12%)
  matrix products  16.6 us (11%)
  other arithmetic  9.19 us (6%)
  starting transfers between devices  6.34 us (4%)
    all_to_all x1, blocking collectives, local(): lax.all_to_all(keep.reshape(owners * (county_here + 1), half), 'rows', 0,...  34.2 us
    pallas_call x1, Pallas kernels, tabulate(): pl.pallas_call(tab_kernel, out_shape=jax.ShapeDtypeStruct((reps, out_widt...  19.2 us
    all_to_all x1, blocking collectives, local(): lax.all_to_all(sent.reshape(shards * groups, stats.shape[1]), 'rep', 0, 0...  19.1 us
    dot_general x7, matrix products, exact_dot(): jnp.dot(left, right, precision=lax.Precision.HIGHEST, preferred_element_t...  16.6 us
    all_to_all x1, waiting for transfers between devices, local(): lax.all_to_all(sent.reshape(owners * county_here, factors.shape[1]), 'row...  15 us
    reshape x1, local copies, waits for them, and re-layouts, tabulate(): out = out.reshape(reps, groups, CELLS)  6.69 us
    transpose x1, local copies, waits for them, and re-layouts, tabulate(): return out.transpose(1, 0, 2).reshape(groups, reps * CELLS)  6.57 us
    all_to_all x1, starting transfers between devices, local(): lax.all_to_all(sent.reshape(owners * county_here, factors.shape[1]), 'row...  4.69 us
  transfers between devices with their start and end apart: 2, of which 2 were waited for; matrix products, arithmetic and copies ran while one was open for 1% of the time, Pallas kernels for 0%

profile of v9, /device:TPU:1, one launch (start us, length us, event | category | flops | bytes accessed | tf_op | source)
XLA Modules:
  0.0 145.2 jit_solution(2113366113172791119)
XLA Ops:
  0.7 1.0 reduce-window.9
  2.2 1.0 reshape.501
  3.2 2.0 %select_reduce_fusion.10 = (s32[256]{0:T(256)S(1)}, s32[256]{0:T(256)S(1)}, s32[256]{0:T(256)S(1)}, s32[256]{0:T(256)S(1)}, s32[256]{0:T(256)S(1)}, /*index=5*/s...) fusion(s32[256]{0:T(256)S(1)} %get-tuple-element.14, ...), kind=kLoop, calls=%fused_computation.36 | loop fusion | flops 8647936 | bytes 26624 | tf_op jit(solution)/shard_map/reduce_sum | solution.py:66
  5.8 1.2 multiply_add_fusion.seg_ref
  7.0 19.2 %shard_map.77 = f32[20,32768]{1,0:T(8,128)} custom-call(s32[256]{0:T(256)} %get-tuple-element.46.offs_ref, s32[256,256]{1,0:T(8,128)} %multiply_add_fusion.seg_ref, bf16[20,65536]{1,0:T(8,128)(2,1)} %w_ref.1), custom_call_target="tpu_custom_call" | custom-call | flops 1006632960 | bytes 5505024 | tf_op jit(solution)/shard_map/pallas_call | solution.py:73
  26.3 6.7 %reshape.502 = f32[20,1024,32]{2,1,0:T(8,128)} reshape(f32[20,32768]{1,0:T(8,128)} %shard_map.77) | data formatting | bytes 5242880 | tf_op jit(solution)/shard_map/reshape | solution.py:90
  32.9 6.6 %copy.30 = f32[1024,20,32]{0,2,1:T(8,128)S(1)} copy(f32[1024,20,32]{2,0,1:T(8,128)} %bitcast.37) | data formatting | bytes 5242880 | tf_op jit(solution)/shard_map/transpose | solution.py:91
  40.1 5.4 %fusion.1 = f32[32,32,640]{2,1,0:T(8,128)S(1)} fusion(f32[1024,640,1]{0,1,2:T(8,128)S(1)} %bitcast.38, s32[32,32]{1,0:T(8,128)S(1)} %multiply_add_fusion.1, s32[1024]{0:T(1024)S(1)} %bitcast.47), kind=kOutput, calls=%fused_computation.3 | convolution fusion | flops 8054112256 | bytes 5251072 | tf_op jit(solution)/shard_map/dot_general | solution.py:95
  46.7 1.6 %collective-permute-start = (f32[32,33,320]{2,0,1:T(8,128)S(1)}, f32[32,33,320]{2,0,1:T(8,128)S(1)}, u32[]{:S(2)}, u32[]{:S(2)}) collective-permute-start(f32[32,33,320]{2,0,1:T(8,128)S(1)} %copy.32), channel_id=1, source_target_pairs={{0,4},{4,0},{8,12},{12,8},{16,20},{20,16},{24,28},{28,24},{32,36},... | collective-permute-start | bytes 4055048 | tf_op jit(solution)/shard_map/ppermute | solution.py:154
  48.3 3.1 %collective-permute-done = f32[32,33,320]{2,0,1:T(8,128)S(1)} collective-permute-done((f32[32,33,320]{2,0,1:T(8,128)S(1)}, f32[32,33,320]{2,0,1:T(8,128)S(1)}, u32[]{:S(2)}, u32[]{:S(2)}) %collective-permute-start) | collective-permute-done | bytes 1351712 | tf_op jit(solution)/shard_map/ppermute | solution.py:154
  51.4 1.1 copy_add_fusion
  52.5 34.2 %all_to_all.24 = f32[32,33,320]{2,1,0:T(8,128)S(1)} all-to-all(f32[32,33,320]{2,1,0:T(8,128)S(1)} %copy_add_fusion), channel_id=1, replica_groups=mesh['rows'=32,'rep'=4] {'rows'}, dimensions={0} | all-to-all | bytes 2703360 | tf_op jit(solution)/shard_map/all_to_all | solution.py:155
  90.7 1.2 broadcast_in_dim.76
  91.8 4.7 %all-to-all-start.1 = ((f32[32,32,240]{2,1,0:T(8,128)}), f32[32,32,240]{2,1,0:T(8,128)}, u32[]{:S(2)}, u32[]{:S(2)}) async-start(f32[32,32,240]{2,1,0:T(8,128)} %broadcast_in_dim.76), calls=%async_computation.1 | async-start | bytes 2097152 | tf_op jit(solution)/shard_map/all_to_all | solution.py:163
  96.5 2.2 %copy.39 = f32[1024,640]{1,0:T(8,128)S(1)} copy(f32[1024,640]{0,1:T(8,128)} %bitcast.39) | data formatting | bytes 5242880 | tf_op jit(solution)/shard_map/reshape | solution.py:91
  98.7 15.0 %all-to-all-done.1 = f32[32,32,240]{2,1,0:T(8,128)} async-done(((f32[32,32,240]{2,1,0:T(8,128)}), f32[32,32,240]{2,1,0:T(8,128)}, u32[]{:S(2)}, u32[]{:S(2)}) %all-to-all-start.1) | async-done | bytes 983072 | tf_op jit(solution)/shard_map/all_to_all | solution.py:163
  113.7 3.4 %fusion = f32[1024,240]{0,1:T(8,128)S(1)} fusion(f32[1024,240]{1,0:T(8,128)} %bitcast.15, s32[1024]{0:T(1024)S(1)} %bitcast.48), kind=kOutput, calls=%fused_computation.2 | convolution fusion | flops 3020947456 | bytes 1970176 | tf_op jit(solution)/shard_map/dot_general | solution.py:95
  117.1 1.7 %fusion.9 = f32[1024,640]{1,0:T(8,128)S(1)} fusion(f32[1024,240]{0,1:T(8,128)S(1)} %fusion, s32[640]{0:T(1024)S(1)} %get-tuple-element.56, s32[640]{0:T(1024)S(1)} %get-tuple-element.57, s32[160]{0:T(256)S(1)} %get-tuple-element.58, s32[160]{0:T(256)S(1)} %get-tuple-element.59), kind=kOutput, calls=%fused_computation.39 | convolution fusion | flops 1258598400 | bytes 3287040 | tf_op jit(solution)/shard_map/dot_general | solution.py:95
  118.8 1.6 %multiply_multiply_fusion = f32[1024,640]{1,0:T(8,128)S(1)} fusion(f32[1024,640]{1,0:T(8,128)S(1)} %copy.39, f32[1024,640]{1,0:T(8,128)S(1)} %fusion.9, f32[1024,240]{0,1:T(8,128)S(1)} %fusion, s32[640]{0:T(1024)S(1)} %add_select_fusion.1, s32[640]{0:T(1024)S(1)} %get-tuple-element.57, s32[80]{0:T(128)S(1)} %get-tuple-element.60, s32[80]{0:T(128)S(1)} %get-tuple-element.61), kind=kOutput, calls=%fused_computation.10 | convolution fusion | flops 630609920 | bytes 8201216 | tf_op jit(solution)/shard_map/dot_general | solution.py:95
  120.4 1.5 %fusion.16 = f32[1024,32]{0,1:T(8,128)S(1)} fusion(f32[1024,640]{1,0:T(8,128)S(1)} %multiply_multiply_fusion, s32[640]{0:T(1024)S(1)} %fusion.49), kind=kOutput, calls=%fused_computation.48 | convolution fusion | flops 251678720 | bytes 2755072 | tf_op jit(solution)/shard_map/dot_general | solution.py:95
  121.9 1.5 %fusion.15 = f32[1024,640]{1,0:T(8,128)S(1)} fusion(s32[640]{0:T(1024)S(1)} %fusion.49, f32[1024,32]{0,1:T(8,128)S(1)} %fusion.16), kind=kOutput, calls=%fused_computation.47 | convolution fusion | flops 251711488 | bytes 2755072 | tf_op jit(solution)/shard_map/dot_general | solution.py:95
  123.4 1.6 %fusion.3 = f32[1024,32]{0,1:T(8,128)S(1)} fusion(f32[1024,640]{1,0:T(8,128)S(1)} %multiply_multiply_fusion, f32[1024,640]{1,0:T(8,128)S(1)} %fusion.15, s32[640]{0:T(1024)S(1)} %fusion.49), kind=kOutput, calls=%fused_computation.7 | convolution fusion | flops 252989440 | bytes 5376512 | tf_op jit(solution)/shard_map/dot_general | solution.py:95
  125.2 19.1 %all_to_all.25 = f32[4,1024,64]{1,2,0:T(8,128)S(1)} all-to-all(f32[4,1024,64]{1,2,0:T(8,128)S(1)} %broadcast_in_dim.77), channel_id=1, replica_groups=mesh['rows'=32,'rep'=4] {'rep'}, dimensions={0} | all-to-all | bytes 2097152 | tf_op jit(solution)/shard_map/all_to_all | solution.py:178
  144.5 0.8 fusion.39
  (79 shorter events, 6.8 us)
Async XLA Ops:
  32.9 6.6 %copy-start.4 = (s32[1024,1]{0,1:T(1,128)S(1)}, s32[1024,1]{0,1:T(1,128)}, u32[]{:S(2)}) copy-start(s32[1024,1]{0,1:T(1,128)} %param.9) | copy-start | bytes 12292
  39.5 6.0 %copy-start.1 = (f32[1024,20,32]{0,2,1:T(8,128)}, f32[1024,20,32]{0,2,1:T(8,128)S(1)}, u32[]{:S(2)}) copy-start(f32[1024,20,32]{0,2,1:T(8,128)S(1)} %copy.30) | copy-start | bytes 7864324
  46.7 4.8 %collective-permute-start = (f32[32,33,320]{2,0,1:T(8,128)S(1)}, f32[32,33,320]{2,0,1:T(8,128)S(1)}, u32[]{:S(2)}, u32[]{:S(2)}) collective-permute-start(f32[32,33,320]{2,0,1:T(8,128)S(1)} %copy.32), channel_id=1, source_target_pairs={{0,4},{4,0},{8,12},{12,8},{16,20},{20,16},{24,28},{28,24},{32,36},... | collective-permute-start | bytes 4055048 | tf_op jit(solution)/shard_map/ppermute | solution.py:154
  86.8 1.3 copy-start.3
  86.8 1.5 %copy-start.2 = (f32[32,8]{0,1:T(8,128)S(1)}, f32[32,8]{0,1:T(8,128)}, u32[]{:S(2)}) copy-start(f32[32,8]{0,1:T(8,128)} %param.11) | copy-start | bytes 3076
  91.8 21.9 %all-to-all-start.1 = ((f32[32,32,240]{2,1,0:T(8,128)}), f32[32,32,240]{2,1,0:T(8,128)}, u32[]{:S(2)}, u32[]{:S(2)}) async-start(f32[32,32,240]{2,1,0:T(8,128)} %broadcast_in_dim.76), calls=%async_computation.1 | async-start | bytes 2097152 | tf_op jit(solution)/shard_map/all_to_all | solution.py:163
  120.4 3.0 %copy-start = (f32[1024,640]{1,0:T(8,128)}, f32[1024,640]{1,0:T(8,128)S(1)}, u32[]{:S(2)}) copy-start(f32[1024,640]{1,0:T(8,128)S(1)} %multiply_multiply_fusion) | copy-start | bytes 7864324

commit v10 on v5

--- a/solution.py
+++ b/solution.py
@@ -10,8 +10,8 @@
 CELLS = 32
 LOW = 32
 ITERS = 4
-BLOCK = 128
-SPAN = 8
+BLOCK = 256
+SPAN = 12
 USE_KERNEL = True
 
 
@@ -33,7 +33,7 @@
         out_ref[:, pl.ds(off, width)] += part
         return carry
 
-    lax.fori_loop(0, steps, body, 0, unroll=8)
+    lax.fori_loop(0, steps, body, 0, unroll=64)
 
 
 def tab_plain(offs, seg, weights, out_width):
@@ -163,7 +163,7 @@
     factors = lax.all_to_all(
         sent.reshape(owners * county_here, factors.shape[1]), "rows", 0, 0, tiled=True
     )
-    mine = jnp.take(factors, county, axis=0)
+    mine = exact_dot(hits.T.astype(jnp.float32), factors)
     to_age, to_kind, cell_sum = spreaders(reps)
     factor = exact_dot(mine[:, :reps * AGES], to_age) * exact_dot(mine[:, reps * AGES:], to_kind)
     raked = tables * factor

time: 149 us -> 145 us (0.973)
  Pallas kernels: 22.7 us -> 18.8 us
  matrix products: 13 us -> 16.6 us
  local copies, waits for them, and re-layouts: 24.7 us -> 21.2 us
  other arithmetic: 11.5 us -> 9.35 us
    pallas_call x1, Pallas kernels: 22.7 us -> 18.8 us  [tabulate(): pl.pallas_call(tab_kernel, out_shape=jax.ShapeDtypeStruct((reps, out_widt...]
    dot_general x6 -> x7, matrix products: 13 us -> 16.6 us  [exact_dot(): jnp.dot(left, right, precision=lax.Precision.HIGHEST, preferred_element_t...]
    gather x1 -> x0, local copies, waits for them, and re-layouts: 3.46 us -> none  [local(): mine = jnp.take(factors, county, axis=0)]
where the time goes in v10:
time: 145 us; the launch traced here: 144 us
  blocking collectives  34.2 us (24%)
  waiting for transfers between devices  32.2 us (22%)
  local copies, waits for them, and re-layouts  21.2 us (15%)
  Pallas kernels  18.8 us (13%)
  matrix products  16.6 us (11%)
  starting transfers between devices  10.7 us (7%)
  other arithmetic  9.35 us (6%)
    all_to_all x1, blocking collectives, local(): lax.all_to_all(keep.reshape(owners * (county_here + 1), half), 'rows', 0,...  34.2 us
    pallas_call x1, Pallas kernels, tabulate(): pl.pallas_call(tab_kernel, out_shape=jax.ShapeDtypeStruct((reps, out_widt...  18.8 us
    dot_general x7, matrix products, exact_dot(): jnp.dot(left, right, precision=lax.Precision.HIGHEST, preferred_element_t...  16.6 us
    all_to_all x1, waiting for transfers between devices, local(): lax.all_to_all(sent.reshape(owners * county_here, factors.shape[1]), 'row...  15 us
    ppermute x3, waiting for transfers between devices, local(): lax.ppermute(stats, 'rep', [(i, (i + s) % shards) for i in range(shards)])  14.1 us
    transpose x1, local copies, waits for them, and re-layouts, tabulate(): return out.transpose(1, 0, 2).reshape(groups, reps * CELLS)  6.75 us
    reshape x1, local copies, waits for them, and re-layouts, tabulate(): out = out.reshape(reps, groups, CELLS)  6.69 us
    all_to_all x1, starting transfers between devices, local(): lax.all_to_all(sent.reshape(owners * county_here, factors.shape[1]), 'row...  4.69 us
  transfers between devices with their start and end apart: 5, of which 4 were waited for; matrix products, arithmetic and copies ran while one was open for 2% of the time, Pallas kernels for 0%

profile of v10, /device:TPU:1, one launch (start us, length us, event | category | flops | bytes accessed | tf_op | source)
XLA Modules:
  0.0 144.2 jit_solution(2199722134853185524)
XLA Ops:
  2.2 1.0 reshape.483
  3.2 2.0 %select_reduce_fusion.10 = (s32[256]{0:T(256)S(1)}, s32[256]{0:T(256)S(1)}, s32[256]{0:T(256)S(1)}, s32[256]{0:T(256)S(1)}, s32[256]{0:T(256)S(1)}, /*index=5*/s...) fusion(s32[256]{0:T(256)S(1)} %get-tuple-element.14, ...), kind=kLoop, calls=%fused_computation.36 | loop fusion | flops 8647936 | bytes 26624 | tf_op jit(solution)/shard_map/reduce_sum | solution.py:66
  5.8 1.2 multiply_add_fusion.seg_ref
  7.0 18.8 %shard_map.77 = f32[20,32768]{1,0:T(8,128)} custom-call(s32[256]{0:T(256)} %get-tuple-element.46.offs_ref, s32[256,256]{1,0:T(8,128)} %multiply_add_fusion.seg_ref, bf16[20,65536]{1,0:T(8,128)(2,1)} %w_ref.1), custom_call_target="tpu_custom_call" | custom-call | flops 1006632960 | bytes 5505024 | tf_op jit(solution)/shard_map/pallas_call | solution.py:73
  25.8 6.7 %reshape.484 = f32[20,1024,32]{2,1,0:T(8,128)} reshape(f32[20,32768]{1,0:T(8,128)} %shard_map.77) | data formatting | bytes 5242880 | tf_op jit(solution)/shard_map/reshape | solution.py:90
  32.5 6.8 %copy.28 = f32[1024,20,32]{0,2,1:T(8,128)S(1)} copy(f32[1024,20,32]{2,0,1:T(8,128)} %bitcast.27) | data formatting | bytes 5242880 | tf_op jit(solution)/shard_map/transpose | solution.py:91
  39.9 5.4 %fusion.1 = f32[32,32,640]{2,1,0:T(8,128)S(1)} fusion(f32[1024,640,1]{0,1,2:T(8,128)S(1)} %bitcast.28, s32[32,32]{1,0:T(8,128)S(1)} %multiply_add_fusion.1, s32[1024]{0:T(1024)S(1)} %bitcast.35), kind=kOutput, calls=%fused_computation.3 | convolution fusion | flops 8054112256 | bytes 5251072 | tf_op jit(solution)/shard_map/dot_general | solution.py:95
  46.4 1.5 %collective-permute-start = (f32[32,33,320]{2,0,1:T(8,128)S(1)}, f32[32,33,320]{2,0,1:T(8,128)S(1)}, u32[]{:S(2)}, u32[]{:S(2)}) collective-permute-start(f32[32,33,320]{2,0,1:T(8,128)S(1)} %copy.30), channel_id=1, source_target_pairs={{0,4},{4,0},{8,12},{12,8},{16,20},{20,16},{24,28},{28,24},{32,36},... | collective-permute-start | bytes 4055048 | tf_op jit(solution)/shard_map/ppermute | solution.py:154
  47.8 3.1 %collective-permute-done = f32[32,33,320]{2,0,1:T(8,128)S(1)} collective-permute-done((f32[32,33,320]{2,0,1:T(8,128)S(1)}, f32[32,33,320]{2,0,1:T(8,128)S(1)}, u32[]{:S(2)}, u32[]{:S(2)}) %collective-permute-start) | collective-permute-done | bytes 1351712 | tf_op jit(solution)/shard_map/ppermute | solution.py:154
  51.0 1.1 copy_add_fusion
  52.1 34.2 %all_to_all.15 = f32[32,33,320]{2,1,0:T(8,128)S(1)} all-to-all(f32[32,33,320]{2,1,0:T(8,128)S(1)} %copy_add_fusion), channel_id=1, replica_groups=mesh['rows'=32,'rep'=4] {'rows'}, dimensions={0} | all-to-all | bytes 2703360 | tf_op jit(solution)/shard_map/all_to_all | solution.py:155
  90.2 1.2 broadcast_in_dim.74
  91.4 4.7 %all-to-all-start.1 = ((f32[32,32,240]{2,1,0:T(8,128)}), f32[32,32,240]{2,1,0:T(8,128)}, u32[]{:S(2)}, u32[]{:S(2)}) async-start(f32[32,32,240]{2,1,0:T(8,128)} %broadcast_in_dim.74), calls=%async_computation.1 | async-start | bytes 2097152 | tf_op jit(solution)/shard_map/all_to_all | solution.py:163
  96.1 2.2 %copy.37 = f32[1024,640]{1,0:T(8,128)S(1)} copy(f32[1024,640]{0,1:T(8,128)} %bitcast.29) | data formatting | bytes 5242880 | tf_op jit(solution)/shard_map/reshape | solution.py:91
  98.3 15.0 %all-to-all-done.1 = f32[32,32,240]{2,1,0:T(8,128)} async-done(((f32[32,32,240]{2,1,0:T(8,128)}), f32[32,32,240]{2,1,0:T(8,128)}, u32[]{:S(2)}, u32[]{:S(2)}) %all-to-all-start.1) | async-done | bytes 983072 | tf_op jit(solution)/shard_map/all_to_all | solution.py:163
  113.3 3.4 %fusion = f32[1024,240]{0,1:T(8,128)S(1)} fusion(f32[1024,240]{1,0:T(8,128)} %bitcast.15, s32[1024]{0:T(1024)S(1)} %bitcast.36), kind=kOutput, calls=%fused_computation.2 | convolution fusion | flops 3020947456 | bytes 1970176 | tf_op jit(solution)/shard_map/dot_general | solution.py:95
  116.6 1.7 %fusion.9 = f32[1024,640]{1,0:T(8,128)S(1)} fusion(f32[1024,240]{0,1:T(8,128)S(1)} %fusion, s32[640]{0:T(1024)S(1)} %get-tuple-element.56, s32[640]{0:T(1024)S(1)} %get-tuple-element.57, s32[160]{0:T(256)S(1)} %get-tuple-element.58, s32[160]{0:T(256)S(1)} %get-tuple-element.59), kind=kOutput, calls=%fused_computation.39 | convolution fusion | flops 1258598400 | bytes 3287040 | tf_op jit(solution)/shard_map/dot_general | solution.py:95
  118.4 1.6 %multiply_multiply_fusion = f32[1024,640]{1,0:T(8,128)S(1)} fusion(f32[1024,640]{1,0:T(8,128)S(1)} %copy.37, f32[1024,640]{1,0:T(8,128)S(1)} %fusion.9, f32[1024,240]{0,1:T(8,128)S(1)} %fusion, s32[640]{0:T(1024)S(1)} %add_select_fusion.1, s32[640]{0:T(1024)S(1)} %get-tuple-element.57, s32[80]{0:T(128)S(1)} %get-tuple-element.60, s32[80]{0:T(128)S(1)} %get-tuple-element.61), kind=kOutput, calls=%fused_computation.10 | convolution fusion | flops 630609920 | bytes 8201216 | tf_op jit(solution)/shard_map/dot_general | solution.py:95
  119.9 1.5 %fusion.16 = f32[1024,32]{0,1:T(8,128)S(1)} fusion(f32[1024,640]{1,0:T(8,128)S(1)} %multiply_multiply_fusion, s32[640]{0:T(1024)S(1)} %fusion.49), kind=kOutput, calls=%fused_computation.48 | convolution fusion | flops 251678720 | bytes 2755072 | tf_op jit(solution)/shard_map/dot_general | solution.py:95
  121.4 1.5 %fusion.15 = f32[1024,640]{1,0:T(8,128)S(1)} fusion(s32[640]{0:T(1024)S(1)} %fusion.49, f32[1024,32]{0,1:T(8,128)S(1)} %fusion.16), kind=kOutput, calls=%fused_computation.47 | convolution fusion | flops 251711488 | bytes 2755072 | tf_op jit(solution)/shard_map/dot_general | solution.py:95
  123.0 1.6 %fusion.3 = f32[1024,32]{0,1:T(8,128)S(1)} fusion(f32[1024,640]{1,0:T(8,128)S(1)} %multiply_multiply_fusion, f32[1024,640]{1,0:T(8,128)S(1)} %fusion.15, s32[640]{0:T(1024)S(1)} %fusion.49), kind=kOutput, calls=%fused_computation.7 | convolution fusion | flops 252989440 | bytes 5376512 | tf_op jit(solution)/shard_map/dot_general | solution.py:95
  124.6 3.8 %collective-permute-start.1 = (f32[1024,64]{0,1:T(8,128)S(1)}, f32[1024,64]{0,1:T(8,128)S(1)}, u32[]{:S(2)}, u32[]{:S(2)}) collective-permute-start(f32[1024,64]{0,1:T(8,128)S(1)} %pad_maximum_fusion), channel_id=1, source_target_pairs={{0,3},{1,0},{2,1},{3,2},{4,7},{5,4},{6,5},{7,6},{8,11},{9,8},{10,9... | collective-permute-start | bytes 786440 | tf_op jit(solution)/shard_map/ppermute | solution.py:179
  129.1 10.2 %collective-permute-done.1 = f32[1024,64]{0,1:T(8,128)S(1)} collective-permute-done((f32[1024,64]{0,1:T(8,128)S(1)}, f32[1024,64]{0,1:T(8,128)S(1)}, u32[]{:S(2)}, u32[]{:S(2)}) %collective-permute-start.1) | collective-permute-done | bytes 262176 | tf_op jit(solution)/shard_map/ppermute | solution.py:179
  139.3 3.9 %collective-permute-done.3 = f32[1024,64]{0,1:T(8,128)S(1)} collective-permute-done((f32[1024,64]{0,1:T(8,128)S(1)}, f32[1024,64]{0,1:T(8,128)S(1)}, u32[]{:S(2)}, u32[]{:S(2)}) %collective-permute-start.3) | collective-permute-done | bytes 262176 | tf_op jit(solution)/shard_map/ppermute | solution.py:179
  (83 shorter events, 9.1 us)
Async XLA Ops:
  32.5 6.8 %copy-start.4 = (s32[1024,1]{0,1:T(1,128)S(1)}, s32[1024,1]{0,1:T(1,128)}, u32[]{:S(2)}) copy-start(s32[1024,1]{0,1:T(1,128)} %param.9) | copy-start | bytes 12292
  39.3 6.0 %copy-start.1 = (f32[1024,20,32]{0,2,1:T(8,128)}, f32[1024,20,32]{0,2,1:T(8,128)S(1)}, u32[]{:S(2)}) copy-start(f32[1024,20,32]{0,2,1:T(8,128)S(1)} %copy.28) | copy-start | bytes 7864324
  46.4 4.6 %collective-permute-start = (f32[32,33,320]{2,0,1:T(8,128)S(1)}, f32[32,33,320]{2,0,1:T(8,128)S(1)}, u32[]{:S(2)}, u32[]{:S(2)}) collective-permute-start(f32[32,33,320]{2,0,1:T(8,128)S(1)} %copy.30), channel_id=1, source_target_pairs={{0,4},{4,0},{8,12},{12,8},{16,20},{20,16},{24,28},{28,24},{32,36},... | collective-permute-start | bytes 4055048 | tf_op jit(solution)/shard_map/ppermute | solution.py:154
  86.3 1.3 copy-start.3
  86.3 1.5 %copy-start.2 = (f32[32,8]{0,1:T(8,128)S(1)}, f32[32,8]{0,1:T(8,128)}, u32[]{:S(2)}) copy-start(f32[32,8]{0,1:T(8,128)} %param.11) | copy-start | bytes 3076
  91.4 21.9 %all-to-all-start.1 = ((f32[32,32,240]{2,1,0:T(8,128)}), f32[32,32,240]{2,1,0:T(8,128)}, u32[]{:S(2)}, u32[]{:S(2)}) async-start(f32[32,32,240]{2,1,0:T(8,128)} %broadcast_in_dim.74), calls=%async_computation.1 | async-start | bytes 2097152 | tf_op jit(solution)/shard_map/all_to_all | solution.py:163
  119.9 3.0 %copy-start = (f32[1024,640]{1,0:T(8,128)}, f32[1024,640]{1,0:T(8,128)S(1)}, u32[]{:S(2)}) copy-start(f32[1024,640]{1,0:T(8,128)S(1)} %multiply_multiply_fusion) | copy-start | bytes 7864324
  124.6 14.7 %collective-permute-start.1 = (f32[1024,64]{0,1:T(8,128)S(1)}, f32[1024,64]{0,1:T(8,128)S(1)}, u32[]{:S(2)}, u32[]{:S(2)}) collective-permute-start(f32[1024,64]{0,1:T(8,128)S(1)} %pad_maximum_fusion), channel_id=1, source_target_pairs={{0,3},{1,0},{2,1},{3,2},{4,7},{5,4},{6,5},{7,6},{8,11},{9,8},{10,9... | collective-permute-start | bytes 786440 | tf_op jit(solution)/shard_map/ppermute | solution.py:179
  128.4 10.9 %collective-permute-start.2 = (f32[1024,64]{0,1:T(8,128)S(1)}, f32[1024,64]{0,1:T(8,128)S(1)}, u32[]{:S(2)}, u32[]{:S(2)}) collective-permute-start(f32[1024,64]{0,1:T(8,128)S(1)} %pad_maximum_fusion), channel_id=1, source_target_pairs={{0,2},{1,3},{2,0},{3,1},{4,6},{5,7},{6,4},{7,5},{8,10},{9,11},{10,... | collective-permute-start | bytes 786440 | tf_op jit(solution)/shard_map/ppermute | solution.py:179
  128.4 14.8 %collective-permute-start.3 = (f32[1024,64]{0,1:T(8,128)S(1)}, f32[1024,64]{0,1:T(8,128)S(1)}, u32[]{:S(2)}, u32[]{:S(2)}) collective-permute-start(f32[1024,64]{0,1:T(8,128)S(1)} %pad_maximum_fusion), channel_id=1, source_target_pairs={{0,1},{1,2},{2,3},{3,0},{4,5},{5,6},{6,7},{7,4},{8,9},{9,10},{10,1... | collective-permute-start | bytes 786440 | tf_op jit(solution)/shard_map/ppermute | solution.py:179

commit v11 on v10

--- a/solution.py
+++ b/solution.py
@@ -10,8 +10,8 @@
 CELLS = 32
 LOW = 32
 ITERS = 4
-BLOCK = 256
-SPAN = 12
+BLOCK = 512
+SPAN = 20
 USE_KERNEL = True
 
 
@@ -33,7 +33,7 @@
         out_ref[:, pl.ds(off, width)] += part
         return carry
 
-    lax.fori_loop(0, steps, body, 0, unroll=64)
+    lax.fori_loop(0, steps, body, 0, unroll=32)
 
 
 def tab_plain(offs, seg, weights, out_width):

time: 145 us -> 156 us (1.076)
  Pallas kernels: 18.8 us -> 29.8 us
    pallas_call x1, Pallas kernels: 18.8 us -> 29.8 us  [tabulate(): pl.pallas_call(tab_kernel, out_shape=jax.ShapeDtypeStruct((reps, out_widt...]
  transfers between devices with their start and end apart: 5 -> 5, of which waited for: 4 -> 4; matrix products, arithmetic and copies ran while one was open for 2% -> 1% of each run, Pallas kernels for 0% -> 0%
where the time goes in v11:
time: 156 us; the launch traced here: 155 us
  blocking collectives  34.2 us (22%)
  waiting for transfers between devices  32.1 us (21%)
  Pallas kernels  29.8 us (19%)
  local copies, waits for them, and re-layouts  21.2 us (14%)
  matrix products  16.6 us (11%)
  starting transfers between devices  10.7 us (7%)
  other arithmetic  9.21 us (6%)
    all_to_all x1, blocking collectives, local(): lax.all_to_all(keep.reshape(owners * (county_here + 1), half), 'rows', 0,...  34.2 us
    pallas_call x1, Pallas kernels, tabulate(): pl.pallas_call(tab_kernel, out_shape=jax.ShapeDtypeStruct((reps, out_widt...  29.8 us
    dot_general x7, matrix products, exact_dot(): jnp.dot(left, right, precision=lax.Precision.HIGHEST, preferred_element_t...  16.6 us
    all_to_all x1, waiting for transfers between devices, local(): lax.all_to_all(sent.reshape(owners * county_here, factors.shape[1]), 'row...  15 us
    ppermute x3, waiting for transfers between devices, local(): lax.ppermute(stats, 'rep', [(i, (i + s) % shards) for i in range(shards)])  14.1 us
    transpose x1, local copies, waits for them, and re-layouts, tabulate(): return out.transpose(1, 0, 2).reshape(groups, reps * CELLS)  6.75 us
    reshape x1, local copies, waits for them, and re-layouts, tabulate(): out = out.reshape(reps, groups, CELLS)  6.69 us
    all_to_all x1, starting transfers between devices, local(): lax.all_to_all(sent.reshape(owners * county_here, factors.shape[1]), 'row...  4.69 us
  transfers between devices with their start and end apart: 5, of which 4 were waited for; matrix products, arithmetic and copies ran while one was open for 1% of the time, Pallas kernels for 0%

profile of v11, /device:TPU:1, one launch (start us, length us, event | category | flops | bytes accessed | tf_op | source)
XLA Modules:
  0.0 155.1 jit_solution(16009319912990555209)
XLA Ops:
  2.2 1.5 select_reduce_fusion.18
  4.5 1.0 reshape.555
  5.5 1.4 multiply_add_fusion.seg_ref
  6.8 29.8 %shard_map.77 = f32[20,32768]{1,0:T(8,128)} custom-call(s32[128]{0:T(128)} %get-tuple-element.61.offs_ref, s32[128,512]{1,0:T(8,128)} %multiply_add_fusion.seg_ref, bf16[20,65536]{1,0:T(8,128)(2,1)} %w_ref.1), custom_call_target="tpu_custom_call" | custom-call | flops 1677721600 | bytes 5505024 | tf_op jit(solution)/shard_map/pallas_call | solution.py:73
  36.7 6.7 %reshape.556 = f32[20,1024,32]{2,1,0:T(8,128)} reshape(f32[20,32768]{1,0:T(8,128)} %shard_map.77) | data formatting | bytes 5242880 | tf_op jit(solution)/shard_map/reshape | solution.py:90
  43.4 6.8 %copy.28 = f32[1024,20,32]{0,2,1:T(8,128)S(1)} copy(f32[1024,20,32]{2,0,1:T(8,128)} %bitcast.27) | data formatting | bytes 5242880 | tf_op jit(solution)/shard_map/transpose | solution.py:91
  50.8 5.4 %fusion.1 = f32[32,32,640]{2,1,0:T(8,128)S(1)} fusion(f32[1024,640,1]{0,1,2:T(8,128)S(1)} %bitcast.28, s32[32,32]{1,0:T(8,128)S(1)} %multiply_add_fusion.1, s32[1024]{0:T(1024)S(1)} %bitcast.35), kind=kOutput, calls=%fused_computation.3 | convolution fusion | flops 8054112256 | bytes 5251072 | tf_op jit(solution)/shard_map/dot_general | solution.py:95
  57.3 1.5 collective-permute-start
  58.7 3.1 %collective-permute-done = f32[32,33,320]{2,0,1:T(8,128)S(1)} collective-permute-done((f32[32,33,320]{2,0,1:T(8,128)S(1)}, f32[32,33,320]{2,0,1:T(8,128)S(1)}, u32[]{:S(2)}, u32[]{:S(2)}) %collective-permute-start) | collective-permute-done | bytes 1351712 | tf_op jit(solution)/shard_map/ppermute | solution.py:154
  61.8 1.1 copy_add_fusion
  63.0 34.2 %all_to_all.15 = f32[32,33,320]{2,1,0:T(8,128)S(1)} all-to-all(f32[32,33,320]{2,1,0:T(8,128)S(1)} %copy_add_fusion), channel_id=1, replica_groups=mesh['rows'=32,'rep'=4] {'rows'}, dimensions={0} | all-to-all | bytes 2703360 | tf_op jit(solution)/shard_map/all_to_all | solution.py:155
  101.1 1.2 broadcast_in_dim.114
  102.3 4.7 %all-to-all-start.1 = ((f32[32,32,240]{2,1,0:T(8,128)}), f32[32,32,240]{2,1,0:T(8,128)}, u32[]{:S(2)}, u32[]{:S(2)}) async-start(f32[32,32,240]{2,1,0:T(8,128)} %broadcast_in_dim.114), calls=%async_computation.1 | async-start | bytes 2097152 | tf_op jit(solution)/shard_map/all_to_all | solution.py:163
  107.0 2.2 %copy.37 = f32[1024,640]{1,0:T(8,128)S(1)} copy(f32[1024,640]{0,1:T(8,128)} %bitcast.29) | data formatting | bytes 5242880 | tf_op jit(solution)/shard_map/reshape | solution.py:91
  109.2 15.0 %all-to-all-done.1 = f32[32,32,240]{2,1,0:T(8,128)} async-done(((f32[32,32,240]{2,1,0:T(8,128)}), f32[32,32,240]{2,1,0:T(8,128)}, u32[]{:S(2)}, u32[]{:S(2)}) %all-to-all-start.1) | async-done | bytes 983072 | tf_op jit(solution)/shard_map/all_to_all | solution.py:163
  124.2 3.4 %fusion = f32[1024,240]{0,1:T(8,128)S(1)} fusion(f32[1024,240]{1,0:T(8,128)} %bitcast.15, s32[1024]{0:T(1024)S(1)} %bitcast.36), kind=kOutput, calls=%fused_computation.2 | convolution fusion | flops 3020947456 | bytes 1970176 | tf_op jit(solution)/shard_map/dot_general | solution.py:95
  127.5 1.7 %fusion.9 = f32[1024,640]{1,0:T(8,128)S(1)} fusion(f32[1024,240]{0,1:T(8,128)S(1)} %fusion, s32[640]{0:T(1024)S(1)} %get-tuple-element.78, s32[640]{0:T(1024)S(1)} %get-tuple-element.79, s32[160]{0:T(256)S(1)} %get-tuple-element.80, s32[160]{0:T(256)S(1)} %get-tuple-element.81), kind=kOutput, calls=%fused_computation.16 | convolution fusion | flops 1258598400 | bytes 3287040 | tf_op jit(solution)/shard_map/dot_general | solution.py:95
  129.3 1.6 %multiply_multiply_fusion = f32[1024,640]{1,0:T(8,128)S(1)} fusion(f32[1024,640]{1,0:T(8,128)S(1)} %copy.37, f32[1024,640]{1,0:T(8,128)S(1)} %fusion.9, f32[1024,240]{0,1:T(8,128)S(1)} %fusion, s32[640]{0:T(1024)S(1)} %add_select_fusion.1, s32[640]{0:T(1024)S(1)} %get-tuple-element.79, s32[80]{0:T(128)S(1)} %get-tuple-element.82, s32[80]{0:T(128)S(1)} %get-tuple-element.83), kind=kOutput, calls=%fused_computation.10 | convolution fusion | flops 630609920 | bytes 8201216 | tf_op jit(solution)/shard_map/dot_general | solution.py:95
  130.8 1.5 fusion.16
  132.3 1.5 fusion.15
  133.9 1.6 %fusion.3 = f32[1024,32]{0,1:T(8,128)S(1)} fusion(f32[1024,640]{1,0:T(8,128)S(1)} %multiply_multiply_fusion, f32[1024,640]{1,0:T(8,128)S(1)} %fusion.15, s32[640]{0:T(1024)S(1)} %fusion.57), kind=kOutput, calls=%fused_computation.7 | convolution fusion | flops 252989440 | bytes 5376512 | tf_op jit(solution)/shard_map/dot_general | solution.py:95
  135.5 3.8 %collective-permute-start.1 = (f32[1024,64]{0,1:T(8,128)S(1)}, f32[1024,64]{0,1:T(8,128)S(1)}, u32[]{:S(2)}, u32[]{:S(2)}) collective-permute-start(f32[1024,64]{0,1:T(8,128)S(1)} %pad_maximum_fusion), channel_id=1, source_target_pairs={{0,3},{1,0},{2,1},{3,2},{4,7},{5,4},{6,5},{7,6},{8,11},{9,8},{10,9... | collective-permute-start | bytes 786440 | tf_op jit(solution)/shard_map/ppermute | solution.py:179
  140.0 10.2 %collective-permute-done.1 = f32[1024,64]{0,1:T(8,128)S(1)} collective-permute-done((f32[1024,64]{0,1:T(8,128)S(1)}, f32[1024,64]{0,1:T(8,128)S(1)}, u32[]{:S(2)}, u32[]{:S(2)}) %collective-permute-start.1) | collective-permute-done | bytes 262176 | tf_op jit(solution)/shard_map/ppermute | solution.py:179
  150.2 3.9 %collective-permute-done.3 = f32[1024,64]{0,1:T(8,128)S(1)} collective-permute-done((f32[1024,64]{0,1:T(8,128)S(1)}, f32[1024,64]{0,1:T(8,128)S(1)}, u32[]{:S(2)}, u32[]{:S(2)}) %collective-permute-start.3) | collective-permute-done | bytes 262176 | tf_op jit(solution)/shard_map/ppermute | solution.py:179
  (85 shorter events, 9.3 us)
Async XLA Ops:
  43.4 6.8 %copy-start.4 = (s32[1024,1]{0,1:T(1,128)S(1)}, s32[1024,1]{0,1:T(1,128)}, u32[]{:S(2)}) copy-start(s32[1024,1]{0,1:T(1,128)} %param.9) | copy-start | bytes 12292
  50.1 6.0 %copy-start.1 = (f32[1024,20,32]{0,2,1:T(8,128)}, f32[1024,20,32]{0,2,1:T(8,128)S(1)}, u32[]{:S(2)}) copy-start(f32[1024,20,32]{0,2,1:T(8,128)S(1)} %copy.28) | copy-start | bytes 7864324
  57.3 4.6 %collective-permute-start = (f32[32,33,320]{2,0,1:T(8,128)S(1)}, f32[32,33,320]{2,0,1:T(8,128)S(1)}, u32[]{:S(2)}, u32[]{:S(2)}) collective-permute-start(f32[32,33,320]{2,0,1:T(8,128)S(1)} %copy.30), channel_id=1, source_target_pairs={{0,4},{4,0},{8,12},{12,8},{16,20},{20,16},{24,28},{28,24},{32,36},... | collective-permute-start | bytes 4055048 | tf_op jit(solution)/shard_map/ppermute | solution.py:154
  97.2 1.3 copy-start.3
  97.2 1.5 copy-start.2
  102.3 21.9 %all-to-all-start.1 = ((f32[32,32,240]{2,1,0:T(8,128)}), f32[32,32,240]{2,1,0:T(8,128)}, u32[]{:S(2)}, u32[]{:S(2)}) async-start(f32[32,32,240]{2,1,0:T(8,128)} %broadcast_in_dim.114), calls=%async_computation.1 | async-start | bytes 2097152 | tf_op jit(solution)/shard_map/all_to_all | solution.py:163
  130.8 3.0 %copy-start = (f32[1024,640]{1,0:T(8,128)}, f32[1024,640]{1,0:T(8,128)S(1)}, u32[]{:S(2)}) copy-start(f32[1024,640]{1,0:T(8,128)S(1)} %multiply_multiply_fusion) | copy-start | bytes 7864324
  135.5 14.7 %collective-permute-start.1 = (f32[1024,64]{0,1:T(8,128)S(1)}, f32[1024,64]{0,1:T(8,128)S(1)}, u32[]{:S(2)}, u32[]{:S(2)}) collective-permute-start(f32[1024,64]{0,1:T(8,128)S(1)} %pad_maximum_fusion), channel_id=1, source_target_pairs={{0,3},{1,0},{2,1},{3,2},{4,7},{5,4},{6,5},{7,6},{8,11},{9,8},{10,9... | collective-permute-start | bytes 786440 | tf_op jit(solution)/shard_map/ppermute | solution.py:179
  139.3 10.9 %collective-permute-start.2 = (f32[1024,64]{0,1:T(8,128)S(1)}, f32[1024,64]{0,1:T(8,128)S(1)}, u32[]{:S(2)}, u32[]{:S(2)}) collective-permute-start(f32[1024,64]{0,1:T(8,128)S(1)} %pad_maximum_fusion), channel_id=1, source_target_pairs={{0,2},{1,3},{2,0},{3,1},{4,6},{5,7},{6,4},{7,5},{8,10},{9,11},{10,... | collective-permute-start | bytes 786440 | tf_op jit(solution)/shard_map/ppermute | solution.py:179
  139.3 14.8 %collective-permute-start.3 = (f32[1024,64]{0,1:T(8,128)S(1)}, f32[1024,64]{0,1:T(8,128)S(1)}, u32[]{:S(2)}, u32[]{:S(2)}) collective-permute-start(f32[1024,64]{0,1:T(8,128)S(1)} %pad_maximum_fusion), channel_id=1, source_target_pairs={{0,1},{1,2},{2,3},{3,0},{4,5},{5,6},{6,7},{7,4},{8,9},{9,10},{10,1... | collective-permute-start | bytes 786440 | tf_op jit(solution)/shard_map/ppermute | solution.py:179

commit v12 on v10

--- a/solution.py
+++ b/solution.py
@@ -159,13 +159,14 @@
     county_tables = jnp.concatenate([summed[0, :county_here], summed[1, :county_here]], axis=1)
     groups_in = summed[0, county_here, :county_here]
     factors = rake_own(county_tables, groups_in, age_rate, kind_rate)
+    factors = jnp.pad(factors, ((0, 0), (0, (-factors.shape[1]) % 128)))
     sent = jnp.broadcast_to(factors[None], (owners,) + factors.shape)
     factors = lax.all_to_all(
         sent.reshape(owners * county_here, factors.shape[1]), "rows", 0, 0, tiled=True
     )
     mine = exact_dot(hits.T.astype(jnp.float32), factors)
     to_age, to_kind, cell_sum = spreaders(reps)
-    factor = exact_dot(mine[:, :reps * AGES], to_age) * exact_dot(mine[:, reps * AGES:], to_kind)
+    factor = exact_dot(mine[:, :reps * AGES], to_age) * exact_dot(mine[:, reps * AGES:reps * (AGES + KINDS)], to_kind)
     raked = tables * factor
 
     part_sum = exact_dot(raked, cell_sum)

time: 145 us -> 145 us (level)
  no operation moved by 1% of the time
where the time goes in v12:
time: 145 us; the launch traced here: 144 us
  blocking collectives  34.3 us (24%)
  waiting for transfers between devices  32.1 us (22%)
  local copies, waits for them, and re-layouts  21.2 us (15%)
  Pallas kernels  18.8 us (13%)
  matrix products  16.7 us (12%)
  starting transfers between devices  10.7 us (7%)
  other arithmetic  9.35 us (6%)
    all_to_all x1, blocking collectives, local(): lax.all_to_all(keep.reshape(owners * (county_here + 1), half), 'rows', 0,...  34.3 us
    pallas_call x1, Pallas kernels, tabulate(): pl.pallas_call(tab_kernel, out_shape=jax.ShapeDtypeStruct((reps, out_widt...  18.8 us
    dot_general x7, matrix products, exact_dot(): jnp.dot(left, right, precision=lax.Precision.HIGHEST, preferred_element_t...  16.7 us
    all_to_all x1, waiting for transfers between devices, local(): lax.all_to_all(sent.reshape(owners * county_here, factors.shape[1]), 'row...  15 us
    ppermute x3, waiting for transfers between devices, local(): lax.ppermute(stats, 'rep', [(i, (i + s) % shards) for i in range(shards)])  14.1 us
    transpose x1, local copies, waits for them, and re-layouts, tabulate(): return out.transpose(1, 0, 2).reshape(groups, reps * CELLS)  6.75 us
    reshape x1, local copies, waits for them, and re-layouts, tabulate(): out = out.reshape(reps, groups, CELLS)  6.69 us
    all_to_all x1, starting transfers between devices, local(): lax.all_to_all(sent.reshape(owners * county_here, factors.shape[1]), 'row...  4.69 us
  transfers between devices with their start and end apart: 5, of which 4 were waited for; matrix products, arithmetic and copies ran while one was open for 2% of the time, Pallas kernels for 0%

profile of v12, /device:TPU:1, one launch (start us, length us, event | category | flops | bytes accessed | tf_op | source)
XLA Modules:
  0.0 144.2 jit_solution(5738061249765818832)
XLA Ops:
  2.2 1.0 reshape.483
  3.2 2.0 %select_reduce_fusion.10 = (s32[256]{0:T(256)S(1)}, s32[256]{0:T(256)S(1)}, s32[256]{0:T(256)S(1)}, s32[256]{0:T(256)S(1)}, s32[256]{0:T(256)S(1)}, /*index=5*/s...) fusion(s32[256]{0:T(256)S(1)} %get-tuple-element.14, ...), kind=kLoop, calls=%fused_computation.36 | loop fusion | flops 8647936 | bytes 26624 | tf_op jit(solution)/shard_map/reduce_sum | solution.py:66
  5.8 1.2 multiply_add_fusion.seg_ref
  7.0 18.8 %shard_map.77 = f32[20,32768]{1,0:T(8,128)} custom-call(s32[256]{0:T(256)} %get-tuple-element.46.offs_ref, s32[256,256]{1,0:T(8,128)} %multiply_add_fusion.seg_ref, bf16[20,65536]{1,0:T(8,128)(2,1)} %w_ref.1), custom_call_target="tpu_custom_call" | custom-call | flops 1006632960 | bytes 5505024 | tf_op jit(solution)/shard_map/pallas_call | solution.py:73
  25.8 6.7 %reshape.484 = f32[20,1024,32]{2,1,0:T(8,128)} reshape(f32[20,32768]{1,0:T(8,128)} %shard_map.77) | data formatting | bytes 5242880 | tf_op jit(solution)/shard_map/reshape | solution.py:90
  32.5 6.8 %copy.28 = f32[1024,20,32]{0,2,1:T(8,128)S(1)} copy(f32[1024,20,32]{2,0,1:T(8,128)} %bitcast.27) | data formatting | bytes 5242880 | tf_op jit(solution)/shard_map/transpose | solution.py:91
  39.9 5.4 %fusion.1 = f32[32,32,640]{2,1,0:T(8,128)S(1)} fusion(f32[1024,640,1]{0,1,2:T(8,128)S(1)} %bitcast.28, s32[32,32]{1,0:T(8,128)S(1)} %multiply_add_fusion.1, s32[1024]{0:T(1024)S(1)} %bitcast.35), kind=kOutput, calls=%fused_computation.3 | convolution fusion | flops 8054112256 | bytes 5251072 | tf_op jit(solution)/shard_map/dot_general | solution.py:95
  46.4 1.5 %collective-permute-start = (f32[32,33,320]{2,0,1:T(8,128)S(1)}, f32[32,33,320]{2,0,1:T(8,128)S(1)}, u32[]{:S(2)}, u32[]{:S(2)}) collective-permute-start(f32[32,33,320]{2,0,1:T(8,128)S(1)} %copy.30), channel_id=1, source_target_pairs={{0,4},{4,0},{8,12},{12,8},{16,20},{20,16},{24,28},{28,24},{32,36},... | collective-permute-start | bytes 4055048 | tf_op jit(solution)/shard_map/ppermute | solution.py:154
  47.8 3.1 %collective-permute-done = f32[32,33,320]{2,0,1:T(8,128)S(1)} collective-permute-done((f32[32,33,320]{2,0,1:T(8,128)S(1)}, f32[32,33,320]{2,0,1:T(8,128)S(1)}, u32[]{:S(2)}, u32[]{:S(2)}) %collective-permute-start) | collective-permute-done | bytes 1351712 | tf_op jit(solution)/shard_map/ppermute | solution.py:154
  50.9 1.1 copy_add_fusion
  52.1 34.3 %all_to_all.15 = f32[32,33,320]{2,1,0:T(8,128)S(1)} all-to-all(f32[32,33,320]{2,1,0:T(8,128)S(1)} %copy_add_fusion), channel_id=1, replica_groups=mesh['rows'=32,'rep'=4] {'rows'}, dimensions={0} | all-to-all | bytes 2703360 | tf_op jit(solution)/shard_map/all_to_all | solution.py:155
  90.2 1.2 broadcast_in_dim.74
  91.4 4.7 %all-to-all-start.1 = ((f32[32,32,256]{2,1,0:T(8,128)}), f32[32,32,256]{2,1,0:T(8,128)}, u32[]{:S(2)}, u32[]{:S(2)}) async-start(f32[32,32,256]{2,1,0:T(8,128)} %broadcast_in_dim.74), calls=%async_computation.1 | async-start | bytes 2097152 | tf_op jit(solution)/shard_map/all_to_all | solution.py:164
  96.1 2.2 %copy.37 = f32[1024,640]{1,0:T(8,128)S(1)} copy(f32[1024,640]{0,1:T(8,128)} %bitcast.29) | data formatting | bytes 5242880 | tf_op jit(solution)/shard_map/reshape | solution.py:91
  98.3 15.0 %all-to-all-done.1 = f32[32,32,256]{2,1,0:T(8,128)} async-done(((f32[32,32,256]{2,1,0:T(8,128)}), f32[32,32,256]{2,1,0:T(8,128)}, u32[]{:S(2)}, u32[]{:S(2)}) %all-to-all-start.1) | async-done | bytes 1048608 | tf_op jit(solution)/shard_map/all_to_all | solution.py:164
  113.3 3.4 %fusion = f32[1024,256]{0,1:T(8,128)S(1)} fusion(f32[1024,256]{1,0:T(8,128)} %bitcast.15, s32[1024]{0:T(1024)S(1)} %bitcast.36), kind=kOutput, calls=%fused_computation.2 | convolution fusion | flops 3222274048 | bytes 2101248 | tf_op jit(solution)/shard_map/dot_general | solution.py:95
  116.7 1.7 %fusion.9 = f32[1024,640]{1,0:T(8,128)S(1)} fusion(f32[1024,256]{0,1:T(8,128)S(1)} %fusion, s32[640]{0:T(1024)S(1)} %get-tuple-element.56, s32[640]{0:T(1024)S(1)} %get-tuple-element.57, s32[160]{0:T(256)S(1)} %get-tuple-element.58, s32[160]{0:T(256)S(1)} %get-tuple-element.59), kind=kOutput, calls=%fused_computation.39 | convolution fusion | flops 1258598400 | bytes 3287040 | tf_op jit(solution)/shard_map/dot_general | solution.py:95
  118.4 1.6 %multiply_multiply_fusion = f32[1024,640]{1,0:T(8,128)S(1)} fusion(f32[1024,640]{1,0:T(8,128)S(1)} %copy.37, f32[1024,640]{1,0:T(8,128)S(1)} %fusion.9, f32[1024,256]{0,1:T(8,128)S(1)} %fusion, s32[640]{0:T(1024)S(1)} %add_select_fusion.1, s32[640]{0:T(1024)S(1)} %get-tuple-element.57, s32[80]{0:T(128)S(1)} %get-tuple-element.60, s32[80]{0:T(128)S(1)} %get-tuple-element.61), kind=kOutput, calls=%fused_computation.10 | convolution fusion | flops 630609920 | bytes 8201216 | tf_op jit(solution)/shard_map/dot_general | solution.py:95
  120.0 1.5 %fusion.16 = f32[1024,32]{0,1:T(8,128)S(1)} fusion(f32[1024,640]{1,0:T(8,128)S(1)} %multiply_multiply_fusion, s32[640]{0:T(1024)S(1)} %fusion.49), kind=kOutput, calls=%fused_computation.48 | convolution fusion | flops 251678720 | bytes 2755072 | tf_op jit(solution)/shard_map/dot_general | solution.py:95
  121.5 1.5 %fusion.15 = f32[1024,640]{1,0:T(8,128)S(1)} fusion(s32[640]{0:T(1024)S(1)} %fusion.49, f32[1024,32]{0,1:T(8,128)S(1)} %fusion.16), kind=kOutput, calls=%fused_computation.47 | convolution fusion | flops 251711488 | bytes 2755072 | tf_op jit(solution)/shard_map/dot_general | solution.py:95
  123.0 1.6 %fusion.3 = f32[1024,32]{0,1:T(8,128)S(1)} fusion(f32[1024,640]{1,0:T(8,128)S(1)} %multiply_multiply_fusion, f32[1024,640]{1,0:T(8,128)S(1)} %fusion.15, s32[640]{0:T(1024)S(1)} %fusion.49), kind=kOutput, calls=%fused_computation.7 | convolution fusion | flops 252989440 | bytes 5376512 | tf_op jit(solution)/shard_map/dot_general | solution.py:95
  124.7 3.8 %collective-permute-start.1 = (f32[1024,64]{0,1:T(8,128)S(1)}, f32[1024,64]{0,1:T(8,128)S(1)}, u32[]{:S(2)}, u32[]{:S(2)}) collective-permute-start(f32[1024,64]{0,1:T(8,128)S(1)} %pad_maximum_fusion), channel_id=1, source_target_pairs={{0,3},{1,0},{2,1},{3,2},{4,7},{5,4},{6,5},{7,6},{8,11},{9,8},{10,9... | collective-permute-start | bytes 786440 | tf_op jit(solution)/shard_map/ppermute | solution.py:180
  129.2 10.2 %collective-permute-done.1 = f32[1024,64]{0,1:T(8,128)S(1)} collective-permute-done((f32[1024,64]{0,1:T(8,128)S(1)}, f32[1024,64]{0,1:T(8,128)S(1)}, u32[]{:S(2)}, u32[]{:S(2)}) %collective-permute-start.1) | collective-permute-done | bytes 262176 | tf_op jit(solution)/shard_map/ppermute | solution.py:180
  139.4 3.9 %collective-permute-done.3 = f32[1024,64]{0,1:T(8,128)S(1)} collective-permute-done((f32[1024,64]{0,1:T(8,128)S(1)}, f32[1024,64]{0,1:T(8,128)S(1)}, u32[]{:S(2)}, u32[]{:S(2)}) %collective-permute-start.3) | collective-permute-done | bytes 262176 | tf_op jit(solution)/shard_map/ppermute | solution.py:180
  (83 shorter events, 9.1 us)
Async XLA Ops:
  32.5 6.8 %copy-start.4 = (s32[1024,1]{0,1:T(1,128)S(1)}, s32[1024,1]{0,1:T(1,128)}, u32[]{:S(2)}) copy-start(s32[1024,1]{0,1:T(1,128)} %param.9) | copy-start | bytes 12292
  39.3 6.0 %copy-start.1 = (f32[1024,20,32]{0,2,1:T(8,128)}, f32[1024,20,32]{0,2,1:T(8,128)S(1)}, u32[]{:S(2)}) copy-start(f32[1024,20,32]{0,2,1:T(8,128)S(1)} %copy.28) | copy-start | bytes 7864324
  46.4 4.6 %collective-permute-start = (f32[32,33,320]{2,0,1:T(8,128)S(1)}, f32[32,33,320]{2,0,1:T(8,128)S(1)}, u32[]{:S(2)}, u32[]{:S(2)}) collective-permute-start(f32[32,33,320]{2,0,1:T(8,128)S(1)} %copy.30), channel_id=1, source_target_pairs={{0,4},{4,0},{8,12},{12,8},{16,20},{20,16},{24,28},{28,24},{32,36},... | collective-permute-start | bytes 4055048 | tf_op jit(solution)/shard_map/ppermute | solution.py:154
  86.3 1.3 copy-start.3
  86.3 1.5 %copy-start.2 = (f32[32,8]{0,1:T(8,128)S(1)}, f32[32,8]{0,1:T(8,128)}, u32[]{:S(2)}) copy-start(f32[32,8]{0,1:T(8,128)} %param.11) | copy-start | bytes 3076
  91.4 21.9 %all-to-all-start.1 = ((f32[32,32,256]{2,1,0:T(8,128)}), f32[32,32,256]{2,1,0:T(8,128)}, u32[]{:S(2)}, u32[]{:S(2)}) async-start(f32[32,32,256]{2,1,0:T(8,128)} %broadcast_in_dim.74), calls=%async_computation.1 | async-start | bytes 2097152 | tf_op jit(solution)/shard_map/all_to_all | solution.py:164
  120.0 3.0 %copy-start = (f32[1024,640]{1,0:T(8,128)}, f32[1024,640]{1,0:T(8,128)S(1)}, u32[]{:S(2)}) copy-start(f32[1024,640]{1,0:T(8,128)S(1)} %multiply_multiply_fusion) | copy-start | bytes 7864324
  124.7 14.7 %collective-permute-start.1 = (f32[1024,64]{0,1:T(8,128)S(1)}, f32[1024,64]{0,1:T(8,128)S(1)}, u32[]{:S(2)}, u32[]{:S(2)}) collective-permute-start(f32[1024,64]{0,1:T(8,128)S(1)} %pad_maximum_fusion), channel_id=1, source_target_pairs={{0,3},{1,0},{2,1},{3,2},{4,7},{5,4},{6,5},{7,6},{8,11},{9,8},{10,9... | collective-permute-start | bytes 786440 | tf_op jit(solution)/shard_map/ppermute | solution.py:180
  128.5 10.9 %collective-permute-start.2 = (f32[1024,64]{0,1:T(8,128)S(1)}, f32[1024,64]{0,1:T(8,128)S(1)}, u32[]{:S(2)}, u32[]{:S(2)}) collective-permute-start(f32[1024,64]{0,1:T(8,128)S(1)} %pad_maximum_fusion), channel_id=1, source_target_pairs={{0,2},{1,3},{2,0},{3,1},{4,6},{5,7},{6,4},{7,5},{8,10},{9,11},{10,... | collective-permute-start | bytes 786440 | tf_op jit(solution)/shard_map/ppermute | solution.py:180
  128.5 14.8 %collective-permute-start.3 = (f32[1024,64]{0,1:T(8,128)S(1)}, f32[1024,64]{0,1:T(8,128)S(1)}, u32[]{:S(2)}, u32[]{:S(2)}) collective-permute-start(f32[1024,64]{0,1:T(8,128)S(1)} %pad_maximum_fusion), channel_id=1, source_target_pairs={{0,1},{1,2},{2,3},{3,0},{4,5},{5,6},{6,7},{7,4},{8,9},{9,10},{10,1... | collective-permute-start | bytes 786440 | tf_op jit(solution)/shard_map/ppermute | solution.py:180
